TPU v7x, 512 devices: a whole 4x4x16 slice. The times are simulated.
512 devices in a mesh: lon: 64 (over x, y, z_hi, core), lat: 8 (over z_lo).
Axes of the slice: x: 4, y: 4, z: 16 (z_hi: 2, z_lo: 8; z = z_hi * 8 + z_lo), core: 2. Of those that a mesh axis runs over, the one named last changes fastest.
Arguments:
- potential_heat: float32 [4, 768, 8192], P(None, 'lat', 'lon'), may hold values from -6 to 6
- salt_anomaly_field: float32 [4, 768, 8192], P(None, 'lat', 'lon'), may hold values from -6 to 6
- zonal_current: float32 [4, 768, 8192], P(None, 'lat', 'lon'), may hold values from -6 to 6
- meridional_current: float32 [4, 768, 8192], P(None, 'lat', 'lon'), may hold values from -6 to 6
- water_indicator: int32 [4, 768, 8192], P(None, 'lat', 'lon'), may hold values 0 or 1
- floor_layer_index: int32 [768, 8192], P('lat', 'lon'), may hold values from 0 to 3
- zonal_spacing: float32 [768, 8192], P('lat', 'lon'), may hold values from 0.7 to 1.4
- meridional_spacing: float32 [768, 8192], P('lat', 'lon'), may hold values from 0.7 to 1.4
- planetary_rotation_factor: float32 [768, 8192], P('lat', 'lon'), may hold values from 0.3 to 1.5
- horizontal_eddy_coefficient: float32 [768, 8192], P('lat', 'lon'), may hold values from 0.05 to 0.25
- diapycnal_diffusivity: float32 [3, 768, 8192], P(None, 'lat', 'lon'), may hold values from 0.02 to 0.5
- layer_height: float32 [4], replicated, may hold values from 0.7 to 1.4
Outputs:
- new_temperature: float32 [4, 768, 8192], P(None, 'lat', 'lon')
- new_salinity: float32 [4, 768, 8192], P(None, 'lat', 'lon')
- new_zonal: float32 [4, 768, 8192], P(None, 'lat', 'lon')
- new_meridional: float32 [4, 768, 8192], P(None, 'lat', 'lon')
All inputs are finite; a program needn't handle non-finite values. No bound on the sum of `water_indicator` on one device may be relied on, other than what follows from the above.
Results may differ from a plain program's by a relative error of at most 0.0003.
Values sent between devices are 32-bit elements; how exact they have to be, the bound alone decides.
No kernel may reach another device: no remote copies, remote signals or barrier semaphores. Data moves between devices by JAX's collectives and lax.ppermute only.
A program may use at most 64 MiB of HBM per device.

v0:
```python
import jax
import jax.numpy as jnp
from jax import lax
from jax.sharding import PartitionSpec as P

TIME_STEP = 0.25
EXPANSION = 0.2
CONTRACTION = 0.8
BOTTOM_DRAG = 1.0


def with_halo(value, sides, width, wrap):
    for axis, dim in sides:
        size, length = (lax.axis_size(axis), value.shape[dim])
        up = [(i, (i + 1) % size) for i in range(size if wrap else size - 1)]
        down = [(j, i) for i, j in up]
        last = lax.slice_in_dim(value, length - width, length, axis=dim)
        leading = lax.slice_in_dim(value, 0, width, axis=dim)
        before = lax.ppermute(last, axis, up)
        after = lax.ppermute(leading, axis, down)
        value = jnp.concatenate([before, value, after], axis=dim)
    return value


def pressure(temp_part, salt_part, layer_height):
    layer_mass = (CONTRACTION * salt_part - EXPANSION * temp_part) * layer_height[:, None, None]
    return jnp.cumsum(layer_mass, axis=0) - 0.5 * layer_mass


def mix_vertically(fields, water_share, diapycnal_diffusivity, layer_height):
    contrast = fields[:, 1:] - fields[:, :-1]
    fluxes = diapycnal_diffusivity * (water_share[1:] * water_share[:-1]) * contrast
    boundary = jnp.zeros_like(fluxes[:, :1])
    flux_below = jnp.concatenate([fluxes, boundary], axis=1)
    flux_above = jnp.concatenate([boundary, fluxes], axis=1)
    return (flux_below - flux_above) / (layer_height * layer_height)[None, :, None, None]


def advance(
    central,
    eastern,
    western,
    northern,
    southern,
    at_bottom,
    zonal_spacing,
    meridional_spacing,
    planetary_rotation_factor,
    horizontal_eddy_coefficient,
    diapycnal_diffusivity,
    layer_height,
):
    water_share = central[4]
    fields = central[:4]
    weight_east = water_share * eastern[4]
    weight_west = water_share * western[4]
    weight_north = water_share * northern[4]
    weight_south = water_share * southern[4]
    diffusion = horizontal_eddy_coefficient * (
        (weight_east * (eastern[:4] - fields) + weight_west * (western[:4] - fields))
        / (zonal_spacing * zonal_spacing)
        + (weight_north * (northern[:4] - fields) + weight_south * (southern[:4] - fields))
        / (meridional_spacing * meridional_spacing)
    )
    zonal = fields[2]
    merid = fields[3]
    advection = -(
        zonal * (eastern[:4] - western[:4]) * (0.5 / zonal_spacing)
        + merid * (northern[:4] - southern[:4]) * (0.5 / meridional_spacing)
    )
    pressure_east = pressure(eastern[0], eastern[1], layer_height)
    pressure_west = pressure(western[0], western[1], layer_height)
    pressure_north = pressure(northern[0], northern[1], layer_height)
    pressure_south = pressure(southern[0], southern[1], layer_height)
    gradient_x = -(pressure_east - pressure_west) * (0.5 / zonal_spacing)
    gradient_y = -(pressure_north - pressure_south) * (0.5 / meridional_spacing)
    mixing = mix_vertically(fields, water_share, diapycnal_diffusivity, layer_height)
    tendency = advection + diffusion + mixing
    tend_zonal = (
        tendency[2]
        + planetary_rotation_factor * merid
        + gradient_x
        - BOTTOM_DRAG * at_bottom * zonal
    )
    tend_merid = (
        tendency[3]
        - planetary_rotation_factor * zonal
        + gradient_y
        - BOTTOM_DRAG * at_bottom * merid
    )
    tendency = jnp.stack([tendency[0], tendency[1], tend_zonal, tend_merid])
    updated = water_share * (fields + TIME_STEP * tendency)
    return jnp.concatenate([updated, water_share[None]], axis=0)


def fold_ghost(top_row):
    fold_sign = jnp.array([1.0, 1.0, -1.0, -1.0, 1.0], jnp.float32).reshape(5, 1, 1)
    row_width = top_row.shape[2]
    gathered = lax.all_gather(top_row, "lon", axis=2, tiled=True)
    partner = lax.axis_size("lon") - 1 - lax.axis_index("lon")
    mirrored = lax.dynamic_slice_in_dim(gathered, partner * row_width, row_width, 2)
    return mirrored[:, :, ::-1] * fold_sign


def shards(
    potential_heat,
    salt_anomaly_field,
    zonal_current,
    meridional_current,
    water_indicator,
    floor_layer_index,
    zonal_spacing,
    meridional_spacing,
    planetary_rotation_factor,
    horizontal_eddy_coefficient,
    diapycnal_diffusivity,
    layer_height,
):
    water_share = water_indicator.astype(jnp.float32)
    combined_tracers = jnp.stack(
        [
            potential_heat * water_share,
            salt_anomaly_field * water_share,
            zonal_current * water_share,
            meridional_current * water_share,
            water_share,
        ]
    )
    levels = combined_tracers.shape[1]
    is_top = lax.axis_index("lat") == lax.axis_size("lat") - 1
    at_bottom = (
        lax.broadcasted_iota(jnp.int32, (levels, 1, 1), 0) == floor_layer_index[None]
    ).astype(jnp.float32)
    for step_index in range(2):
        lon_padded = with_halo(combined_tracers, (("lon", 3),), 1, True)
        lat_padded = with_halo(combined_tracers, (("lat", 2),), 1, False)
        ghost_row = fold_ghost(combined_tracers[:, :, -1, :])
        north_rim = jnp.where(is_top, ghost_row, lat_padded[:, :, -1, :])
        northern = jnp.concatenate([lat_padded[:, :, 2:-1, :], north_rim[:, :, None, :]], axis=2)
        southern = lat_padded[:, :, :-2, :]
        eastern = lon_padded[..., 2:]
        western = lon_padded[..., :-2]
        combined_tracers = advance(
            combined_tracers,
            eastern,
            western,
            northern,
            southern,
            at_bottom,
            zonal_spacing,
            meridional_spacing,
            planetary_rotation_factor,
            horizontal_eddy_coefficient,
            diapycnal_diffusivity,
            layer_height,
        )
    return (combined_tracers[0], combined_tracers[1], combined_tracers[2], combined_tracers[3])


def solution(mesh):
    return jax.shard_map(
        shards,
        mesh=mesh,
        in_specs=(
            P(None, "lat", "lon"),
            P(None, "lat", "lon"),
            P(None, "lat", "lon"),
            P(None, "lat", "lon"),
            P(None, "lat", "lon"),
            P("lat", "lon"),
            P("lat", "lon"),
            P("lat", "lon"),
            P("lat", "lon"),
            P("lat", "lon"),
            P(None, "lat", "lon"),
            P(),
        ),
        out_specs=(
            P(None, "lat", "lon"),
            P(None, "lat", "lon"),
            P(None, "lat", "lon"),
            P(None, "lat", "lon"),
        ),
        check_vma=False,
    )
```

profile of v0, /device:TPU:64, one launch (start us, length us, event | category | flops | bytes accessed | tf_op | source)
XLA Modules:
  0.0 402.3 jit_solution(17297029420401216242)
XLA Ops:
  0.7 1.1 constant_dynamic-update-slice_fusion.4
  1.8 1.1 constant_dynamic-update-slice_fusion.3
  2.9 1.1 constant_dynamic-update-slice_fusion.2
  4.7 2.0 collective-permute-start.2
  6.8 3.8 collective-permute-start.3
  10.6 1.3 fusion.149
  11.9 2.2 copy.83
  14.0 17.4 %collective-permute-start = (f32[5,4,96,1]{2,1,3,0:T(4,128)}, f32[5,4,96,1]{2,1,3,0:T(4,128)}, u32[]{:S(2)}, u32[]{:S(2)}) collective-permute-start(f32[5,4,96,1]{2,1,3,0:T(4,128)} %copy.83), channel_id=1, source_target_pairs={{8,0},{16,8},{24,16},{32,24},{40,32},{48,40},{56,48},{64,56},{72,6... | collective-permute-start | bytes 23048 | tf_op jit(solution)/shard_map/ppermute | solution.py:20
  31.8 1.9 collective-permute-start.1
  33.7 151.1 %all-gather = f32[5,4,1,8192]{3,2,1,0:T(1,128)S(1)} all-gather(f32[5,4,1,128]{3,2,1,0:T(1,128)} %get-tuple-element.27), channel_id=2, replica_groups=mesh['lon'=64,'lat'=8] {'lon'}, dimensions={3}, use_global_device_ids=true | all-gather | bytes 665600 | tf_op jit(solution)/shard_map/all_gather | solution.py:99
  188.0 1.1 copy.86
  190.0 2.0 copy.84
  193.0 1.4 fusion.74
  194.6 1.3 divide_add_fusion.1
  197.7 1.3 fusion.22
  199.1 163.0 %all-gather.1 = f32[5,4,1,8192]{3,2,1,0:T(1,128)} all-gather(f32[5,4,1,128]{3,2,1,0:T(1,128)S(1)} %get-tuple-element.23), channel_id=3, replica_groups=mesh['lon'=64,'lat'=8] {'lon'}, dimensions={3}, use_global_device_ids=true | all-gather | bytes 665600 | tf_op jit(solution)/shard_map/all_gather | solution.py:99
  362.1 5.1 %collective-permute-start.7 = (f32[5,4,1,128]{3,2,1,0:T(1,128)S(1)}, f32[5,4,1,128]{3,2,1,0:T(1,128)S(1)}, u32[]{:S(2)}, u32[]{:S(2)}) collective-permute-start(f32[5,4,1,128]{3,2,1,0:T(1,128)S(1)} %get-tuple-element.23), channel_id=1, source_target_pairs={{0,1},{1,2},{2,3},{3,4},{4,5},{5,6},{6,7},{8,9},{9,10},{10,11},{11... | collective-permute-start | bytes 30728 | tf_op jit(solution)/shard_map/ppermute | solution.py:19
  368.8 1.5 copy.91
  370.4 2.0 collective-permute-start.5
  372.7 16.5 %collective-permute-start.4 = (f32[5,4,96,1]{2,1,3,0:T(4,128)S(1)}, f32[5,4,96,1]{2,1,3,0:T(4,128)S(1)}, u32[]{:S(2)}, u32[]{:S(2)}) collective-permute-start(f32[5,4,96,1]{2,1,3,0:T(4,128)S(1)} %copy.89), channel_id=1, source_target_pairs={{8,0},{16,8},{24,16},{32,24},{40,32},{48,40},{56,48},{64,56},{72,6... | collective-permute-start | bytes 23048 | tf_op jit(solution)/shard_map/ppermute | solution.py:20
  390.0 1.9 collective-permute-start.6
  393.3 1.3 copy.90
  394.6 1.9 pad_maximum_fusion
  396.7 1.0 copy-done.1
  (144 shorter events, 16.6 us)
Async XLA Ops:
  0.6 3.4 copy-start.2
  0.6 3.4 copy-start.41
  1.8 183.2 %copy-start.4 = (f32[1,4,96,128]{3,2,1,0:T(8,128)}, f32[1,4,96,128]{3,2,1,0:T(8,128)S(1)}, u32[]{:S(2)}) copy-start(f32[1,4,96,128]{3,2,1,0:T(8,128)S(1)} %get-tuple-element.11) | copy-start | bytes 589828
  2.9 182.0 %copy-start.7 = (f32[1,4,96,128]{3,2,1,0:T(8,128)}, f32[1,4,96,128]{3,2,1,0:T(8,128)S(1)}, u32[]{:S(2)}) copy-start(f32[1,4,96,128]{3,2,1,0:T(8,128)S(1)} %get-tuple-element.9) | copy-start | bytes 589828
  4.7 187.3 %collective-permute-start.2 = (f32[5,4,1,128]{3,1,0,2:T(4,128)}, f32[5,4,1,128]{3,1,0,2:T(4,128)}, u32[]{:S(2)}, u32[]{:S(2)}) collective-permute-start(f32[5,4,1,128]{3,1,0,2:T(4,128)} %bitcast.37), channel_id=1, source_target_pairs={{1,0},{2,1},{3,2},{4,3},{5,4},{6,5},{7,6},{9,8},{10,9},{11,10},{12... | collective-permute-start | bytes 30728 | tf_op jit(solution)/shard_map/ppermute | solution.py:20
  6.8 186.1 %collective-permute-start.3 = (f32[5,4,1,128]{3,2,1,0:T(1,128)}, f32[5,4,1,128]{3,2,1,0:T(1,128)S(1)}, u32[]{:S(2)}, u32[]{:S(2)}) collective-permute-start(f32[5,4,1,128]{3,2,1,0:T(1,128)} %get-tuple-element.27), channel_id=1, source_target_pairs={{0,1},{1,2},{2,3},{3,4},{4,5},{5,6},{6,7},{8,9},{9,10},{10,11},{11... | collective-permute-start | bytes 30728 | tf_op jit(solution)/shard_map/ppermute | solution.py:19
  11.9 173.0 %copy-start.42 = (f32[3,96,128]{2,1,0:T(8,128)S(1)}, f32[3,96,128]{2,1,0:T(8,128)}, u32[]{:S(2)}) copy-start(f32[3,96,128]{2,1,0:T(8,128)} %param.24) | copy-start | bytes 442372
  14.0 176.0 %collective-permute-start = (f32[5,4,96,1]{2,1,3,0:T(4,128)}, f32[5,4,96,1]{2,1,3,0:T(4,128)}, u32[]{:S(2)}, u32[]{:S(2)}) collective-permute-start(f32[5,4,96,1]{2,1,3,0:T(4,128)} %copy.83), channel_id=1, source_target_pairs={{8,0},{16,8},{24,16},{32,24},{40,32},{48,40},{56,48},{64,56},{72,6... | collective-permute-start | bytes 23048 | tf_op jit(solution)/shard_map/ppermute | solution.py:20
  31.8 156.2 %collective-permute-start.1 = (f32[5,4,96,1]{2,1,3,0:T(4,128)S(1)}, f32[5,4,96,1]{2,1,3,0:T(4,128)}, u32[]{:S(2)}, u32[]{:S(2)}) collective-permute-start(f32[5,4,96,1]{2,1,3,0:T(4,128)S(1)} %copy.85), channel_id=1, source_target_pairs={{0,8},{8,16},{16,24},{24,32},{32,40},{40,48},{48,56},{56,64},{64,7... | collective-permute-start | bytes 23048 | tf_op jit(solution)/shard_map/ppermute | solution.py:19
  184.9 1.7 copy-start.21
  185.0 2.4 copy-start.43
  192.9 1.6 copy-start.19
  192.9 1.6 copy-start.23
  192.9 1.6 copy-start.25
  192.9 1.6 copy-start.35
  199.0 168.2 %copy-start.22 = (f32[3,96,128]{2,1,0:T(8,128)S(1)}, f32[3,96,128]{2,1,0:T(8,128)}, u32[]{:S(2)}) copy-start(f32[3,96,128]{2,1,0:T(8,128)} %copy-done.21) | copy-start | bytes 442372
  362.1 34.5 %collective-permute-start.7 = (f32[5,4,1,128]{3,2,1,0:T(1,128)S(1)}, f32[5,4,1,128]{3,2,1,0:T(1,128)S(1)}, u32[]{:S(2)}, u32[]{:S(2)}) collective-permute-start(f32[5,4,1,128]{3,2,1,0:T(1,128)S(1)} %get-tuple-element.23), channel_id=1, source_target_pairs={{0,1},{1,2},{2,3},{3,4},{4,5},{5,6},{6,7},{8,9},{9,10},{10,11},{11... | collective-permute-start | bytes 30728 | tf_op jit(solution)/shard_map/ppermute | solution.py:19
  370.4 21.6 %collective-permute-start.5 = (f32[5,4,96,1]{2,1,3,0:T(4,128)S(1)}, f32[5,4,96,1]{2,1,3,0:T(4,128)S(1)}, u32[]{:S(2)}, u32[]{:S(2)}) collective-permute-start(f32[5,4,96,1]{2,1,3,0:T(4,128)S(1)} %copy.91), channel_id=1, source_target_pairs={{0,8},{8,16},{16,24},{24,32},{32,40},{40,48},{48,56},{56,64},{64,7... | collective-permute-start | bytes 23048 | tf_op jit(solution)/shard_map/ppermute | solution.py:19
  372.7 20.6 %collective-permute-start.4 = (f32[5,4,96,1]{2,1,3,0:T(4,128)S(1)}, f32[5,4,96,1]{2,1,3,0:T(4,128)S(1)}, u32[]{:S(2)}, u32[]{:S(2)}) collective-permute-start(f32[5,4,96,1]{2,1,3,0:T(4,128)S(1)} %copy.89), channel_id=1, source_target_pairs={{8,0},{16,8},{24,16},{32,24},{40,32},{48,40},{56,48},{64,56},{72,6... | collective-permute-start | bytes 23048 | tf_op jit(solution)/shard_map/ppermute | solution.py:20
  390.0 6.5 %collective-permute-start.6 = (f32[5,4,1,128]{3,2,1,0:T(1,128)S(1)}, f32[5,4,1,128]{3,2,1,0:T(1,128)S(1)}, u32[]{:S(2)}, u32[]{:S(2)}) collective-permute-start(f32[5,4,1,128]{3,2,1,0:T(1,128)S(1)} %get-tuple-element.22), channel_id=1, source_target_pairs={{1,0},{2,1},{3,2},{4,3},{5,4},{6,5},{7,6},{9,8},{10,9},{11,10},{12... | collective-permute-start | bytes 30728 | tf_op jit(solution)/shard_map/ppermute | solution.py:20
  394.6 1.9 copy-start.46
  397.8 1.6 copy-start.34
  397.8 1.6 copy-start.36
  397.8 1.6 copy-start.38
  (33 other events, 42.2 us)
where the time goes:
time: 403 us; the launch traced here: 402 us
  blocking collectives  314 us (78%)
  starting transfers between devices  50.7 us (13%)
  other arithmetic  18.4 us (5%)
  local copies, waits for them, and re-layouts  17.8 us (4%)
    all_gather x2, blocking collectives, fold_ghost(): gathered = lax.all_gather(top_row, 'lon', axis=2, tiled=True)  314 us
    ppermute x4, starting transfers between devices, with_halo(): after = lax.ppermute(leading, axis, down)  37.9 us
    ppermute x4, starting transfers between devices, with_halo(): before = lax.ppermute(last, axis, up)  12.8 us
  transfers between devices with their start and end apart: 8, of which 0 were waited for; matrix products, arithmetic and copies ran while one was open for 5% of the time, Pallas kernels for 0%

commit v1 on v0

--- a/solution.py
+++ b/solution.py
@@ -95,10 +95,11 @@
 
 def fold_ghost(top_row):
     fold_sign = jnp.array([1.0, 1.0, -1.0, -1.0, 1.0], jnp.float32).reshape(5, 1, 1)
-    row_width = top_row.shape[2]
-    gathered = lax.all_gather(top_row, "lon", axis=2, tiled=True)
-    partner = lax.axis_size("lon") - 1 - lax.axis_index("lon")
-    mirrored = lax.dynamic_slice_in_dim(gathered, partner * row_width, row_width, 2)
+    lon_count = lax.axis_size("lon")
+    lat_count = lax.axis_size("lat")
+    top = lat_count - 1
+    pairs = [(i * lat_count + top, (lon_count - 1 - i) * lat_count + top) for i in range(lon_count)]
+    mirrored = lax.ppermute(top_row, ("lon", "lat"), pairs)
     return mirrored[:, :, ::-1] * fold_sign
 
 

time: 403 us -> 115 us (0.29)
  the two profiles are of different devices: /device:TPU:64 before, /device:TPU:96 now
where the time goes in v1:
time: 115 us; the launch traced here: 114 us
  starting transfers between devices  53.5 us (47%)
  other arithmetic  26.9 us (23%)
  local copies, waits for them, and re-layouts  19.1 us (17%)
  waiting for transfers between devices  13.1 us (11%)
  between operations  1.39 us (1%)
    ppermute x4, starting transfers between devices, with_halo(): after = lax.ppermute(leading, axis, down)  37 us
    ppermute x4, starting transfers between devices, with_halo(): before = lax.ppermute(last, axis, up)  14 us
    ppermute x4, waiting for transfers between devices, with_halo(): before = lax.ppermute(last, axis, up)  13.1 us
    concatenate x2, other arithmetic, with_halo(): value = jnp.concatenate([before, value, after], axis=dim)  4.95 us
    another operation x8, other arithmetic, pressure(): return jnp.cumsum(layer_mass, axis=0) - 0.5 * layer_mass  4.84 us
    add x2, other arithmetic, advance(): tendency = advection + diffusion + mixing  3.98 us
    unnamed x102, local copies, waits for them, and re-layouts  3.46 us
    ppermute x2, local copies, waits for them, and re-layouts, with_halo(): after = lax.ppermute(leading, axis, down)  3.4 us
  transfers between devices with their start and end apart: 10, of which 1 were waited for; matrix products, arithmetic and copies ran while one was open for 20% of the time, Pallas kernels for 0%

profile of v1, /device:TPU:96, one launch (start us, length us, event | category | flops | bytes accessed | tf_op | source)
XLA Modules:
  0.0 114.1 jit_solution(16415329810303004652)
XLA Ops:
  4.7 1.2 %collective-permute-start.2 = (f32[5,4,128]{2,1,0:T(4,128)}, f32[5,4,128]{2,1,0:T(4,128)}, u32[]{:S(2)}, u32[]{:S(2)}) collective-permute-start(f32[5,4,128]{2,1,0:T(4,128)} %bitcast.5), channel_id=1, source_target_pairs={{7,511},{15,503},{23,495},{31,487},{39,479},{47,471},{55,463},{63,... | collective-permute-start | bytes 30728 | tf_op jit(solution)/shard_map/ppermute | solution.py:102
  6.0 2.0 %collective-permute-start.3 = (f32[5,4,1,128]{3,1,0,2:T(4,128)}, f32[5,4,1,128]{3,1,0,2:T(4,128)}, u32[]{:S(2)}, u32[]{:S(2)}) collective-permute-start(f32[5,4,1,128]{3,1,0,2:T(4,128)} %bitcast.41), channel_id=1, source_target_pairs={{1,0},{2,1},{3,2},{4,3},{5,4},{6,5},{7,6},{9,8},{10,9},{11,10},{12... | collective-permute-start | bytes 30728 | tf_op jit(solution)/shard_map/ppermute | solution.py:20
  8.0 5.0 %collective-permute-start.4 = (f32[5,4,1,128]{3,1,0,2:T(4,128)}, f32[5,4,1,128]{3,1,0,2:T(4,128)S(1)}, u32[]{:S(2)}, u32[]{:S(2)}) collective-permute-start(f32[5,4,1,128]{3,1,0,2:T(4,128)} %bitcast.39), channel_id=1, source_target_pairs={{0,1},{1,2},{2,3},{3,4},{4,5},{5,6},{6,7},{8,9},{9,10},{10,11},{11... | collective-permute-start | bytes 30728 | tf_op jit(solution)/shard_map/ppermute | solution.py:19
  13.0 1.3 %fusion.149 = (f32[5,4,96,1]{3,2,1,0:T(8,128)S(1)}, f32[5,4,96,1]{3,2,1,0:T(8,128)}) fusion(f32[5,4,96,128]{3,2,1,0:T(8,128)S(1)} %constant_dynamic-update-slice_fusion), kind=kLoop, calls=%fused_computation.239 | loop fusion | bytes 30720 | tf_op jit(solution)/shard_map/slice | solution.py:17
  14.4 2.2 %copy.87 = f32[5,4,96,1]{2,1,3,0:T(4,128)} copy(f32[5,4,96,1]{3,2,1,0:T(8,128)} %get-tuple-element.25) | data formatting | bytes 15360 | tf_op jit(solution)/shard_map/slice | solution.py:18
  16.5 16.5 %collective-permute-start = (f32[5,4,96,1]{2,1,3,0:T(4,128)}, f32[5,4,96,1]{2,1,3,0:T(4,128)}, u32[]{:S(2)}, u32[]{:S(2)}) collective-permute-start(f32[5,4,96,1]{2,1,3,0:T(4,128)} %copy.87), channel_id=1, source_target_pairs={{8,0},{16,8},{24,16},{32,24},{40,32},{48,40},{56,48},{64,56},{72,6... | collective-permute-start | bytes 23048 | tf_op jit(solution)/shard_map/ppermute | solution.py:20
  33.4 1.9 %collective-permute-start.1 = (f32[5,4,96,1]{2,1,3,0:T(4,128)S(1)}, f32[5,4,96,1]{2,1,3,0:T(4,128)}, u32[]{:S(2)}, u32[]{:S(2)}) collective-permute-start(f32[5,4,96,1]{2,1,3,0:T(4,128)S(1)} %copy.89), channel_id=1, source_target_pairs={{0,8},{8,16},{16,24},{24,32},{32,40},{40,48},{48,56},{56,64},{64,7... | collective-permute-start | bytes 23048 | tf_op jit(solution)/shard_map/ppermute | solution.py:19
  38.3 13.1 %collective-permute-done.1 = f32[5,4,96,1]{2,1,3,0:T(4,128)} collective-permute-done((f32[5,4,96,1]{2,1,3,0:T(4,128)S(1)}, f32[5,4,96,1]{2,1,3,0:T(4,128)}, u32[]{:S(2)}, u32[]{:S(2)}) %collective-permute-start.1) | collective-permute-done | bytes 7712 | tf_op jit(solution)/shard_map/ppermute | solution.py:19
  53.5 2.0 %copy.88 = f32[5,4,96,1]{3,2,1,0:T(8,128)} copy(f32[5,4,96,1]{2,1,3,0:T(4,128)} %collective-permute-done) | data formatting | bytes 15360 | tf_op jit(solution)/shard_map/ppermute | solution.py:20
  56.3 1.4 %rev.6 = f32[5,4,128]{2,1,0:T(4,128)} reverse(f32[5,4,128]{2,1,0:T(4,128)} %collective-permute-done.2), dimensions={2} | reverse | bytes 20480 | tf_op jit(solution)/shard_map/rev | solution.py:103
  58.6 1.4 %fusion.74 = (f32[4,96,128]{2,1,0:T(8,128)S(1)}, f32[4,96,128]{2,1,0:T(8,128)S(1)}, f32[4,96,128]{2,1,0:T(8,128)S(1)}, f32[4,96,128]{2,1,0:T(8,128)S(1)}) fusion(f32[5,4,96,128]{3,2,1,0:T(8,128)S(1)} %constant_dynamic-update-slice_fusion, f32[5,4,96,1]{3,2,1,0:T(8,128)} %copy.88, s32[4,96,128]{2,1,0:T(8,128)} %param.18, f32[5,4,1,128]{3,2,1,0:T(1,128)S(1)} %bitcast.140, ...), kind=kLoop, calls=%fused_computation.130 | loop fusion | flops 442368 | bytes 2974720 | tf_op jit(solution)/shard_map/mul | solution.py:55
  60.2 1.3 %divide_add_fusion.1 = f32[4,4,96,128]{3,2,1,0:T(8,128)S(1)} fusion(f32[4,3,96,128]{3,2,1,0:T(8,128)S(1)} %copy-done.20, f32[5,4,96,128]{3,2,1,0:T(8,128)S(1)} %constant_dynamic-update-slice_fusion, f32[5,4,1,128]{3,2,1,0:T(1,128)S(1)} %bitcast.141, f32[5,4,1,128]{3,2,1,0:T(1,128)S(1)} %bitcast.137, f32[5,4,95,128]{3,2,1,0:T(8,128)S(1)} %slice.300, ...), kind=kLoop, calls=%fused_computation.87 | loop fusion | flops 6488064 | bytes 5579792 | tf_op jit(solution)/shard_map/add | solution.py:78
  63.8 1.3 %fusion.22 = (f32[5,4,96,1]{3,2,1,0:T(8,128)S(1)}, f32[5,4,96,1]{3,2,1,0:T(8,128)}) fusion(f32[4,4,96,128]{3,2,1,0:T(8,128)S(1)} %fusion.31, f32[1,4,96,128]{3,2,1,0:T(8,128)S(1)} %get-tuple-element.35), kind=kLoop, calls=%fused_computation.65 | loop fusion | flops 3840 | bytes 998400 | tf_op jit(solution)/shard_map/concatenate | solution.py:93
  67.0 1.5 %copy.97 = f32[5,4,96,1]{2,1,3,0:T(4,128)S(1)} copy(f32[5,4,96,1]{3,2,1,0:T(8,128)} %get-tuple-element.21) | data formatting | bytes 15360 | tf_op jit(solution)/shard_map/slice | solution.py:17
  68.5 1.9 %collective-permute-start.6 = (f32[5,4,96,1]{2,1,3,0:T(4,128)S(1)}, f32[5,4,96,1]{2,1,3,0:T(4,128)S(1)}, u32[]{:S(2)}, u32[]{:S(2)}) collective-permute-start(f32[5,4,96,1]{2,1,3,0:T(4,128)S(1)} %copy.97), channel_id=1, source_target_pairs={{0,8},{8,16},{16,24},{24,32},{32,40},{40,48},{48,56},{56,64},{64,7... | collective-permute-start | bytes 23048 | tf_op jit(solution)/shard_map/ppermute | solution.py:19
  71.4 16.6 %collective-permute-start.5 = (f32[5,4,96,1]{2,1,3,0:T(4,128)S(1)}, f32[5,4,96,1]{2,1,3,0:T(4,128)S(1)}, u32[]{:S(2)}, u32[]{:S(2)}) collective-permute-start(f32[5,4,96,1]{2,1,3,0:T(4,128)S(1)} %copy.95), channel_id=1, source_target_pairs={{8,0},{16,8},{24,16},{32,24},{40,32},{48,40},{56,48},{64,56},{72,6... | collective-permute-start | bytes 23048 | tf_op jit(solution)/shard_map/ppermute | solution.py:20
  88.0 1.3 %collective-permute-start.7 = (f32[5,4,128]{2,1,0:T(4,128)}, f32[5,4,128]{2,1,0:T(4,128)}, u32[]{:S(2)}, u32[]{:S(2)}) collective-permute-start(f32[5,4,128]{2,1,0:T(4,128)} %bitcast.24), channel_id=1, source_target_pairs={{7,511},{15,503},{23,495},{31,487},{39,479},{47,471},{55,463},{63,... | collective-permute-start | bytes 30728 | tf_op jit(solution)/shard_map/ppermute | solution.py:102
  89.2 1.9 %collective-permute-start.8 = (f32[5,4,1,128]{3,2,1,0:T(1,128)}, f32[5,4,1,128]{3,2,1,0:T(1,128)}, u32[]{:S(2)}, u32[]{:S(2)}) collective-permute-start(f32[5,4,1,128]{3,2,1,0:T(1,128)} %get-tuple-element.22), channel_id=1, source_target_pairs={{1,0},{2,1},{3,2},{4,3},{5,4},{6,5},{7,6},{9,8},{10,9},{11,10},{12... | collective-permute-start | bytes 30728 | tf_op jit(solution)/shard_map/ppermute | solution.py:20
  91.2 5.1 %collective-permute-start.9 = (f32[5,4,1,128]{3,1,0,2:T(4,128)}, f32[5,4,1,128]{3,1,0,2:T(4,128)S(1)}, u32[]{:S(2)}, u32[]{:S(2)}) collective-permute-start(f32[5,4,1,128]{3,1,0,2:T(4,128)} %bitcast.42), channel_id=1, source_target_pairs={{0,1},{1,2},{2,3},{3,4},{4,5},{5,6},{6,7},{8,9},{9,10},{10,11},{11... | collective-permute-start | bytes 30728 | tf_op jit(solution)/shard_map/ppermute | solution.py:19
  97.7 1.4 %copy.96 = f32[5,4,96,1]{3,2,1,0:T(8,128)} copy(f32[5,4,96,1]{2,1,3,0:T(4,128)S(1)} %collective-permute-done.5) | data formatting | bytes 15360 | tf_op jit(solution)/shard_map/ppermute | solution.py:20
  99.0 3.8 %pad_maximum_fusion = (f32[5,4,96,129]{3,2,1,0:T(8,128)}, f32[5,4,96,129]{3,2,1,0:T(8,128)}) fusion(f32[5,4,96,1]{3,2,1,0:T(8,128)} %copy.96, f32[1,4,96,128]{3,2,1,0:T(8,128)S(1)} %get-tuple-element.35, f32[4,4,96,128]{3,2,1,0:T(8,128)S(1)} %fusion.31, f32[5,4,96,1]{3,2,1,0:T(8,128)S(1)} %copy.98), kind=kLoop, calls=%fused_computation.19 | loop fusion | flops 990720 | bytes 2979840 | tf_op jit(solution)/shard_map/concatenate | solution.py:21
  104.7 1.4 %rev.7 = f32[5,4,128]{2,1,0:T(4,128)} reverse(f32[5,4,128]{2,1,0:T(4,128)} %collective-permute-done.7), dimensions={2} | reverse | bytes 20480 | tf_op jit(solution)/shard_map/rev | solution.py:103
  107.1 1.3 %fusion.84 = (f32[4,96,128]{2,1,0:T(8,128)S(1)}, f32[4,96,128]{2,1,0:T(8,128)S(1)}, f32[4,96,128]{2,1,0:T(8,128)S(1)}, f32[4,96,128]{2,1,0:T(8,128)S(1)}) fusion(f32[5,4,96,1]{3,2,1,0:T(8,128)} %copy.96, f32[1,4,96,128]{3,2,1,0:T(8,128)S(1)} %get-tuple-element.35, f32[4,4,96,128]{3,2,1,0:T(8,128)S(1)} %fusion.31, s32[4,96,128]{2,1,0:T(8,128)S(1)} %copy-done.3, ...), kind=kLoop, calls=%fused_computation.156 | loop fusion | flops 589824 | bytes 2974720 | tf_op jit(solution)/shard_map/mul | solution.py:55
  109.1 2.6 %divide_add_fusion = f32[4,4,96,128]{3,2,1,0:T(8,128)S(1)} fusion(f32[4,3,96,128]{3,2,1,0:T(8,128)S(1)} %copy-done.21, f32[5,4,1,128]{3,2,1,0:T(1,128)S(1)} %bitcast.134, f32[5,4,95,128]{3,2,1,0:T(8,128)S(1)} %fusion.24, f32[5,4,97,128]{3,2,1,0:T(8,128)S(1)} %copy-done.15, f32[5,4,96,129]{3,2,1,0:T(8,128)} %get-tuple-element.19, ...), kind=kLoop, calls=%fused_computation.86 | loop fusion | flops 6881280 | bytes 7913488 | tf_op jit(solution)/shard_map/add | solution.py:78
  (148 shorter events, 23.1 us)
Async XLA Ops:
  0.6 3.4 %copy-start.2 = (s32[4,96,128]{2,1,0:T(8,128)S(1)}, s32[4,96,128]{2,1,0:T(8,128)}, u32[]{:S(2)}) copy-start(s32[4,96,128]{2,1,0:T(8,128)} %param.18) | copy-start | bytes 589828
  0.6 3.4 %copy-start.44 = (f32[4,96,128]{2,1,0:T(8,128)S(1)}, f32[4,96,128]{2,1,0:T(8,128)}, u32[]{:S(2)}) copy-start(f32[4,96,128]{2,1,0:T(8,128)} %param.17) | copy-start | bytes 589828
  1.8 34.3 %copy-start.4 = (f32[1,4,96,128]{3,2,1,0:T(8,128)}, f32[1,4,96,128]{3,2,1,0:T(8,128)S(1)}, u32[]{:S(2)}) copy-start(f32[1,4,96,128]{3,2,1,0:T(8,128)S(1)} %get-tuple-element.11) | copy-start | bytes 589828
  2.9 33.2 %copy-start.7 = (f32[1,4,96,128]{3,2,1,0:T(8,128)}, f32[1,4,96,128]{3,2,1,0:T(8,128)S(1)}, u32[]{:S(2)}) copy-start(f32[1,4,96,128]{3,2,1,0:T(8,128)S(1)} %get-tuple-element.9) | copy-start | bytes 589828
  4.7 51.5 %collective-permute-start.2 = (f32[5,4,128]{2,1,0:T(4,128)}, f32[5,4,128]{2,1,0:T(4,128)}, u32[]{:S(2)}, u32[]{:S(2)}) collective-permute-start(f32[5,4,128]{2,1,0:T(4,128)} %bitcast.5), channel_id=1, source_target_pairs={{7,511},{15,503},{23,495},{31,487},{39,479},{47,471},{55,463},{63,... | collective-permute-start | bytes 30728 | tf_op jit(solution)/shard_map/ppermute | solution.py:102
  6.0 51.7 %collective-permute-start.3 = (f32[5,4,1,128]{3,1,0,2:T(4,128)}, f32[5,4,1,128]{3,1,0,2:T(4,128)}, u32[]{:S(2)}, u32[]{:S(2)}) collective-permute-start(f32[5,4,1,128]{3,1,0,2:T(4,128)} %bitcast.41), channel_id=1, source_target_pairs={{1,0},{2,1},{3,2},{4,3},{5,4},{6,5},{7,6},{9,8},{10,9},{11,10},{12... | collective-permute-start | bytes 30728 | tf_op jit(solution)/shard_map/ppermute | solution.py:20
  8.0 47.5 %collective-permute-start.4 = (f32[5,4,1,128]{3,1,0,2:T(4,128)}, f32[5,4,1,128]{3,1,0,2:T(4,128)S(1)}, u32[]{:S(2)}, u32[]{:S(2)}) collective-permute-start(f32[5,4,1,128]{3,1,0,2:T(4,128)} %bitcast.39), channel_id=1, source_target_pairs={{0,1},{1,2},{2,3},{3,4},{4,5},{5,6},{6,7},{8,9},{9,10},{10,11},{11... | collective-permute-start | bytes 30728 | tf_op jit(solution)/shard_map/ppermute | solution.py:19
  14.3 21.7 %copy-start.45 = (f32[3,96,128]{2,1,0:T(8,128)S(1)}, f32[3,96,128]{2,1,0:T(8,128)}, u32[]{:S(2)}) copy-start(f32[3,96,128]{2,1,0:T(8,128)} %param.24) | copy-start | bytes 442372
  16.5 36.9 %collective-permute-start = (f32[5,4,96,1]{2,1,3,0:T(4,128)}, f32[5,4,96,1]{2,1,3,0:T(4,128)}, u32[]{:S(2)}, u32[]{:S(2)}) collective-permute-start(f32[5,4,96,1]{2,1,3,0:T(4,128)} %copy.87), channel_id=1, source_target_pairs={{8,0},{16,8},{24,16},{32,24},{40,32},{48,40},{56,48},{64,56},{72,6... | collective-permute-start | bytes 23048 | tf_op jit(solution)/shard_map/ppermute | solution.py:20
  33.4 18.0 %collective-permute-start.1 = (f32[5,4,96,1]{2,1,3,0:T(4,128)S(1)}, f32[5,4,96,1]{2,1,3,0:T(4,128)}, u32[]{:S(2)}, u32[]{:S(2)}) collective-permute-start(f32[5,4,96,1]{2,1,3,0:T(4,128)S(1)} %copy.89), channel_id=1, source_target_pairs={{0,8},{8,16},{16,24},{24,32},{32,40},{40,48},{48,56},{56,64},{64,7... | collective-permute-start | bytes 23048 | tf_op jit(solution)/shard_map/ppermute | solution.py:19
  68.5 27.8 %collective-permute-start.6 = (f32[5,4,96,1]{2,1,3,0:T(4,128)S(1)}, f32[5,4,96,1]{2,1,3,0:T(4,128)S(1)}, u32[]{:S(2)}, u32[]{:S(2)}) collective-permute-start(f32[5,4,96,1]{2,1,3,0:T(4,128)S(1)} %copy.97), channel_id=1, source_target_pairs={{0,8},{8,16},{16,24},{24,32},{32,40},{40,48},{48,56},{56,64},{64,7... | collective-permute-start | bytes 23048 | tf_op jit(solution)/shard_map/ppermute | solution.py:19
  71.4 26.3 %collective-permute-start.5 = (f32[5,4,96,1]{2,1,3,0:T(4,128)S(1)}, f32[5,4,96,1]{2,1,3,0:T(4,128)S(1)}, u32[]{:S(2)}, u32[]{:S(2)}) collective-permute-start(f32[5,4,96,1]{2,1,3,0:T(4,128)S(1)} %copy.95), channel_id=1, source_target_pairs={{8,0},{16,8},{24,16},{32,24},{40,32},{48,40},{56,48},{64,56},{72,6... | collective-permute-start | bytes 23048 | tf_op jit(solution)/shard_map/ppermute | solution.py:20
  88.0 16.8 %collective-permute-start.7 = (f32[5,4,128]{2,1,0:T(4,128)}, f32[5,4,128]{2,1,0:T(4,128)}, u32[]{:S(2)}, u32[]{:S(2)}) collective-permute-start(f32[5,4,128]{2,1,0:T(4,128)} %bitcast.24), channel_id=1, source_target_pairs={{7,511},{15,503},{23,495},{31,487},{39,479},{47,471},{55,463},{63,... | collective-permute-start | bytes 30728 | tf_op jit(solution)/shard_map/ppermute | solution.py:102
  89.2 16.9 %collective-permute-start.8 = (f32[5,4,1,128]{3,2,1,0:T(1,128)}, f32[5,4,1,128]{3,2,1,0:T(1,128)}, u32[]{:S(2)}, u32[]{:S(2)}) collective-permute-start(f32[5,4,1,128]{3,2,1,0:T(1,128)} %get-tuple-element.22), channel_id=1, source_target_pairs={{1,0},{2,1},{3,2},{4,3},{5,4},{6,5},{7,6},{9,8},{10,9},{11,10},{12... | collective-permute-start | bytes 30728 | tf_op jit(solution)/shard_map/ppermute | solution.py:20
  91.2 11.7 %collective-permute-start.9 = (f32[5,4,1,128]{3,1,0,2:T(4,128)}, f32[5,4,1,128]{3,1,0,2:T(4,128)S(1)}, u32[]{:S(2)}, u32[]{:S(2)}) collective-permute-start(f32[5,4,1,128]{3,1,0,2:T(4,128)} %bitcast.42), channel_id=1, source_target_pairs={{0,1},{1,2},{2,3},{3,4},{4,5},{5,6},{6,7},{8,9},{9,10},{10,11},{11... | collective-permute-start | bytes 30728 | tf_op jit(solution)/shard_map/ppermute | solution.py:19
  102.8 4.1 %copy-start.3 = (s32[4,96,128]{2,1,0:T(8,128)S(1)}, s32[4,96,128]{2,1,0:T(8,128)}, u32[]{:S(2)}) copy-start(s32[4,96,128]{2,1,0:T(8,128)} %param.18) | copy-start | bytes 589828
  107.0 2.0 %copy-start.37 = (f32[4,96,128]{2,1,0:T(8,128)S(1)}, f32[4,96,128]{2,1,0:T(8,128)}, u32[]{:S(2)}) copy-start(f32[4,96,128]{2,1,0:T(8,128)} %get-tuple-element.33) | copy-start | bytes 589828
  107.0 2.0 %copy-start.39 = (f32[96,128]{1,0:T(8,128)S(1)}, f32[96,128]{1,0:T(8,128)}, u32[]{:S(2)}) copy-start(f32[96,128]{1,0:T(8,128)} %get-tuple-element.41) | copy-start | bytes 147460
  107.1 2.0 %copy-start.41 = (f32[96,128]{1,0:T(8,128)S(1)}, f32[96,128]{1,0:T(8,128)}, u32[]{:S(2)}) copy-start(f32[96,128]{1,0:T(8,128)} %get-tuple-element.42) | copy-start | bytes 147460
  107.1 2.0 %copy-start.43 = (f32[96,128]{1,0:T(8,128)S(1)}, f32[96,128]{1,0:T(8,128)}, u32[]{:S(2)}) copy-start(f32[96,128]{1,0:T(8,128)} %param.23) | copy-start | bytes 147460
  109.1 2.7 %copy-start.1 = (f32[5,4,96,1]{3,2,1,0:T(8,128)S(1)}, f32[5,4,96,1]{3,2,1,0:T(8,128)}, u32[]{:S(2)}) copy-start(f32[5,4,96,1]{3,2,1,0:T(8,128)} %copy.96) | copy-start | bytes 23044
  109.1 2.7 %copy-start.28 = (f32[1,4,96,128]{3,2,1,0:T(8,128)S(1)}, f32[1,4,96,128]{3,2,1,0:T(8,128)}, u32[]{:S(2)}) copy-start(f32[1,4,96,128]{3,2,1,0:T(8,128)} %reduce-window_subtract_fusion.2) | copy-start | bytes 589828
  109.1 2.7 %copy-start.31 = (s32[96,128]{1,0:T(8,128)S(1)}, s32[96,128]{1,0:T(8,128)}, u32[]{:S(2)}) copy-start(s32[96,128]{1,0:T(8,128)} %param.19) | copy-start | bytes 147460
  109.1 2.7 %copy-start.33 = (f32[96,128]{1,0:T(8,128)S(1)}, f32[96,128]{1,0:T(8,128)}, u32[]{:S(2)}) copy-start(f32[96,128]{1,0:T(8,128)} %param.22) | copy-start | bytes 147460
  (37 other events, 55.2 us)

commit v2 on v1

--- a/solution.py
+++ b/solution.py
@@ -7,19 +7,7 @@
 EXPANSION = 0.2
 CONTRACTION = 0.8
 BOTTOM_DRAG = 1.0
-
-
-def with_halo(value, sides, width, wrap):
-    for axis, dim in sides:
-        size, length = (lax.axis_size(axis), value.shape[dim])
-        up = [(i, (i + 1) % size) for i in range(size if wrap else size - 1)]
-        down = [(j, i) for i, j in up]
-        last = lax.slice_in_dim(value, length - width, length, axis=dim)
-        leading = lax.slice_in_dim(value, 0, width, axis=dim)
-        before = lax.ppermute(last, axis, up)
-        after = lax.ppermute(leading, axis, down)
-        value = jnp.concatenate([before, value, after], axis=dim)
-    return value
+HALO = 2
 
 
 def pressure(temp_part, salt_part, layer_height):
@@ -93,14 +81,78 @@
     return jnp.concatenate([updated, water_share[None]], axis=0)
 
 
-def fold_ghost(top_row):
-    fold_sign = jnp.array([1.0, 1.0, -1.0, -1.0, 1.0], jnp.float32).reshape(5, 1, 1)
+def step(state, params, levels, layer_height):
+    floor_index = params[0]
+    at_bottom = (
+        lax.broadcasted_iota(jnp.int32, (levels, 1, 1), 0).astype(jnp.float32) == floor_index[None]
+    ).astype(jnp.float32)
+    return advance(
+        state[:, :, 1:-1, 1:-1],
+        state[:, :, 1:-1, 2:],
+        state[:, :, 1:-1, :-2],
+        state[:, :, 2:, 1:-1],
+        state[:, :, :-2, 1:-1],
+        at_bottom,
+        params[1],
+        params[2],
+        params[3],
+        params[4],
+        params[5:8],
+        layer_height,
+    )
+
+
+def neighbour_pairs(lon_count, lat_count, d_lon, d_lat):
+    pairs = []
+    for i in range(lon_count):
+        for j in range(lat_count):
+            k = j + d_lat
+            if 0 <= k < lat_count:
+                pairs.append((i * lat_count + j, ((i + d_lon) % lon_count) * lat_count + k))
+    return pairs
+
+
+def fold_pairs(lon_count, lat_count, target_of):
+    top = lat_count - 1
+    return [(i * lat_count + top, (target_of(i) % lon_count) * lat_count + top) for i in range(lon_count)]
+
+
+def exchange(block, sign):
     lon_count = lax.axis_size("lon")
     lat_count = lax.axis_size("lat")
-    top = lat_count - 1
-    pairs = [(i * lat_count + top, (lon_count - 1 - i) * lat_count + top) for i in range(lon_count)]
-    mirrored = lax.ppermute(top_row, ("lon", "lat"), pairs)
-    return mirrored[:, :, ::-1] * fold_sign
+    axes = ("lon", "lat")
+    h = HALO
+
+    def send(piece, d_lon, d_lat):
+        return lax.ppermute(piece, axes, neighbour_pairs(lon_count, lat_count, d_lon, d_lat))
+
+    rows_lo, rows_hi = block[:, :h, :], block[:, -h:, :]
+    cols_lo, cols_hi = block[:, :, :h], block[:, :, -h:]
+    west = send(cols_hi, 1, 0)
+    east = send(cols_lo, -1, 0)
+    south = send(rows_hi, 0, 1)
+    north = send(rows_lo, 0, -1)
+    south_west = send(rows_hi[:, :, -h:], 1, 1)
+    south_east = send(rows_hi[:, :, :h], -1, 1)
+    north_west = send(rows_lo[:, :, -h:], 1, -1)
+    north_east = send(rows_lo[:, :, :h], -1, -1)
+
+    mirror = lax.ppermute(rows_hi, axes, fold_pairs(lon_count, lat_count, lambda i: lon_count - 1 - i))
+    mirror_lo = lax.ppermute(
+        rows_hi[:, :, :h], axes, fold_pairs(lon_count, lat_count, lambda i: lon_count - i)
+    )
+    mirror_hi = lax.ppermute(
+        rows_hi[:, :, -h:], axes, fold_pairs(lon_count, lat_count, lambda i: lon_count - 2 - i)
+    )
+    mirrored = jnp.concatenate([mirror_hi, mirror, mirror_lo], axis=2)
+    folded = mirrored[:, ::-1, ::-1] * sign[:, None, None]
+
+    is_top = lax.axis_index("lat") == lat_count - 1
+    north_row = jnp.concatenate([north_west, north, north_east], axis=2)
+    north_row = jnp.where(is_top, folded, north_row)
+    south_row = jnp.concatenate([south_west, south, south_east], axis=2)
+    middle = jnp.concatenate([west, block, east], axis=2)
+    return jnp.concatenate([south_row, middle, north_row], axis=1)
 
 
 def shards(
@@ -118,7 +170,7 @@
     layer_height,
 ):
     water_share = water_indicator.astype(jnp.float32)
-    combined_tracers = jnp.stack(
+    state = jnp.stack(
         [
             potential_heat * water_share,
             salt_anomaly_field * water_share,
@@ -127,35 +179,37 @@
             water_share,
         ]
     )
-    levels = combined_tracers.shape[1]
-    is_top = lax.axis_index("lat") == lax.axis_size("lat") - 1
-    at_bottom = (
-        lax.broadcasted_iota(jnp.int32, (levels, 1, 1), 0) == floor_layer_index[None]
-    ).astype(jnp.float32)
-    for step_index in range(2):
-        lon_padded = with_halo(combined_tracers, (("lon", 3),), 1, True)
-        lat_padded = with_halo(combined_tracers, (("lat", 2),), 1, False)
-        ghost_row = fold_ghost(combined_tracers[:, :, -1, :])
-        north_rim = jnp.where(is_top, ghost_row, lat_padded[:, :, -1, :])
-        northern = jnp.concatenate([lat_padded[:, :, 2:-1, :], north_rim[:, :, None, :]], axis=2)
-        southern = lat_padded[:, :, :-2, :]
-        eastern = lon_padded[..., 2:]
-        western = lon_padded[..., :-2]
-        combined_tracers = advance(
-            combined_tracers,
-            eastern,
-            western,
-            northern,
-            southern,
-            at_bottom,
-            zonal_spacing,
-            meridional_spacing,
-            planetary_rotation_factor,
-            horizontal_eddy_coefficient,
+    channels, levels, rows, cols = state.shape
+    params = jnp.concatenate(
+        [
+            jnp.stack(
+                [
+                    floor_layer_index.astype(jnp.float32),
+                    zonal_spacing,
+                    meridional_spacing,
+                    planetary_rotation_factor,
+                    horizontal_eddy_coefficient,
+                ]
+            ),
             diapycnal_diffusivity,
-            layer_height,
-        )
-    return (combined_tracers[0], combined_tracers[1], combined_tracers[2], combined_tracers[3])
+        ]
+    )
+    planes = jnp.concatenate([state.reshape(channels * levels, rows, cols), params])
+    channel_sign = jnp.array([1.0, 1.0, -1.0, -1.0, 1.0], jnp.float32)
+    sign = jnp.concatenate(
+        [jnp.repeat(channel_sign, levels), jnp.ones((params.shape[0],), jnp.float32)]
+    )
+    padded = exchange(planes, sign)
+    n_state = channels * levels
+    state0 = padded[:n_state].reshape(channels, levels, rows + 2 * HALO, cols + 2 * HALO)
+    params_outer = padded[n_state:, 1:-1, 1:-1]
+    state1 = step(state0, params_outer, levels, layer_height)
+    is_bottom = lax.axis_index("lat") == 0
+    first_row = jnp.where(is_bottom, 0.0, state1[:, :, :1, :])
+    state1 = jnp.concatenate([first_row, state1[:, :, 1:, :]], axis=2)
+    params_inner = params
+    state2 = step(state1, params_inner, levels, layer_height)
+    return (state2[0], state2[1], state2[2], state2[3])
 
 
 def solution(mesh):

time: 115 us -> 131 us (1.14)
  the two profiles are of different devices: /device:TPU:96 before, /device:TPU:511 now
where the time goes in v2:
time: 131 us; the launch traced here: 130 us
  starting transfers between devices  80.3 us (61%)
  other arithmetic  19.8 us (15%)
  waiting for transfers between devices  15.8 us (12%)
  local copies, waits for them, and re-layouts  12.6 us (10%)
    ppermute x8, starting transfers between devices, send(): lax.ppermute(piece, axes, neighbour_pairs(lon_count, lat_count, d_lon, d_...  59.6 us
    ppermute x8, waiting for transfers between devices, send(): lax.ppermute(piece, axes, neighbour_pairs(lon_count, lat_count, d_lon, d_...  15.8 us
    ppermute x1, starting transfers between devices, exchange(): lax.ppermute(rows_hi[:, :, :h], axes, fold_pairs(lon_count, lat_count, la...  13.8 us
    ppermute x1, starting transfers between devices, exchange(): lax.ppermute(rows_hi, axes, fold_pairs(lon_count, lat_count, lambda i: lo...  6.19 us
    slice x3, local copies, waits for them, and re-layouts, exchange(): cols_lo, cols_hi = (block[:, :, :h], block[:, :, -h:])  5.03 us
    add x2, other arithmetic, advance(): tendency = advection + diffusion + mixing  4.23 us
    ppermute x2, local copies, waits for them, and re-layouts, send(): lax.ppermute(piece, axes, neighbour_pairs(lon_count, lat_count, d_lon, d_...  3.51 us
    another operation x8, other arithmetic, pressure(): return jnp.cumsum(layer_mass, axis=0) - 0.5 * layer_mass  3.41 us
  transfers between devices with their start and end apart: 11, of which 2 were waited for; matrix products, arithmetic and copies ran while one was open for 9% of the time, Pallas kernels for 0%

profile of v2, /device:TPU:511, one launch (start us, length us, event | category | flops | bytes accessed | tf_op | source)
XLA Modules:
  0.0 129.8 jit_solution(16311656017535777100)
XLA Ops:
  0.7 1.1 bitcast_dynamic-update-slice_fusion.4
  1.7 1.0 bitcast_dynamic-update-slice_fusion.3
  2.8 1.1 bitcast_dynamic-update-slice_fusion.2
  5.0 6.2 %collective-permute-start.6 = (f32[28,2,128]{2,1,0:T(2,128)S(1)}, f32[28,2,128]{2,1,0:T(2,128)S(1)}, u32[]{:S(2)}, u32[]{:S(2)}) collective-permute-start(f32[28,2,128]{2,1,0:T(2,128)S(1)} %get-tuple-element.36), channel_id=1, source_target_pairs={{7,511},{15,503},{23,495},{31,487},{39,479},{47,471},{55,463},{63,... | collective-permute-start | bytes 86024 | tf_op jit(solution)/shard_map/ppermute | solution.py:140
  12.5 13.8 %collective-permute-start.7 = (f32[28,2,2]{2,1,0:T(2,128)S(1)}, f32[28,2,2]{2,1,0:T(2,128)}, u32[]{:S(2)}, u32[]{:S(2)}) collective-permute-start(f32[28,2,2]{2,1,0:T(2,128)S(1)} %get-tuple-element.35), channel_id=1, source_target_pairs={{7,7},{15,511},{23,503},{31,495},{39,487},{47,479},{55,471},{63,46... | collective-permute-start | bytes 1352 | tf_op jit(solution)/shard_map/ppermute | solution.py:141
  26.4 1.6 %fusion.103 = (f32[28,96,2]{2,1,0:T(8,128)S(1)}, f32[28,96,2]{2,1,0:T(8,128)}) fusion(f32[28,96,128]{2,1,0:T(8,128)S(1)} %constant_dynamic-update-slice_fusion), kind=kLoop, calls=%fused_computation.183 | loop fusion | bytes 86016 | tf_op jit(solution)/shard_map/slice | solution.py:130
  28.0 2.4 %copy.38 = f32[28,96,2]{1,2,0:T(2,128)} copy(f32[28,96,2]{2,1,0:T(8,128)} %get-tuple-element.31) | data formatting | bytes 43008 | tf_op jit(solution)/shard_map/slice | solution.py:130
  30.4 2.1 %collective-permute-start.4 = (f32[28,96,2]{1,2,0:T(2,128)}, f32[28,96,2]{1,2,0:T(2,128)}, u32[]{:S(2)}, u32[]{:S(2)}) collective-permute-start(f32[28,96,2]{1,2,0:T(2,128)} %copy.38), channel_id=1, source_target_pairs={{0,504},{1,505},{2,506},{3,507},{4,508},{5,509},{6,510},{7,511},{8... | collective-permute-start | bytes 64520 | tf_op jit(solution)/shard_map/ppermute | solution.py:127
  32.5 1.0 copy.37
  33.6 16.3 %collective-permute-start.3 = (f32[28,96,2]{1,2,0:T(2,128)}, f32[28,96,2]{1,2,0:T(2,128)}, u32[]{:S(2)}, u32[]{:S(2)}) collective-permute-start(f32[28,96,2]{1,2,0:T(2,128)} %copy.37), channel_id=1, source_target_pairs={{0,8},{1,9},{2,10},{3,11},{4,12},{5,13},{6,14},{7,15},{8,16},{9,17... | collective-permute-start | bytes 64520 | tf_op jit(solution)/shard_map/ppermute | solution.py:127
  50.2 0.9 collective-permute-done.3
  51.1 1.3 collective-permute-start.1
  52.4 1.2 copy.39
  53.6 1.3 collective-permute-start
  54.9 2.3 %copy.40 = f32[28,96,2]{2,1,0:T(8,128)} copy(f32[28,96,2]{1,2,0:T(2,128)} %collective-permute-done.4) | data formatting | bytes 43008 | tf_op jit(solution)/shard_map/ppermute | solution.py:127
  57.2 18.7 %collective-permute-start.9 = (f32[28,2,128]{2,1,0:T(2,128)S(1)}, f32[28,2,128]{2,1,0:T(2,128)}, u32[]{:S(2)}, u32[]{:S(2)}) collective-permute-start(f32[28,2,128]{2,1,0:T(2,128)S(1)} %get-tuple-element.37), channel_id=1, source_target_pairs={{1,0},{2,1},{3,2},{4,3},{5,4},{6,5},{7,6},{9,8},{10,9},{11,10},{12... | collective-permute-start | bytes 86024 | tf_op jit(solution)/shard_map/ppermute | solution.py:127
  76.0 1.9 %collective-permute-start.10 = (f32[28,2,2]{2,1,0:T(2,128)}, f32[28,2,2]{2,1,0:T(2,128)}, u32[]{:S(2)}, u32[]{:S(2)}) collective-permute-start(f32[28,2,2]{2,1,0:T(2,128)} %get-tuple-element.33), channel_id=1, source_target_pairs={{1,504},{2,505},{3,506},{4,507},{5,508},{6,509},{7,510},{9,0},{10,... | collective-permute-start | bytes 1352 | tf_op jit(solution)/shard_map/ppermute | solution.py:127
  77.8 16.7 %collective-permute-start.8 = (f32[28,2,2]{2,1,0:T(2,128)}, f32[28,2,2]{2,1,0:T(2,128)}, u32[]{:S(2)}, u32[]{:S(2)}) collective-permute-start(f32[28,2,2]{2,1,0:T(2,128)} %get-tuple-element.34), channel_id=1, source_target_pairs={{1,8},{2,9},{3,10},{4,11},{5,12},{6,13},{7,14},{9,16},{10,17},{11,... | collective-permute-start | bytes 1352 | tf_op jit(solution)/shard_map/ppermute | solution.py:127
  95.8 1.3 collective-permute-start.2
  97.2 1.0 maximum_select_fusion
  98.2 14.9 %collective-permute-done.2 = f32[28,2,2]{2,1,0:T(2,128)S(1)} collective-permute-done((f32[28,2,2]{2,1,0:T(2,128)S(1)}, f32[28,2,2]{2,1,0:T(2,128)S(1)}, u32[]{:S(2)}, u32[]{:S(2)}) %collective-permute-start.2) | collective-permute-done | bytes 480 | tf_op jit(solution)/shard_map/ppermute | solution.py:127
  113.1 2.6 %pad_maximum_fusion = f32[28,100,132]{2,1,0:T(8,128)S(1)} fusion(f32[28,2,132]{2,1,0:T(2,128)S(1)} %maximum_select_fusion, f32[28,96,2]{2,1,0:T(8,128)} %copy.40, f32[28,96,128]{2,1,0:T(8,128)S(1)} %constant_dynamic-update-slice_fusion, f32[28,96,2]{2,1,0:T(8,128)S(1)} %copy.39, f32[28,2,2]{2,1,0:T(2,128)S(1)} %collective-permute-done.2, ...), kind=kLoop, calls=%fused_computation | loop fusion | flops 2217600 | bytes 2956800 | tf_op jit(solution)/shard_map/concatenate | solution.py:155
  119.6 3.0 %divide_add_fusion = f32[4,4,98,130]{3,2,1,0:T(8,128)S(1)} fusion(f32[4,3,98,130]{3,2,1,0:T(8,128)S(1)} %fusion.3, f32[5,4,100,132]{3,2,1,0:T(8,128)S(1)} %bitcast.87, f32[4]{0:T(128)S(1)} %mul.628, f32[98,130]{1,0:T(8,128)S(1)} %get-tuple-element.46, f32[4,98,130]{2,1,0:T(8,128)S(1)} %get-tuple-element.21, f32[4,98,130]{2,1,0:T(8,128)S(1)} %get-tuple-element.22, ...), kind=kLoop, calls=%fused_computation.7 | loop fusion | flops 5299840 | bytes 6981536 | tf_op jit(solution)/shard_map/add | solution.py:66
  126.5 1.3 divide_add_fusion.1
  (79 shorter events, 13.5 us)
Async XLA Ops:
  0.6 3.3 %copy-start.1 = (s32[4,96,128]{2,1,0:T(8,128)S(1)}, s32[4,96,128]{2,1,0:T(8,128)}, u32[]{:S(2)}) copy-start(s32[4,96,128]{2,1,0:T(8,128)} %param.17) | copy-start | bytes 589828
  0.6 3.3 %copy-start.8 = (f32[4,96,128]{2,1,0:T(8,128)S(1)}, f32[4,96,128]{2,1,0:T(8,128)}, u32[]{:S(2)}) copy-start(f32[4,96,128]{2,1,0:T(8,128)} %param.16) | copy-start | bytes 589828
  2.8 1.3 copy-start.7
  2.8 1.3 %copy-start.5 = (f32[96,128]{1,0:T(8,128)S(1)}, f32[96,128]{1,0:T(8,128)}, u32[]{:S(2)}) copy-start(f32[96,128]{1,0:T(8,128)} %param.19) | copy-start | bytes 147460
  3.9 0.8 copy-start.6
  3.9 0.8 copy-start.3
  3.9 0.8 copy-start.4
  3.9 1.0 copy-start.2
  5.0 72.9 %collective-permute-start.6 = (f32[28,2,128]{2,1,0:T(2,128)S(1)}, f32[28,2,128]{2,1,0:T(2,128)S(1)}, u32[]{:S(2)}, u32[]{:S(2)}) collective-permute-start(f32[28,2,128]{2,1,0:T(2,128)S(1)} %get-tuple-element.36), channel_id=1, source_target_pairs={{7,511},{15,503},{23,495},{31,487},{39,479},{47,471},{55,463},{63,... | collective-permute-start | bytes 86024 | tf_op jit(solution)/shard_map/ppermute | solution.py:140
  11.9 45.3 %collective-permute-start.5 = (f32[28,2,2]{2,1,0:T(2,128)S(1)}, f32[28,2,2]{2,1,0:T(2,128)S(1)}, u32[]{:S(2)}, u32[]{:S(2)}) collective-permute-start(f32[28,2,2]{2,1,0:T(2,128)S(1)} %get-tuple-element.32), channel_id=1, source_target_pairs={{7,503},{15,495},{23,487},{31,479},{39,471},{47,463},{55,455},{63,... | collective-permute-start | bytes 1352 | tf_op jit(solution)/shard_map/ppermute | solution.py:144
  12.5 63.4 %collective-permute-start.7 = (f32[28,2,2]{2,1,0:T(2,128)S(1)}, f32[28,2,2]{2,1,0:T(2,128)}, u32[]{:S(2)}, u32[]{:S(2)}) collective-permute-start(f32[28,2,2]{2,1,0:T(2,128)S(1)} %get-tuple-element.35), channel_id=1, source_target_pairs={{7,7},{15,511},{23,503},{31,495},{39,487},{47,479},{55,471},{63,46... | collective-permute-start | bytes 1352 | tf_op jit(solution)/shard_map/ppermute | solution.py:141
  28.0 22.0 %copy-start.9 = (f32[4]{0:T(128)S(1)}, f32[4]{0:T(128)}, u32[]{:S(2)}) copy-start(f32[4]{0:T(128)} %param.24) | copy-start | bytes 52
  28.0 22.0 %copy-start.10 = (f32[5]{0:T(128)S(1)}, f32[5]{0:T(128)}, u32[]{:S(2)}) copy-start(f32[5]{0:T(128)} %constant.46.clone) | copy-start | bytes 64
  30.4 23.2 %collective-permute-start.4 = (f32[28,96,2]{1,2,0:T(2,128)}, f32[28,96,2]{1,2,0:T(2,128)}, u32[]{:S(2)}, u32[]{:S(2)}) collective-permute-start(f32[28,96,2]{1,2,0:T(2,128)} %copy.38), channel_id=1, source_target_pairs={{0,504},{1,505},{2,506},{3,507},{4,508},{5,509},{6,510},{7,511},{8... | collective-permute-start | bytes 64520 | tf_op jit(solution)/shard_map/ppermute | solution.py:127
  33.6 17.5 %collective-permute-start.3 = (f32[28,96,2]{1,2,0:T(2,128)}, f32[28,96,2]{1,2,0:T(2,128)}, u32[]{:S(2)}, u32[]{:S(2)}) collective-permute-start(f32[28,96,2]{1,2,0:T(2,128)} %copy.37), channel_id=1, source_target_pairs={{0,8},{1,9},{2,10},{3,11},{4,12},{5,13},{6,14},{7,15},{8,16},{9,17... | collective-permute-start | bytes 64520 | tf_op jit(solution)/shard_map/ppermute | solution.py:127
  51.1 62.0 %collective-permute-start.1 = (f32[28,2,128]{2,1,0:T(2,128)S(1)}, f32[28,2,128]{2,1,0:T(2,128)S(1)}, u32[]{:S(2)}, u32[]{:S(2)}) collective-permute-start(f32[28,2,128]{2,1,0:T(2,128)S(1)} %get-tuple-element.36), channel_id=1, source_target_pairs={{0,1},{1,2},{2,3},{3,4},{4,5},{5,6},{6,7},{8,9},{9,10},{10,11},{11... | collective-permute-start | bytes 86024 | tf_op jit(solution)/shard_map/ppermute | solution.py:127
  53.6 44.6 %collective-permute-start = (f32[28,2,2]{2,1,0:T(2,128)S(1)}, f32[28,2,2]{2,1,0:T(2,128)S(1)}, u32[]{:S(2)}, u32[]{:S(2)}) collective-permute-start(f32[28,2,2]{2,1,0:T(2,128)S(1)} %get-tuple-element.32), channel_id=1, source_target_pairs={{0,9},{1,10},{2,11},{3,12},{4,13},{5,14},{6,15},{8,17},{9,18},{10,... | collective-permute-start | bytes 1352 | tf_op jit(solution)/shard_map/ppermute | solution.py:127
  57.2 39.9 %collective-permute-start.9 = (f32[28,2,128]{2,1,0:T(2,128)S(1)}, f32[28,2,128]{2,1,0:T(2,128)}, u32[]{:S(2)}, u32[]{:S(2)}) collective-permute-start(f32[28,2,128]{2,1,0:T(2,128)S(1)} %get-tuple-element.37), channel_id=1, source_target_pairs={{1,0},{2,1},{3,2},{4,3},{5,4},{6,5},{7,6},{9,8},{10,9},{11,10},{12... | collective-permute-start | bytes 86024 | tf_op jit(solution)/shard_map/ppermute | solution.py:127
  76.0 19.9 %collective-permute-start.10 = (f32[28,2,2]{2,1,0:T(2,128)}, f32[28,2,2]{2,1,0:T(2,128)}, u32[]{:S(2)}, u32[]{:S(2)}) collective-permute-start(f32[28,2,2]{2,1,0:T(2,128)} %get-tuple-element.33), channel_id=1, source_target_pairs={{1,504},{2,505},{3,506},{4,507},{5,508},{6,509},{7,510},{9,0},{10,... | collective-permute-start | bytes 1352 | tf_op jit(solution)/shard_map/ppermute | solution.py:127
  77.8 19.3 %collective-permute-start.8 = (f32[28,2,2]{2,1,0:T(2,128)}, f32[28,2,2]{2,1,0:T(2,128)}, u32[]{:S(2)}, u32[]{:S(2)}) collective-permute-start(f32[28,2,2]{2,1,0:T(2,128)} %get-tuple-element.34), channel_id=1, source_target_pairs={{1,8},{2,9},{3,10},{4,11},{5,12},{6,13},{7,14},{9,16},{10,17},{11,... | collective-permute-start | bytes 1352 | tf_op jit(solution)/shard_map/ppermute | solution.py:127
  95.8 17.2 %collective-permute-start.2 = (f32[28,2,2]{2,1,0:T(2,128)S(1)}, f32[28,2,2]{2,1,0:T(2,128)S(1)}, u32[]{:S(2)}, u32[]{:S(2)}) collective-permute-start(f32[28,2,2]{2,1,0:T(2,128)S(1)} %get-tuple-element.35), channel_id=1, source_target_pairs={{0,505},{1,506},{2,507},{3,508},{4,509},{5,510},{6,511},{8,1},{9,2... | collective-permute-start | bytes 1352 | tf_op jit(solution)/shard_map/ppermute | solution.py:127
  116.7 1.3 %copy-start = (f32[28,96,2]{2,1,0:T(8,128)S(1)}, f32[28,96,2]{2,1,0:T(8,128)}, u32[]{:S(2)}) copy-start(f32[28,96,2]{2,1,0:T(8,128)} %copy.40) | copy-start | bytes 64516

commit v3 on v2

--- a/solution.py
+++ b/solution.py
@@ -102,16 +102,6 @@
     )
 
 
-def neighbour_pairs(lon_count, lat_count, d_lon, d_lat):
-    pairs = []
-    for i in range(lon_count):
-        for j in range(lat_count):
-            k = j + d_lat
-            if 0 <= k < lat_count:
-                pairs.append((i * lat_count + j, ((i + d_lon) % lon_count) * lat_count + k))
-    return pairs
-
-
 def fold_pairs(lon_count, lat_count, target_of):
     top = lat_count - 1
     return [(i * lat_count + top, (target_of(i) % lon_count) * lat_count + top) for i in range(lon_count)]
@@ -120,23 +110,15 @@
 def exchange(block, sign):
     lon_count = lax.axis_size("lon")
     lat_count = lax.axis_size("lat")
+    h = HALO
+
+    east_pairs = [(i, (i + 1) % lon_count) for i in range(lon_count)]
+    west_pairs = [(j, i) for i, j in east_pairs]
+    west = lax.ppermute(block[:, :, -h:], "lon", east_pairs)
+    east = lax.ppermute(block[:, :, :h], "lon", west_pairs)
+
     axes = ("lon", "lat")
-    h = HALO
-
-    def send(piece, d_lon, d_lat):
-        return lax.ppermute(piece, axes, neighbour_pairs(lon_count, lat_count, d_lon, d_lat))
-
-    rows_lo, rows_hi = block[:, :h, :], block[:, -h:, :]
-    cols_lo, cols_hi = block[:, :, :h], block[:, :, -h:]
-    west = send(cols_hi, 1, 0)
-    east = send(cols_lo, -1, 0)
-    south = send(rows_hi, 0, 1)
-    north = send(rows_lo, 0, -1)
-    south_west = send(rows_hi[:, :, -h:], 1, 1)
-    south_east = send(rows_hi[:, :, :h], -1, 1)
-    north_west = send(rows_lo[:, :, -h:], 1, -1)
-    north_east = send(rows_lo[:, :, :h], -1, -1)
-
+    rows_hi = block[:, -h:, :]
     mirror = lax.ppermute(rows_hi, axes, fold_pairs(lon_count, lat_count, lambda i: lon_count - 1 - i))
     mirror_lo = lax.ppermute(
         rows_hi[:, :, :h], axes, fold_pairs(lon_count, lat_count, lambda i: lon_count - i)
@@ -147,12 +129,14 @@
     mirrored = jnp.concatenate([mirror_hi, mirror, mirror_lo], axis=2)
     folded = mirrored[:, ::-1, ::-1] * sign[:, None, None]
 
+    middle = jnp.concatenate([west, block, east], axis=2)
+    north_pairs = [(j, j + 1) for j in range(lat_count - 1)]
+    south_pairs = [(j, i) for i, j in north_pairs]
+    south = lax.ppermute(middle[:, -h:, :], "lat", north_pairs)
+    north = lax.ppermute(middle[:, :h, :], "lat", south_pairs)
     is_top = lax.axis_index("lat") == lat_count - 1
-    north_row = jnp.concatenate([north_west, north, north_east], axis=2)
-    north_row = jnp.where(is_top, folded, north_row)
-    south_row = jnp.concatenate([south_west, south, south_east], axis=2)
-    middle = jnp.concatenate([west, block, east], axis=2)
-    return jnp.concatenate([south_row, middle, north_row], axis=1)
+    north = jnp.where(is_top, folded, north)
+    return jnp.concatenate([south, middle, north], axis=1)
 
 
 def shards(

time: 131 us -> 131 us (level)
  the two profiles are of different devices: /device:TPU:511 before, /device:TPU:193 now
where the time goes in v3:
time: 131 us; the launch traced here: 128 us
  local copies, waits for them, and re-layouts  60.6 us (46%)
  starting transfers between devices  38.6 us (29%)
  other arithmetic  20.8 us (16%)
  waiting for transfers between devices  6.76 us (5%)
    rev x1, local copies, waits for them, and re-layouts, exchange(): folded = mirrored[:, ::-1, ::-1] * sign[:, None, None]  29.3 us
    ppermute x1, starting transfers between devices, exchange(): south = lax.ppermute(middle[:, -h:, :], 'lat', north_pairs)  22.6 us
    unnamed x39, local copies, waits for them, and re-layouts  12.5 us
    ppermute x1, starting transfers between devices, exchange(): west = lax.ppermute(block[:, :, -h:], 'lon', east_pairs)  9.4 us
    ppermute x1, waiting for transfers between devices, exchange(): east = lax.ppermute(block[:, :, :h], 'lon', west_pairs)  6.74 us
    slice x2, local copies, waits for them, and re-layouts, exchange(): south = lax.ppermute(middle[:, -h:, :], 'lat', north_pairs)  5.04 us
    slice x2, local copies, waits for them, and re-layouts, exchange(): rows_hi = block[:, -h:, :]  3.84 us
    select_n x1, other arithmetic, exchange(): north = jnp.where(is_top, folded, north)  3.63 us
  transfers between devices with their start and end apart: 7, of which 1 were waited for; matrix products, arithmetic and copies ran while one was open for 41% of the time, Pallas kernels for 0%

profile of v3, /device:TPU:193, one launch (start us, length us, event | category | flops | bytes accessed | tf_op | source)
XLA Modules:
  0.0 127.9 jit_solution(2007390227169891091)
XLA Ops:
  3.4 1.5 %copy.67 = f32[96,128]{0,1:T(8,128)} copy(f32[96,128]{1,0:T(8,128)} %param.19) | data formatting | bytes 98304 | tf_op args[6]
  5.0 1.5 %copy.68 = f32[96,128]{0,1:T(8,128)} copy(f32[96,128]{1,0:T(8,128)} %param.20) | data formatting | bytes 98304 | tf_op args[7]
  6.5 1.0 copy.71
  7.5 1.1 bitcast_dynamic-update-slice_fusion.4
  11.6 9.4 %collective-permute-start = (f32[28,96,2]{1,2,0:T(2,128)S(1)}, f32[28,96,2]{1,2,0:T(2,128)S(1)}, u32[]{:S(2)}, u32[]{:S(2)}) collective-permute-start(f32[28,96,2]{1,2,0:T(2,128)S(1)} %get-tuple-element.29), channel_id=1, source_target_pairs={{0,8},{8,16},{16,24},{24,32},{32,40},{40,48},{48,56},{56,64},{64,7... | collective-permute-start | bytes 64520 | tf_op jit(solution)/shard_map/ppermute | solution.py:117
  21.0 1.9 %collective-permute-start.1 = (f32[28,96,2]{1,2,0:T(2,128)S(1)}, f32[28,96,2]{1,2,0:T(2,128)S(1)}, u32[]{:S(2)}, u32[]{:S(2)}) collective-permute-start(f32[28,96,2]{1,2,0:T(2,128)S(1)} %get-tuple-element.30), channel_id=1, source_target_pairs={{8,0},{16,8},{24,16},{32,24},{40,32},{48,40},{56,48},{64,56},{72,6... | collective-permute-start | bytes 64520 | tf_op jit(solution)/shard_map/ppermute | solution.py:118
  22.9 1.8 %slice.405 = f32[28,2,128]{1,2,0:T(8,128)} slice(f32[28,96,128]{1,2,0:T(8,128)S(1)} %constant_dynamic-update-slice_fusion), slice={[0:28], [94:96], [0:128]} | slice | bytes 57344 | tf_op jit(solution)/shard_map/slice | solution.py:121
  24.7 2.1 %copy.73 = f32[28,2,128]{2,1,0:T(2,128)S(1)} copy(f32[28,2,128]{1,2,0:T(8,128)} %slice.405) | data formatting | bytes 57344 | tf_op jit(solution)/shard_map/slice | solution.py:121
  28.2 6.7 %collective-permute-done.1 = f32[28,96,2]{1,2,0:T(2,128)S(1)} collective-permute-done((f32[28,96,2]{1,2,0:T(2,128)S(1)}, f32[28,96,2]{1,2,0:T(2,128)S(1)}, u32[]{:S(2)}, u32[]{:S(2)}) %collective-permute-start.1) | collective-permute-done | bytes 21536 | tf_op jit(solution)/shard_map/ppermute | solution.py:118
  35.1 2.4 %fusion.106 = (f32[28,2,132]{1,2,0:T(8,128)}, f32[28,2,132]{1,2,0:T(8,128)}) fusion(f32[28,96,132]{1,2,0:T(8,128)S(1)} %pad_maximum_fusion), kind=kLoop, calls=%fused_computation.189 | loop fusion | bytes 118272 | tf_op jit(solution)/shard_map/slice | solution.py:135
  37.6 2.6 %copy.72 = f32[28,2,132]{2,1,0:T(2,128)S(1)} copy(f32[28,2,132]{1,2,0:T(8,128)} %get-tuple-element.25) | data formatting | bytes 59136 | tf_op jit(solution)/shard_map/slice | solution.py:135
  40.2 2.6 %copy.75 = f32[28,2,132]{2,1,0:T(2,128)S(1)} copy(f32[28,2,132]{1,2,0:T(8,128)} %get-tuple-element.26) | data formatting | bytes 59136 | tf_op jit(solution)/shard_map/slice | solution.py:136
  42.8 2.6 %collective-permute-start.6 = (f32[28,2,132]{2,1,0:T(2,128)S(1)}, f32[28,2,132]{2,1,0:T(2,128)S(1)}, u32[]{:S(2)}, u32[]{:S(2)}) collective-permute-start(f32[28,2,132]{2,1,0:T(2,128)S(1)} %copy.75), channel_id=1, source_target_pairs={{1,0},{2,1},{3,2},{4,3},{5,4},{6,5},{7,6},{9,8},{10,9},{11,10},{12... | collective-permute-start | bytes 88712 | tf_op jit(solution)/shard_map/ppermute | solution.py:136
  45.4 22.6 %collective-permute-start.2 = (f32[28,2,132]{2,1,0:T(2,128)S(1)}, f32[28,2,132]{2,1,0:T(2,128)S(1)}, u32[]{:S(2)}, u32[]{:S(2)}) collective-permute-start(f32[28,2,132]{2,1,0:T(2,128)S(1)} %copy.72), channel_id=1, source_target_pairs={{0,1},{1,2},{2,3},{3,4},{4,5},{5,6},{6,7},{8,9},{9,10},{10,11},{11... | collective-permute-start | bytes 88712 | tf_op jit(solution)/shard_map/ppermute | solution.py:135
  68.0 1.8 %copy.74 = f32[28,2,128]{1,2,0:T(8,128)} copy(f32[28,2,128]{2,1,0:T(2,128)S(1)} %collective-permute-done.4) | data formatting | bytes 57344 | tf_op jit(solution)/shard_map/ppermute | solution.py:122
  69.9 3.0 %pad_maximum_fusion.1 = f32[28,2,132]{1,2,0:T(8,128)} fusion(f32[28,2,2]{1,2,0:T(2,128)S(1)} %collective-permute-done.5, f32[28,2,128]{1,2,0:T(8,128)} %copy.74, f32[28,2,2]{1,2,0:T(2,128)S(1)} %collective-permute-done.3), kind=kLoop, calls=%fused_computation.1 | loop fusion | flops 14784 | bytes 59136 | tf_op jit(solution)/shard_map/concatenate | solution.py:129
  72.9 29.3 %rev.3 = f32[28,2,132]{1,2,0:T(8,128)} reverse(f32[28,2,132]{1,2,0:T(8,128)} %pad_maximum_fusion.1), dimensions={1,2} | reverse | bytes 59136 | tf_op jit(solution)/shard_map/rev | solution.py:130
  102.2 1.9 %copy.76 = f32[28,2,132]{1,2,0:T(8,128)} copy(f32[28,2,132]{2,1,0:T(2,128)S(1)} %collective-permute-done.6) | data formatting | bytes 59136 | tf_op jit(solution)/shard_map/ppermute | solution.py:136
  104.1 3.6 %multiply_select_fusion = f32[28,2,132]{1,2,0:T(8,128)} fusion(f32[28,2,132]{1,2,0:T(8,128)} %copy.76, f32[28,2,132]{1,2,0:T(8,128)} %rev.3, f32[28]{0:T(128)S(1)} %concatenate.36, pred[]{:T(512)S(6)} %eq.50), kind=kLoop, calls=%fused_computation.3 | loop fusion | flops 14784 | bytes 88817 | tf_op jit(solution)/shard_map/jit(_where)/select_n | solution.py:138
  107.7 2.0 %copy.77 = f32[28,2,132]{1,2,0:T(8,128)} copy(f32[28,2,132]{2,1,0:T(2,128)S(1)} %collective-permute-done.2) | data formatting | bytes 59136 | tf_op jit(solution)/shard_map/ppermute | solution.py:135
  109.7 3.3 %pad_maximum_fusion.2 = f32[28,100,132]{1,2,0:T(8,128)S(1)} fusion(f32[28,2,132]{1,2,0:T(8,128)} %multiply_select_fusion, f32[28,96,2]{1,2,0:T(2,128)S(1)} %collective-permute-done.1, f32[28,96,128]{1,2,0:T(8,128)S(1)} %constant_dynamic-update-slice_fusion, f32[28,96,2]{1,2,0:T(2,128)S(1)} %collective-permute-done, f32[28,2,132]{1,2,0:T(8,128)} %copy.77), kind=kLoop, calls=%fused_computation.2 | loop fusion | flops 1478400 | bytes 2956800 | tf_op jit(solution)/shard_map/concatenate | solution.py:139
  114.3 1.0 copy-done
  117.2 1.4 %divide_add_fusion = f32[4,4,98,130]{2,3,1,0:T(8,128)S(1)} fusion(f32[4,3,98,130]{2,3,1,0:T(8,128)S(1)} %fusion.26, f32[5,4,100,132]{2,3,1,0:T(8,128)S(1)} %bitcast.86, f32[4]{0:T(128)S(1)} %mul.628, f32[98,130]{0,1:T(8,128)S(1)} %get-tuple-element.54, f32[4,98,130]{1,2,0:T(8,128)S(1)} %get-tuple-element.38, f32[4,98,130]{1,2,0:T(8,128)S(1)} %get-tuple-element.39, ...), kind=kLoop, calls=%fused_computation.36 | loop fusion | flops 5299840 | bytes 6981536 | tf_op jit(solution)/shard_map/add | solution.py:66
  122.0 1.3 %divide_add_fusion.1 = f32[4,4,96,128]{2,3,1,0:T(8,128)S(1)} fusion(f32[4,3,96,128]{2,3,1,0:T(8,128)S(1)} %fusion.27, f32[5,4,98,130]{2,3,1,0:T(8,128)S(1)} %fusion.3, f32[4,4,98,130]{2,3,1,0:T(8,128)S(1)} %fusion.17, f32[4]{0:T(128)S(1)} %mul.628, f32[96,128]{0,1:T(8,128)S(1)} %copy.82, f32[4,96,128]{1,2,0:T(8,128)S(1)} %get-tuple-element.34, ...), kind=kLoop, calls=%fused_computation.46 | loop fusion | flops 5111808 | bytes 6733840 | tf_op jit(solution)/shard_map/add | solution.py:66
  (92 shorter events, 18.1 us)
Async XLA Ops:
  0.6 8.0 %copy-start.2 = (s32[4,96,128]{2,1,0:T(8,128)S(1)}, s32[4,96,128]{2,1,0:T(8,128)}, u32[]{:S(2)}) copy-start(s32[4,96,128]{2,1,0:T(8,128)} %param.17) | copy-start | bytes 589828
  0.6 8.0 %copy-start.7 = (f32[4,96,128]{2,1,0:T(8,128)S(1)}, f32[4,96,128]{2,1,0:T(8,128)}, u32[]{:S(2)}) copy-start(f32[4,96,128]{2,1,0:T(8,128)} %param.14) | copy-start | bytes 589828
  0.7 8.0 %copy-start.8 = (f32[4,96,128]{2,1,0:T(8,128)S(1)}, f32[4,96,128]{2,1,0:T(8,128)}, u32[]{:S(2)}) copy-start(f32[4,96,128]{2,1,0:T(8,128)} %param.15) | copy-start | bytes 589828
  0.7 8.0 %copy-start.9 = (f32[4,96,128]{2,1,0:T(8,128)S(1)}, f32[4,96,128]{2,1,0:T(8,128)}, u32[]{:S(2)}) copy-start(f32[4,96,128]{2,1,0:T(8,128)} %param.16) | copy-start | bytes 589828
  9.2 0.8 copy-start.4
  9.2 0.9 copy-start.3
  10.2 59.7 %collective-permute-start.3 = (f32[28,2,2]{1,2,0:T(2,128)S(1)}, f32[28,2,2]{1,2,0:T(2,128)S(1)}, u32[]{:S(2)}, u32[]{:S(2)}) collective-permute-start(f32[28,2,2]{1,2,0:T(2,128)S(1)} %get-tuple-element.27), channel_id=1, source_target_pairs={{7,503},{15,495},{23,487},{31,479},{39,471},{47,463},{55,455},{63,... | collective-permute-start | bytes 1352 | tf_op jit(solution)/shard_map/ppermute | solution.py:126
  10.9 59.0 %collective-permute-start.5 = (f32[28,2,2]{1,2,0:T(2,128)S(1)}, f32[28,2,2]{1,2,0:T(2,128)S(1)}, u32[]{:S(2)}, u32[]{:S(2)}) collective-permute-start(f32[28,2,2]{1,2,0:T(2,128)S(1)} %get-tuple-element.28), channel_id=1, source_target_pairs={{7,7},{15,511},{23,503},{31,495},{39,487},{47,479},{55,471},{63,46... | collective-permute-start | bytes 1352 | tf_op jit(solution)/shard_map/ppermute | solution.py:123
  11.6 16.6 %collective-permute-start = (f32[28,96,2]{1,2,0:T(2,128)S(1)}, f32[28,96,2]{1,2,0:T(2,128)S(1)}, u32[]{:S(2)}, u32[]{:S(2)}) collective-permute-start(f32[28,96,2]{1,2,0:T(2,128)S(1)} %get-tuple-element.29), channel_id=1, source_target_pairs={{0,8},{8,16},{16,24},{24,32},{32,40},{40,48},{48,56},{56,64},{64,7... | collective-permute-start | bytes 64520 | tf_op jit(solution)/shard_map/ppermute | solution.py:117
  21.0 13.9 %collective-permute-start.1 = (f32[28,96,2]{1,2,0:T(2,128)S(1)}, f32[28,96,2]{1,2,0:T(2,128)S(1)}, u32[]{:S(2)}, u32[]{:S(2)}) collective-permute-start(f32[28,96,2]{1,2,0:T(2,128)S(1)} %get-tuple-element.30), channel_id=1, source_target_pairs={{8,0},{16,8},{24,16},{32,24},{40,32},{48,40},{56,48},{64,56},{72,6... | collective-permute-start | bytes 64520 | tf_op jit(solution)/shard_map/ppermute | solution.py:118
  24.7 2.7 %copy-start.5 = (f32[96,128]{1,0:T(8,128)S(1)}, f32[96,128]{1,0:T(8,128)}, u32[]{:S(2)}) copy-start(f32[96,128]{1,0:T(8,128)} %param.19) | copy-start | bytes 147460
  24.7 2.8 %copy-start.6 = (f32[96,128]{1,0:T(8,128)S(1)}, f32[96,128]{1,0:T(8,128)}, u32[]{:S(2)}) copy-start(f32[96,128]{1,0:T(8,128)} %param.20) | copy-start | bytes 147460
  24.7 2.8 %copy-start.10 = (f32[4]{0:T(128)S(1)}, f32[4]{0:T(128)}, u32[]{:S(2)}) copy-start(f32[4]{0:T(128)} %param.24) | copy-start | bytes 52
  24.7 2.9 %copy-start.11 = (f32[5]{0:T(128)S(1)}, f32[5]{0:T(128)}, u32[]{:S(2)}) copy-start(f32[5]{0:T(128)} %constant.46.clone) | copy-start | bytes 64
  26.8 41.3 %collective-permute-start.4 = (f32[28,2,128]{2,1,0:T(2,128)S(1)}, f32[28,2,128]{2,1,0:T(2,128)S(1)}, u32[]{:S(2)}, u32[]{:S(2)}) collective-permute-start(f32[28,2,128]{2,1,0:T(2,128)S(1)} %copy.73), channel_id=1, source_target_pairs={{7,511},{15,503},{23,495},{31,487},{39,479},{47,471},{55,463},{63,... | collective-permute-start | bytes 86024 | tf_op jit(solution)/shard_map/ppermute | solution.py:122
  42.8 59.4 %collective-permute-start.6 = (f32[28,2,132]{2,1,0:T(2,128)S(1)}, f32[28,2,132]{2,1,0:T(2,128)S(1)}, u32[]{:S(2)}, u32[]{:S(2)}) collective-permute-start(f32[28,2,132]{2,1,0:T(2,128)S(1)} %copy.75), channel_id=1, source_target_pairs={{1,0},{2,1},{3,2},{4,3},{5,4},{6,5},{7,6},{9,8},{10,9},{11,10},{12... | collective-permute-start | bytes 88712 | tf_op jit(solution)/shard_map/ppermute | solution.py:136
  45.4 62.3 %collective-permute-start.2 = (f32[28,2,132]{2,1,0:T(2,128)S(1)}, f32[28,2,132]{2,1,0:T(2,128)S(1)}, u32[]{:S(2)}, u32[]{:S(2)}) collective-permute-start(f32[28,2,132]{2,1,0:T(2,128)S(1)} %copy.72), channel_id=1, source_target_pairs={{0,1},{1,2},{2,3},{3,4},{4,5},{5,6},{6,7},{8,9},{9,10},{10,11},{11... | collective-permute-start | bytes 88712 | tf_op jit(solution)/shard_map/ppermute | solution.py:135
  113.8 1.5 %copy-start = (f32[28,2,132]{1,2,0:T(8,128)S(1)}, f32[28,2,132]{1,2,0:T(8,128)}, u32[]{:S(2)}) copy-start(f32[28,2,132]{1,2,0:T(8,128)} %multiply_select_fusion) | copy-start | bytes 88708
  113.8 2.1 %copy-start.1 = (f32[28,2,132]{1,2,0:T(8,128)S(1)}, f32[28,2,132]{1,2,0:T(8,128)}, u32[]{:S(2)}) copy-start(f32[28,2,132]{1,2,0:T(8,128)} %copy.77) | copy-start | bytes 88708

commit v4 on v3

--- a/solution.py
+++ b/solution.py
@@ -126,8 +126,11 @@
     mirror_hi = lax.ppermute(
         rows_hi[:, :, -h:], axes, fold_pairs(lon_count, lat_count, lambda i: lon_count - 2 - i)
     )
-    mirrored = jnp.concatenate([mirror_hi, mirror, mirror_lo], axis=2)
-    folded = mirrored[:, ::-1, ::-1] * sign[:, None, None]
+    mirrored = jnp.concatenate(
+        [mirror_lo[:, :, ::-1], mirror[:, :, ::-1], mirror_hi[:, :, ::-1]], axis=2
+    )
+    folded = jnp.concatenate([mirrored[:, 1:2, :], mirrored[:, 0:1, :]], axis=1)
+    folded = folded * sign[:, None, None]
 
     middle = jnp.concatenate([west, block, east], axis=2)
     north_pairs = [(j, j + 1) for j in range(lat_count - 1)]

time: 131 us -> 97.8 us (0.75)
  the two profiles are of different devices: /device:TPU:193 before, /device:TPU:449 now
where the time goes in v4:
time: 97.8 us; the launch traced here: 97.1 us
  starting transfers between devices  38.5 us (39%)
  local copies, waits for them, and re-layouts  32.3 us (33%)
  other arithmetic  18 us (18%)
  waiting for transfers between devices  6.96 us (7%)
  between operations  1.26 us (1%)
    ppermute x1, starting transfers between devices, exchange(): south = lax.ppermute(middle[:, -h:, :], 'lat', north_pairs)  26 us
    unnamed x39, local copies, waits for them, and re-layouts  12.5 us
    ppermute x1, waiting for transfers between devices, exchange(): east = lax.ppermute(block[:, :, :h], 'lon', west_pairs)  6.95 us
    ppermute x1, starting transfers between devices, exchange(): west = lax.ppermute(block[:, :, -h:], 'lon', east_pairs)  6.73 us
    slice x2, local copies, waits for them, and re-layouts, exchange(): south = lax.ppermute(middle[:, -h:, :], 'lat', north_pairs)  5.05 us
    slice x2, local copies, waits for them, and re-layouts, exchange(): rows_hi = block[:, -h:, :]  3.84 us
    select_n x1, other arithmetic, exchange(): north = jnp.where(is_top, folded, north)  3.64 us
    concatenate x1, other arithmetic, exchange(): return jnp.concatenate([south, middle, north], axis=1)  3.26 us
  transfers between devices with their start and end apart: 7, of which 1 were waited for; matrix products, arithmetic and copies ran while one was open for 22% of the time, Pallas kernels for 0%

profile of v4, /device:TPU:449, one launch (start us, length us, event | category | flops | bytes accessed | tf_op | source)
XLA Modules:
  0.0 97.1 jit_solution(18353371583816455965)
XLA Ops:
  0.7 1.0 copy.41
  1.6 0.9 copy.38
  3.4 1.5 %copy.39 = f32[96,128]{0,1:T(8,128)} copy(f32[96,128]{1,0:T(8,128)} %param.19) | data formatting | bytes 98304 | tf_op args[6]
  5.0 1.5 %copy.40 = f32[96,128]{0,1:T(8,128)} copy(f32[96,128]{1,0:T(8,128)} %param.20) | data formatting | bytes 98304 | tf_op args[7]
  6.5 1.0 %copy.43 = f32[3,96,128]{1,2,0:T(8,128)S(1)} copy(f32[3,96,128]{2,1,0:T(8,128)} %param.23) | data formatting | bytes 294912 | tf_op args[10]
  7.5 1.1 %bitcast_dynamic-update-slice_fusion.4 = f32[5,4,96,128]{3,2,1,0:T(8,128)S(1)} fusion(f32[4,96,128]{2,1,0:T(8,128)} %param.13, s32[4,96,128]{2,1,0:T(8,128)} %param.17), kind=kLoop, calls=%fused_computation.127 | loop fusion | flops 98303 | bytes 589824
  11.6 6.7 %collective-permute-start = (f32[28,96,2]{1,2,0:T(2,128)S(1)}, f32[28,96,2]{1,2,0:T(2,128)S(1)}, u32[]{:S(2)}, u32[]{:S(2)}) collective-permute-start(f32[28,96,2]{1,2,0:T(2,128)S(1)} %get-tuple-element.25), channel_id=1, source_target_pairs={{0,8},{8,16},{16,24},{24,32},{32,40},{40,48},{48,56},{56,64},{64,7... | collective-permute-start | bytes 64520 | tf_op jit(solution)/shard_map/ppermute | solution.py:117
  18.3 1.9 %collective-permute-start.1 = (f32[28,96,2]{1,2,0:T(2,128)S(1)}, f32[28,96,2]{1,2,0:T(2,128)S(1)}, u32[]{:S(2)}, u32[]{:S(2)}) collective-permute-start(f32[28,96,2]{1,2,0:T(2,128)S(1)} %get-tuple-element.26), channel_id=1, source_target_pairs={{8,0},{16,8},{24,16},{32,24},{40,32},{48,40},{56,48},{64,56},{72,6... | collective-permute-start | bytes 64520 | tf_op jit(solution)/shard_map/ppermute | solution.py:118
  20.2 1.8 %slice.413 = f32[28,2,128]{1,2,0:T(8,128)} slice(f32[28,96,128]{1,2,0:T(8,128)S(1)} %constant_dynamic-update-slice_fusion), slice={[0:28], [94:96], [0:128]} | slice | bytes 57344 | tf_op jit(solution)/shard_map/slice | solution.py:121
  22.0 2.1 %copy.45 = f32[28,2,128]{2,1,0:T(2,128)S(1)} copy(f32[28,2,128]{1,2,0:T(8,128)} %slice.413) | data formatting | bytes 57344 | tf_op jit(solution)/shard_map/slice | solution.py:121
  26.2 6.9 %collective-permute-done.1 = f32[28,96,2]{1,2,0:T(2,128)S(1)} collective-permute-done((f32[28,96,2]{1,2,0:T(2,128)S(1)}, f32[28,96,2]{1,2,0:T(2,128)S(1)}, u32[]{:S(2)}, u32[]{:S(2)}) %collective-permute-start.1) | collective-permute-done | bytes 21536 | tf_op jit(solution)/shard_map/ppermute | solution.py:118
  33.4 2.5 %fusion.106 = (f32[28,2,132]{1,2,0:T(8,128)}, f32[28,2,132]{1,2,0:T(8,128)}) fusion(f32[28,96,132]{1,2,0:T(8,128)S(1)} %pad_maximum_fusion), kind=kLoop, calls=%fused_computation.190 | loop fusion | bytes 118272 | tf_op jit(solution)/shard_map/slice | solution.py:138
  35.8 2.6 %copy.44 = f32[28,2,132]{2,1,0:T(2,128)S(1)} copy(f32[28,2,132]{1,2,0:T(8,128)} %get-tuple-element.21) | data formatting | bytes 59136 | tf_op jit(solution)/shard_map/slice | solution.py:138
  38.4 2.6 %copy.49 = f32[28,2,132]{2,1,0:T(2,128)S(1)} copy(f32[28,2,132]{1,2,0:T(8,128)} %get-tuple-element.22) | data formatting | bytes 59136 | tf_op jit(solution)/shard_map/slice | solution.py:139
  41.0 1.9 %collective-permute-start.6 = (f32[28,2,132]{2,1,0:T(2,128)S(1)}, f32[28,2,132]{2,1,0:T(2,128)S(1)}, u32[]{:S(2)}, u32[]{:S(2)}) collective-permute-start(f32[28,2,132]{2,1,0:T(2,128)S(1)} %copy.49), channel_id=1, source_target_pairs={{1,0},{2,1},{3,2},{4,3},{5,4},{6,5},{7,6},{9,8},{10,9},{11,10},{12... | collective-permute-start | bytes 88712 | tf_op jit(solution)/shard_map/ppermute | solution.py:139
  43.0 26.0 %collective-permute-start.2 = (f32[28,2,132]{2,1,0:T(2,128)S(1)}, f32[28,2,132]{2,1,0:T(2,128)S(1)}, u32[]{:S(2)}, u32[]{:S(2)}) collective-permute-start(f32[28,2,132]{2,1,0:T(2,128)S(1)} %copy.44), channel_id=1, source_target_pairs={{0,1},{1,2},{2,3},{3,4},{4,5},{5,6},{6,7},{8,9},{9,10},{10,11},{11... | collective-permute-start | bytes 88712 | tf_op jit(solution)/shard_map/ppermute | solution.py:138
  69.4 2.0 %copy.48 = f32[28,2,132]{1,2,0:T(8,128)} copy(f32[28,2,132]{2,1,0:T(2,128)S(1)} %pad_maximum_fusion.5) | data formatting | bytes 59136 | tf_op jit(solution)/shard_map/concatenate | solution.py:132
  71.4 1.9 %copy.50 = f32[28,2,132]{1,2,0:T(8,128)} copy(f32[28,2,132]{2,1,0:T(2,128)S(1)} %collective-permute-done.6) | data formatting | bytes 59136 | tf_op jit(solution)/shard_map/ppermute | solution.py:139
  73.3 3.6 %multiply_select_fusion = f32[28,2,132]{1,2,0:T(8,128)} fusion(f32[28,2,132]{1,2,0:T(8,128)} %copy.50, f32[28,2,132]{1,2,0:T(8,128)} %copy.48, f32[28]{0:T(128)S(1)} %concatenate.40, pred[]{:T(512)S(6)} %eq.50), kind=kLoop, calls=%fused_computation.2 | loop fusion | flops 14784 | bytes 88817 | tf_op jit(solution)/shard_map/jit(_where)/select_n | solution.py:141
  76.9 2.0 %copy.51 = f32[28,2,132]{1,2,0:T(8,128)} copy(f32[28,2,132]{2,1,0:T(2,128)S(1)} %collective-permute-done.2) | data formatting | bytes 59136 | tf_op jit(solution)/shard_map/ppermute | solution.py:138
  78.9 3.3 %pad_maximum_fusion.1 = f32[28,100,132]{1,2,0:T(8,128)S(1)} fusion(f32[28,2,132]{1,2,0:T(8,128)} %multiply_select_fusion, f32[28,96,2]{1,2,0:T(2,128)S(1)} %collective-permute-done.1, f32[28,96,128]{1,2,0:T(8,128)S(1)} %constant_dynamic-update-slice_fusion, f32[28,96,2]{1,2,0:T(2,128)S(1)} %collective-permute-done, f32[28,2,132]{1,2,0:T(8,128)} %copy.51), kind=kLoop, calls=%fused_computation.1 | loop fusion | flops 1478400 | bytes 2956800 | tf_op jit(solution)/shard_map/concatenate | solution.py:142
  83.5 1.0 %copy-done = f32[28,2,132]{1,2,0:T(8,128)S(1)} copy-done((f32[28,2,132]{1,2,0:T(8,128)S(1)}, f32[28,2,132]{1,2,0:T(8,128)}, u32[]{:S(2)}) %copy-start) | copy-done | bytes 29592
  86.4 1.4 %divide_add_fusion = f32[4,4,98,130]{2,3,1,0:T(8,128)S(1)} fusion(f32[4,3,98,130]{2,3,1,0:T(8,128)S(1)} %fusion.26, f32[5,4,100,132]{2,3,1,0:T(8,128)S(1)} %bitcast.86, f32[4]{0:T(128)S(1)} %mul.628, f32[98,130]{0,1:T(8,128)S(1)} %get-tuple-element.52, f32[4,98,130]{1,2,0:T(8,128)S(1)} %get-tuple-element.34, f32[4,98,130]{1,2,0:T(8,128)S(1)} %get-tuple-element.35, ...), kind=kLoop, calls=%fused_computation.35 | loop fusion | flops 5299840 | bytes 6981536 | tf_op jit(solution)/shard_map/add | solution.py:66
  91.1 1.3 %divide_add_fusion.1 = f32[4,4,96,128]{2,3,1,0:T(8,128)S(1)} fusion(f32[4,3,96,128]{2,3,1,0:T(8,128)S(1)} %fusion.27, f32[5,4,98,130]{2,3,1,0:T(8,128)S(1)} %fusion.3, f32[4,4,98,130]{2,3,1,0:T(8,128)S(1)} %fusion.17, f32[4]{0:T(128)S(1)} %mul.628, f32[96,128]{0,1:T(8,128)S(1)} %copy.56, f32[4,96,128]{1,2,0:T(8,128)S(1)} %get-tuple-element.30, ...), kind=kLoop, calls=%fused_computation.45 | loop fusion | flops 5111808 | bytes 6733840 | tf_op jit(solution)/shard_map/add | solution.py:66
  (98 shorter events, 17.4 us)
Async XLA Ops:
  0.6 8.0 %copy-start.2 = (s32[4,96,128]{2,1,0:T(8,128)S(1)}, s32[4,96,128]{2,1,0:T(8,128)}, u32[]{:S(2)}) copy-start(s32[4,96,128]{2,1,0:T(8,128)} %param.17) | copy-start | bytes 589828
  0.6 8.0 %copy-start.7 = (f32[4,96,128]{2,1,0:T(8,128)S(1)}, f32[4,96,128]{2,1,0:T(8,128)}, u32[]{:S(2)}) copy-start(f32[4,96,128]{2,1,0:T(8,128)} %param.14) | copy-start | bytes 589828
  0.7 8.0 %copy-start.8 = (f32[4,96,128]{2,1,0:T(8,128)S(1)}, f32[4,96,128]{2,1,0:T(8,128)}, u32[]{:S(2)}) copy-start(f32[4,96,128]{2,1,0:T(8,128)} %param.15) | copy-start | bytes 589828
  0.7 8.0 %copy-start.9 = (f32[4,96,128]{2,1,0:T(8,128)S(1)}, f32[4,96,128]{2,1,0:T(8,128)}, u32[]{:S(2)}) copy-start(f32[4,96,128]{2,1,0:T(8,128)} %param.16) | copy-start | bytes 589828
  9.2 0.8 copy-start.4
  9.2 0.9 copy-start.3
  10.2 15.3 %collective-permute-start.3 = (f32[28,2,2]{1,2,0:T(2,128)S(1)}, f32[28,2,2]{1,2,0:T(2,128)S(1)}, u32[]{:S(2)}, u32[]{:S(2)}) collective-permute-start(f32[28,2,2]{1,2,0:T(2,128)S(1)} %get-tuple-element.23), channel_id=1, source_target_pairs={{7,7},{15,511},{23,503},{31,495},{39,487},{47,479},{55,471},{63,46... | collective-permute-start | bytes 1352 | tf_op jit(solution)/shard_map/ppermute | solution.py:123
  10.9 15.0 %collective-permute-start.5 = (f32[28,2,2]{1,2,0:T(2,128)S(1)}, f32[28,2,2]{1,2,0:T(2,128)S(1)}, u32[]{:S(2)}, u32[]{:S(2)}) collective-permute-start(f32[28,2,2]{1,2,0:T(2,128)S(1)} %get-tuple-element.24), channel_id=1, source_target_pairs={{7,503},{15,495},{23,487},{31,479},{39,471},{47,463},{55,455},{63,... | collective-permute-start | bytes 1352 | tf_op jit(solution)/shard_map/ppermute | solution.py:126
  11.6 14.6 %collective-permute-start = (f32[28,96,2]{1,2,0:T(2,128)S(1)}, f32[28,96,2]{1,2,0:T(2,128)S(1)}, u32[]{:S(2)}, u32[]{:S(2)}) collective-permute-start(f32[28,96,2]{1,2,0:T(2,128)S(1)} %get-tuple-element.25), channel_id=1, source_target_pairs={{0,8},{8,16},{16,24},{24,32},{32,40},{40,48},{48,56},{56,64},{64,7... | collective-permute-start | bytes 64520 | tf_op jit(solution)/shard_map/ppermute | solution.py:117
  18.3 14.8 %collective-permute-start.1 = (f32[28,96,2]{1,2,0:T(2,128)S(1)}, f32[28,96,2]{1,2,0:T(2,128)S(1)}, u32[]{:S(2)}, u32[]{:S(2)}) collective-permute-start(f32[28,96,2]{1,2,0:T(2,128)S(1)} %get-tuple-element.26), channel_id=1, source_target_pairs={{8,0},{16,8},{24,16},{32,24},{40,32},{48,40},{56,48},{64,56},{72,6... | collective-permute-start | bytes 64520 | tf_op jit(solution)/shard_map/ppermute | solution.py:118
  22.0 2.7 %copy-start.5 = (f32[96,128]{1,0:T(8,128)S(1)}, f32[96,128]{1,0:T(8,128)}, u32[]{:S(2)}) copy-start(f32[96,128]{1,0:T(8,128)} %param.19) | copy-start | bytes 147460
  22.0 2.8 %copy-start.6 = (f32[96,128]{1,0:T(8,128)S(1)}, f32[96,128]{1,0:T(8,128)}, u32[]{:S(2)}) copy-start(f32[96,128]{1,0:T(8,128)} %param.20) | copy-start | bytes 147460
  22.0 2.8 %copy-start.10 = (f32[4]{0:T(128)S(1)}, f32[4]{0:T(128)}, u32[]{:S(2)}) copy-start(f32[4]{0:T(128)} %param.24) | copy-start | bytes 52
  22.0 2.9 %copy-start.11 = (f32[5]{0:T(128)S(1)}, f32[5]{0:T(128)}, u32[]{:S(2)}) copy-start(f32[5]{0:T(128)} %constant.46.clone) | copy-start | bytes 64
  24.1 44.8 %collective-permute-start.4 = (f32[28,2,128]{2,1,0:T(2,128)S(1)}, f32[28,2,128]{2,1,0:T(2,128)S(1)}, u32[]{:S(2)}, u32[]{:S(2)}) collective-permute-start(f32[28,2,128]{2,1,0:T(2,128)S(1)} %copy.45), channel_id=1, source_target_pairs={{7,511},{15,503},{23,495},{31,487},{39,479},{47,471},{55,463},{63,... | collective-permute-start | bytes 86024 | tf_op jit(solution)/shard_map/ppermute | solution.py:122
  41.0 30.3 %collective-permute-start.6 = (f32[28,2,132]{2,1,0:T(2,128)S(1)}, f32[28,2,132]{2,1,0:T(2,128)S(1)}, u32[]{:S(2)}, u32[]{:S(2)}) collective-permute-start(f32[28,2,132]{2,1,0:T(2,128)S(1)} %copy.49), channel_id=1, source_target_pairs={{1,0},{2,1},{3,2},{4,3},{5,4},{6,5},{7,6},{9,8},{10,9},{11,10},{12... | collective-permute-start | bytes 88712 | tf_op jit(solution)/shard_map/ppermute | solution.py:139
  43.0 34.0 %collective-permute-start.2 = (f32[28,2,132]{2,1,0:T(2,128)S(1)}, f32[28,2,132]{2,1,0:T(2,128)S(1)}, u32[]{:S(2)}, u32[]{:S(2)}) collective-permute-start(f32[28,2,132]{2,1,0:T(2,128)S(1)} %copy.44), channel_id=1, source_target_pairs={{0,1},{1,2},{2,3},{3,4},{4,5},{5,6},{6,7},{8,9},{9,10},{10,11},{11... | collective-permute-start | bytes 88712 | tf_op jit(solution)/shard_map/ppermute | solution.py:138
  82.9 1.5 %copy-start = (f32[28,2,132]{1,2,0:T(8,128)S(1)}, f32[28,2,132]{1,2,0:T(8,128)}, u32[]{:S(2)}) copy-start(f32[28,2,132]{1,2,0:T(8,128)} %multiply_select_fusion) | copy-start | bytes 88708
  83.0 2.1 %copy-start.1 = (f32[28,2,132]{1,2,0:T(8,128)S(1)}, f32[28,2,132]{1,2,0:T(8,128)}, u32[]{:S(2)}) copy-start(f32[28,2,132]{1,2,0:T(8,128)} %copy.51) | copy-start | bytes 88708

commit v5 on v4

--- a/solution.py
+++ b/solution.py
@@ -107,18 +107,20 @@
     return [(i * lat_count + top, (target_of(i) % lon_count) * lat_count + top) for i in range(lon_count)]
 
 
-def exchange(block, sign):
+def exchange(take, sign):
     lon_count = lax.axis_size("lon")
     lat_count = lax.axis_size("lat")
     h = HALO
+    every = slice(None)
 
     east_pairs = [(i, (i + 1) % lon_count) for i in range(lon_count)]
     west_pairs = [(j, i) for i, j in east_pairs]
-    west = lax.ppermute(block[:, :, -h:], "lon", east_pairs)
-    east = lax.ppermute(block[:, :, :h], "lon", west_pairs)
+    west = lax.ppermute(take(every, slice(-h, None)), "lon", east_pairs)
+    east = lax.ppermute(take(every, slice(0, h)), "lon", west_pairs)
 
     axes = ("lon", "lat")
-    rows_hi = block[:, -h:, :]
+    rows_hi = take(slice(-h, None), every)
+    rows_lo = take(slice(0, h), every)
     mirror = lax.ppermute(rows_hi, axes, fold_pairs(lon_count, lat_count, lambda i: lon_count - 1 - i))
     mirror_lo = lax.ppermute(
         rows_hi[:, :, :h], axes, fold_pairs(lon_count, lat_count, lambda i: lon_count - i)
@@ -132,14 +134,15 @@
     folded = jnp.concatenate([mirrored[:, 1:2, :], mirrored[:, 0:1, :]], axis=1)
     folded = folded * sign[:, None, None]
 
-    middle = jnp.concatenate([west, block, east], axis=2)
     north_pairs = [(j, j + 1) for j in range(lat_count - 1)]
     south_pairs = [(j, i) for i, j in north_pairs]
-    south = lax.ppermute(middle[:, -h:, :], "lat", north_pairs)
-    north = lax.ppermute(middle[:, :h, :], "lat", south_pairs)
+    top_band = jnp.concatenate([west[:, -h:, :], rows_hi, east[:, -h:, :]], axis=2)
+    bottom_band = jnp.concatenate([west[:, :h, :], rows_lo, east[:, :h, :]], axis=2)
+    south = lax.ppermute(top_band, "lat", north_pairs)
+    north = lax.ppermute(bottom_band, "lat", south_pairs)
     is_top = lax.axis_index("lat") == lat_count - 1
     north = jnp.where(is_top, folded, north)
-    return jnp.concatenate([south, middle, north], axis=1)
+    return west, east, south, north
 
 
 def shards(
@@ -156,37 +159,32 @@
     diapycnal_diffusivity,
     layer_height,
 ):
-    water_share = water_indicator.astype(jnp.float32)
-    state = jnp.stack(
-        [
-            potential_heat * water_share,
-            salt_anomaly_field * water_share,
-            zonal_current * water_share,
-            meridional_current * water_share,
-            water_share,
-        ]
-    )
-    channels, levels, rows, cols = state.shape
-    params = jnp.concatenate(
-        [
-            jnp.stack(
-                [
-                    floor_layer_index.astype(jnp.float32),
-                    zonal_spacing,
-                    meridional_spacing,
-                    planetary_rotation_factor,
-                    horizontal_eddy_coefficient,
-                ]
-            ),
-            diapycnal_diffusivity,
-        ]
-    )
-    planes = jnp.concatenate([state.reshape(channels * levels, rows, cols), params])
+    fields = (potential_heat, salt_anomaly_field, zonal_current, meridional_current)
+    surfaces = (
+        floor_layer_index,
+        zonal_spacing,
+        meridional_spacing,
+        planetary_rotation_factor,
+        horizontal_eddy_coefficient,
+    )
+
+    def take(rs, cs):
+        wet = water_indicator[:, rs, cs].astype(jnp.float32)
+        parts = [f[:, rs, cs] * wet for f in fields] + [wet]
+        parts += [s[None, rs, cs].astype(jnp.float32) for s in surfaces]
+        parts.append(diapycnal_diffusivity[:, rs, cs])
+        return jnp.concatenate(parts, axis=0)
+
+    channels = len(fields) + 1
+    levels, rows, cols = potential_heat.shape
     channel_sign = jnp.array([1.0, 1.0, -1.0, -1.0, 1.0], jnp.float32)
     sign = jnp.concatenate(
-        [jnp.repeat(channel_sign, levels), jnp.ones((params.shape[0],), jnp.float32)]
-    )
-    padded = exchange(planes, sign)
+        [jnp.repeat(channel_sign, levels), jnp.ones((len(surfaces) + levels - 1,), jnp.float32)]
+    )
+    west, east, south, north = exchange(take, sign)
+    every = slice(None)
+    middle = jnp.concatenate([west, take(every, every), east], axis=2)
+    padded = jnp.concatenate([south, middle, north], axis=1)
     n_state = channels * levels
     state0 = padded[:n_state].reshape(channels, levels, rows + 2 * HALO, cols + 2 * HALO)
     params_outer = padded[n_state:, 1:-1, 1:-1]
@@ -194,7 +192,7 @@
     is_bottom = lax.axis_index("lat") == 0
     first_row = jnp.where(is_bottom, 0.0, state1[:, :, :1, :])
     state1 = jnp.concatenate([first_row, state1[:, :, 1:, :]], axis=2)
-    params_inner = params
+    params_inner = padded[n_state:, HALO:-HALO, HALO:-HALO]
     state2 = step(state1, params_inner, levels, layer_height)
     return (state2[0], state2[1], state2[2], state2[3])
 

time: 97.8 us -> 84.3 us (0.86)
  the two profiles are of different devices: /device:TPU:449 before, /device:TPU:169 now
where the time goes in v5:
time: 84.3 us; the launch traced here: 83.8 us
  waiting for transfers between devices  26.1 us (31%)
  other arithmetic  22.9 us (27%)
  starting transfers between devices  20.1 us (24%)
  local copies, waits for them, and re-layouts  13.5 us (16%)
  between operations  1.28 us (2%)
    ppermute x1, waiting for transfers between devices, exchange(): north = lax.ppermute(bottom_band, 'lat', south_pairs)  25.2 us
    ppermute x1, starting transfers between devices, exchange(): west = lax.ppermute(take(every, slice(-h, None)), 'lon', east_pairs)  10.3 us
    unnamed x66, local copies, waits for them, and re-layouts  4.65 us
    unnamed x22, other arithmetic  4.34 us
    add x2, other arithmetic, advance(): tendency = advection + diffusion + mixing  4.23 us
    another operation x8, other arithmetic, pressure(): return jnp.cumsum(layer_mass, axis=0) - 0.5 * layer_mass  3.4 us
    ppermute x1, starting transfers between devices, exchange(): south = lax.ppermute(top_band, 'lat', north_pairs)  2.65 us
    ppermute x1, starting transfers between devices, exchange(): north = lax.ppermute(bottom_band, 'lat', south_pairs)  2.64 us
  transfers between devices with their start and end apart: 7, of which 2 were waited for; matrix products, arithmetic and copies ran while one was open for 16% of the time, Pallas kernels for 0%

profile of v5, /device:TPU:169, one launch (start us, length us, event | category | flops | bytes accessed | tf_op | source)
XLA Modules:
  0.0 83.8 jit_solution(11431623920874427095)
XLA Ops:
  0.7 1.2 %fusion.107 = (s32[4,96,2]{2,1,0:T(8,128)S(1)}, s32[4,96,2]{2,1,0:T(8,128)S(1)}) fusion(s32[4,96,128]{2,1,0:T(8,128)} %param.17), kind=kLoop, calls=%fused_computation.234 | loop fusion | bytes 12288 | tf_op jit(solution)/shard_map/slice | solution.py:172
  1.9 1.1 %fusion.108 = (f32[4,96,2]{2,1,0:T(8,128)S(1)}, f32[4,96,2]{2,1,0:T(8,128)S(1)}) fusion(f32[4,96,128]{2,1,0:T(8,128)} %param.13), kind=kLoop, calls=%fused_computation.235 | loop fusion | bytes 12288 | tf_op jit(solution)/shard_map/slice | solution.py:173
  5.2 10.3 %collective-permute-start = (f32[28,96,2]{1,2,0:T(2,128)S(1)}, f32[28,96,2]{1,2,0:T(2,128)S(1)}, u32[]{:S(2)}, u32[]{:S(2)}) collective-permute-start(f32[28,96,2]{1,2,0:T(2,128)S(1)} %constant_dynamic-update-slice_fusion), channel_id=1, source_target_pairs={{0,8},{8,16},{16,24},{24,32},{32,40},{40,48},{48,56},{56,64},{64,7... | collective-permute-start | bytes 64520 | tf_op jit(solution)/shard_map/ppermute | solution.py:118
  16.7 1.9 %collective-permute-start.1 = (f32[28,96,2]{1,2,0:T(2,128)S(1)}, f32[28,96,2]{1,2,0:T(2,128)S(1)}, u32[]{:S(2)}, u32[]{:S(2)}) collective-permute-start(f32[28,96,2]{1,2,0:T(2,128)S(1)} %constant_dynamic-update-slice_fusion.22), channel_id=1, source_target_pairs={{8,0},{16,8},{24,16},{32,24},{40,32},{48,40},{56,48},{64,56},{72,6... | collective-permute-start | bytes 64520 | tf_op jit(solution)/shard_map/ppermute | solution.py:119
  18.8 1.3 %collective-permute-start.4 = (f32[28,2,128]{2,1,0:T(2,128)S(1)}, f32[28,2,128]{2,1,0:T(2,128)}, u32[]{:S(2)}, u32[]{:S(2)}) collective-permute-start(f32[28,2,128]{2,1,0:T(2,128)S(1)} %get-tuple-element.52), channel_id=1, source_target_pairs={{7,511},{15,503},{23,495},{31,487},{39,479},{47,471},{55,463},{63,... | collective-permute-start | bytes 86024 | tf_op jit(solution)/shard_map/ppermute | solution.py:124
  21.5 0.7 multiply_dynamic-update-slice_fusion.3
  23.6 0.7 multiply_dynamic-update-slice_fusion
  29.7 0.9 %collective-permute-done.1 = f32[28,96,2]{1,2,0:T(2,128)S(1)} collective-permute-done((f32[28,96,2]{1,2,0:T(2,128)S(1)}, f32[28,96,2]{1,2,0:T(2,128)S(1)}, u32[]{:S(2)}, u32[]{:S(2)}) %collective-permute-start.1) | collective-permute-done | bytes 21536 | tf_op jit(solution)/shard_map/ppermute | solution.py:119
  31.1 2.6 %collective-permute-start.2 = (f32[28,2,132]{2,1,0:T(2,128)S(1)}, f32[28,2,132]{2,1,0:T(2,128)S(1)}, u32[]{:S(2)}, u32[]{:S(2)}) collective-permute-start(f32[28,2,132]{2,1,0:T(2,128)S(1)} %pad_maximum_fusion.3), channel_id=1, source_target_pairs={{0,1},{1,2},{2,3},{3,4},{4,5},{5,6},{6,7},{8,9},{9,10},{10,11},{11... | collective-permute-start | bytes 88712 | tf_op jit(solution)/shard_map/ppermute | solution.py:141
  34.5 2.6 %collective-permute-start.6 = (f32[28,2,132]{2,1,0:T(2,128)S(1)}, f32[28,2,132]{2,1,0:T(2,128)}, u32[]{:S(2)}, u32[]{:S(2)}) collective-permute-start(f32[28,2,132]{2,1,0:T(2,128)S(1)} %pad_maximum_fusion.5), channel_id=1, source_target_pairs={{1,0},{2,1},{3,2},{4,3},{5,4},{6,5},{7,6},{9,8},{10,9},{11,10},{12... | collective-permute-start | bytes 88712 | tf_op jit(solution)/shard_map/ppermute | solution.py:142
  38.1 0.9 %rev.10 = f32[28,2,128]{2,1,0:T(2,128)S(1)} reverse(f32[28,2,128]{2,1,0:T(2,128)} %collective-permute-done.4), dimensions={2} | reverse | bytes 57344 | tf_op jit(solution)/shard_map/rev | solution.py:132
  39.2 25.2 %collective-permute-done.6 = f32[28,2,132]{2,1,0:T(2,128)} collective-permute-done((f32[28,2,132]{2,1,0:T(2,128)S(1)}, f32[28,2,132]{2,1,0:T(2,128)}, u32[]{:S(2)}, u32[]{:S(2)}) %collective-permute-start.6) | collective-permute-done | bytes 29600 | tf_op jit(solution)/shard_map/ppermute | solution.py:142
  64.4 0.9 %fusion.87 = f32[28,2,132]{2,1,0:T(2,128)S(1)} fusion(f32[28,2,132]{2,1,0:T(2,128)} %collective-permute-done.6, f32[28,1,132]{2,1,0:T(1,128)S(1)} %get-tuple-element.61, f32[28,1,132]{2,1,0:T(1,128)S(1)} %get-tuple-element.60, pred[]{:T(512)S(6)} %eq.50, f32[28]{0:T(128)S(1)} %concatenate.63), kind=kLoop, calls=%fused_computation.206 | loop fusion | flops 22176 | bytes 88817 | tf_op jit(solution)/shard_map/jit(_where)/select_n | solution.py:144
  65.3 2.6 %pad_maximum_fusion = f32[28,100,132]{2,1,0:T(8,128)S(1)} fusion(f32[28,2,132]{2,1,0:T(2,128)S(1)} %fusion.87, f32[28,96,2]{2,1,0:T(8,128)S(1)} %copy.42, f32[28,96,128]{2,1,0:T(8,128)} %constant_dynamic-update-slice_fusion.33, f32[28,96,2]{2,1,0:T(8,128)S(1)} %copy.41, f32[28,2,132]{2,1,0:T(2,128)S(1)} %collective-permute-done.2), kind=kLoop, calls=%fused_computation | loop fusion | flops 1478400 | bytes 2956800 | tf_op jit(solution)/shard_map/concatenate | solution.py:187
  68.1 0.7 slice_bitcast_fusion.9
  69.6 1.3 %fusion.44 = f32[3,98,130]{2,1,0:T(8,128)S(1)} fusion(f32[5,4,100,132]{3,2,1,0:T(8,128)S(1)} %bitcast.113, f32[28,2,132]{2,1,0:T(2,128)S(1)} %fusion.87, f32[28,2,132]{2,1,0:T(2,128)S(1)} %collective-permute-done.2, f32[28,96,2]{2,1,0:T(8,128)S(1)} %copy.42, f32[28,96,128]{2,1,0:T(8,128)} %constant_dynamic-update-slice_fusion.33, f32[28,96,2]{2,1,0:T(8,128)S(1)} %copy.41), kind=kLoop, calls=%fused_computation.76 | loop fusion | flops 229320 | bytes 1937040 | tf_op jit(solution)/shard_map/mul | solution.py:20
  71.0 0.7 fusion.3
  71.7 1.0 %divide_bitcast_fusion.1 = (f32[98,130]{1,0:T(8,128)S(1)}, f32[1,98,130]{2,1,0:T(8,128)S(1)}, f32[98,130]{1,0:T(8,128)S(1)}, f32[1,98,130]{2,1,0:T(8,128)S(1)}) fusion(f32[28,2,132]{2,1,0:T(2,128)S(1)} %fusion.87, f32[28,96,2]{2,1,0:T(8,128)S(1)} %copy.42, f32[28,96,128]{2,1,0:T(8,128)} %constant_dynamic-update-slice_fusion.33, f32[28,96,2]{2,1,0:T(8,128)S(1)} %copy.41, ...), kind=kLoop, calls=%fused_computation.190 | loop fusion | flops 127400 | bytes 1682240 | tf_op jit(solution)/shard_map/div | solution.py:56
  72.8 1.1 %maximum_bitcast_fusion.1 = (f32[98,130]{1,0:T(8,128)S(1)}, f32[98,130]{1,0:T(8,128)S(1)}, f32[98,130]{1,0:T(8,128)S(1)}) fusion(f32[28,2,132]{2,1,0:T(2,128)S(1)} %fusion.87, f32[28,2,132]{2,1,0:T(2,128)S(1)} %collective-permute-done.2, f32[28,96,2]{2,1,0:T(8,128)S(1)} %copy.42, f32[28,96,128]{2,1,0:T(8,128)} %constant_dynamic-update-slice_fusion.33, ...), kind=kLoop, calls=%fused_computation.183 | loop fusion | flops 152880 | bytes 1631280 | tf_op jit(solution)/shard_map/mul | solution.py:69
  73.9 3.0 %divide_add_fusion = f32[4,4,98,130]{3,2,1,0:T(8,128)S(1)} fusion(f32[4,3,98,130]{3,2,1,0:T(8,128)S(1)} %fusion.3, f32[5,4,100,132]{3,2,1,0:T(8,128)S(1)} %bitcast.115, f32[4]{0:T(128)S(1)} %mul.694, f32[98,130]{1,0:T(8,128)S(1)} %get-tuple-element.88, f32[4,98,130]{2,1,0:T(8,128)S(1)} %get-tuple-element.19, f32[4,98,130]{2,1,0:T(8,128)S(1)} %get-tuple-element.20, ...), kind=kLoop, calls=%fused_computation.7 | loop fusion | flops 5299840 | bytes 6981536 | tf_op jit(solution)/shard_map/add | solution.py:66
  76.9 0.8 fusion.25
  77.7 0.8 fusion.26
  80.5 1.3 %divide_add_fusion.1 = f32[4,4,96,128]{3,2,1,0:T(8,128)S(1)} fusion(f32[4,3,96,128]{3,2,1,0:T(8,128)S(1)} %fusion.24, f32[5,4,98,130]{3,2,1,0:T(8,128)S(1)} %fusion, f32[4,4,98,130]{3,2,1,0:T(8,128)S(1)} %fusion.2, f32[4]{0:T(128)S(1)} %mul.694, f32[96,128]{1,0:T(8,128)S(1)} %get-tuple-element.59, f32[4,96,128]{2,1,0:T(8,128)S(1)} %get-tuple-element.16, ...), kind=kLoop, calls=%fused_computation.39 | loop fusion | flops 5111808 | bytes 6733840 | tf_op jit(solution)/shard_map/add | solution.py:66
  82.9 0.9 %slice_bitcast_fusion.2 = (f32[4,96,128]{2,1,0:T(8,128)}, f32[4,96,128]{2,1,0:T(8,128)}, f32[4,96,128]{2,1,0:T(8,128)}, f32[4,96,128]{2,1,0:T(8,128)}) fusion(f32[4,4,96,128]{3,2,1,0:T(8,128)S(1)} %fusion.23), kind=kLoop, calls=%fused_computation.91 | loop fusion | bytes 1572864 | tf_op jit(solution)/shard_map/squeeze | solution.py:197
  (146 shorter events, 18.0 us)
Async XLA Ops:
  0.6 2.6 %copy-start.3 = (f32[4,96,128]{2,1,0:T(8,128)S(1)}, f32[4,96,128]{2,1,0:T(8,128)}, u32[]{:S(2)}) copy-start(f32[4,96,128]{2,1,0:T(8,128)} %param.14) | copy-start | bytes 589828
  0.6 2.8 %copy-start.4 = (f32[4,96,128]{2,1,0:T(8,128)S(1)}, f32[4,96,128]{2,1,0:T(8,128)}, u32[]{:S(2)}) copy-start(f32[4,96,128]{2,1,0:T(8,128)} %param.15) | copy-start | bytes 589828
  1.8 1.9 %copy-start.5 = (f32[4,96,128]{2,1,0:T(8,128)S(1)}, f32[4,96,128]{2,1,0:T(8,128)}, u32[]{:S(2)}) copy-start(f32[4,96,128]{2,1,0:T(8,128)} %param.16) | copy-start | bytes 589828
  3.1 0.9 %copy-start.10 = (s32[96,128]{1,0:T(8,128)S(1)}, s32[96,128]{1,0:T(8,128)}, u32[]{:S(2)}) copy-start(s32[96,128]{1,0:T(8,128)} %param.18) | copy-start | bytes 147460
  3.1 1.1 %copy-start.8 = (f32[96,128]{1,0:T(8,128)S(1)}, f32[96,128]{1,0:T(8,128)}, u32[]{:S(2)}) copy-start(f32[96,128]{1,0:T(8,128)} %param.19) | copy-start | bytes 147460
  3.2 1.2 %copy-start.9 = (f32[96,128]{1,0:T(8,128)S(1)}, f32[96,128]{1,0:T(8,128)}, u32[]{:S(2)}) copy-start(f32[96,128]{1,0:T(8,128)} %param.20) | copy-start | bytes 147460
  3.2 1.3 %copy-start.6 = (f32[96,128]{1,0:T(8,128)S(1)}, f32[96,128]{1,0:T(8,128)}, u32[]{:S(2)}) copy-start(f32[96,128]{1,0:T(8,128)} %param.21) | copy-start | bytes 147460
  3.4 1.4 %copy-start.7 = (f32[96,128]{1,0:T(8,128)S(1)}, f32[96,128]{1,0:T(8,128)}, u32[]{:S(2)}) copy-start(f32[96,128]{1,0:T(8,128)} %param.22) | copy-start | bytes 147460
  3.4 1.5 %copy-start.1 = (f32[3,96,128]{2,1,0:T(8,128)S(1)}, f32[3,96,128]{2,1,0:T(8,128)}, u32[]{:S(2)}) copy-start(f32[3,96,128]{2,1,0:T(8,128)} %param.23) | copy-start | bytes 442372
  4.0 14.5 %copy-start = (s32[4,96,128]{2,1,0:T(8,128)S(1)}, s32[4,96,128]{2,1,0:T(8,128)}, u32[]{:S(2)}) copy-start(s32[4,96,128]{2,1,0:T(8,128)} %param.17) | copy-start | bytes 589828
  4.0 14.5 %copy-start.2 = (f32[4,96,128]{2,1,0:T(8,128)S(1)}, f32[4,96,128]{2,1,0:T(8,128)}, u32[]{:S(2)}) copy-start(f32[4,96,128]{2,1,0:T(8,128)} %param.13) | copy-start | bytes 589828
  5.2 24.1 %collective-permute-start = (f32[28,96,2]{1,2,0:T(2,128)S(1)}, f32[28,96,2]{1,2,0:T(2,128)S(1)}, u32[]{:S(2)}, u32[]{:S(2)}) collective-permute-start(f32[28,96,2]{1,2,0:T(2,128)S(1)} %constant_dynamic-update-slice_fusion), channel_id=1, source_target_pairs={{0,8},{8,16},{16,24},{24,32},{32,40},{40,48},{48,56},{56,64},{64,7... | collective-permute-start | bytes 64520 | tf_op jit(solution)/shard_map/ppermute | solution.py:118
  16.7 13.9 %collective-permute-start.1 = (f32[28,96,2]{1,2,0:T(2,128)S(1)}, f32[28,96,2]{1,2,0:T(2,128)S(1)}, u32[]{:S(2)}, u32[]{:S(2)}) collective-permute-start(f32[28,96,2]{1,2,0:T(2,128)S(1)} %constant_dynamic-update-slice_fusion.22), channel_id=1, source_target_pairs={{8,0},{16,8},{24,16},{32,24},{40,32},{48,40},{56,48},{64,56},{72,6... | collective-permute-start | bytes 64520 | tf_op jit(solution)/shard_map/ppermute | solution.py:119
  18.8 19.3 %collective-permute-start.4 = (f32[28,2,128]{2,1,0:T(2,128)S(1)}, f32[28,2,128]{2,1,0:T(2,128)}, u32[]{:S(2)}, u32[]{:S(2)}) collective-permute-start(f32[28,2,128]{2,1,0:T(2,128)S(1)} %get-tuple-element.52), channel_id=1, source_target_pairs={{7,511},{15,503},{23,495},{31,487},{39,479},{47,471},{55,463},{63,... | collective-permute-start | bytes 86024 | tf_op jit(solution)/shard_map/ppermute | solution.py:124
  20.2 8.9 %collective-permute-start.5 = (f32[28,2,2]{2,1,0:T(2,128)S(1)}, f32[28,2,2]{2,1,0:T(2,128)S(1)}, u32[]{:S(2)}, u32[]{:S(2)}) collective-permute-start(f32[28,2,2]{2,1,0:T(2,128)S(1)} %get-tuple-element.87), channel_id=1, source_target_pairs={{7,503},{15,495},{23,487},{31,479},{39,471},{47,463},{55,455},{63,... | collective-permute-start | bytes 1352 | tf_op jit(solution)/shard_map/ppermute | solution.py:128
  20.8 8.3 %collective-permute-start.3 = (f32[28,2,2]{2,1,0:T(2,128)S(1)}, f32[28,2,2]{2,1,0:T(2,128)S(1)}, u32[]{:S(2)}, u32[]{:S(2)}) collective-permute-start(f32[28,2,2]{2,1,0:T(2,128)S(1)} %get-tuple-element.86), channel_id=1, source_target_pairs={{7,7},{15,511},{23,503},{31,495},{39,487},{47,479},{55,471},{63,46... | collective-permute-start | bytes 1352 | tf_op jit(solution)/shard_map/ppermute | solution.py:125
  22.2 6.6 %copy-start.12 = (f32[5]{0:T(128)S(1)}, f32[5]{0:T(128)}, u32[]{:S(2)}) copy-start(f32[5]{0:T(128)} %constant.46.clone) | copy-start | bytes 64
  22.2 6.8 %copy-start.11 = (f32[4]{0:T(128)S(1)}, f32[4]{0:T(128)}, u32[]{:S(2)}) copy-start(f32[4]{0:T(128)} %param.24) | copy-start | bytes 52
  31.1 34.2 %collective-permute-start.2 = (f32[28,2,132]{2,1,0:T(2,128)S(1)}, f32[28,2,132]{2,1,0:T(2,128)S(1)}, u32[]{:S(2)}, u32[]{:S(2)}) collective-permute-start(f32[28,2,132]{2,1,0:T(2,128)S(1)} %pad_maximum_fusion.3), channel_id=1, source_target_pairs={{0,1},{1,2},{2,3},{3,4},{4,5},{5,6},{6,7},{8,9},{9,10},{10,11},{11... | collective-permute-start | bytes 88712 | tf_op jit(solution)/shard_map/ppermute | solution.py:141
  34.5 29.9 %collective-permute-start.6 = (f32[28,2,132]{2,1,0:T(2,128)S(1)}, f32[28,2,132]{2,1,0:T(2,128)}, u32[]{:S(2)}, u32[]{:S(2)}) collective-permute-start(f32[28,2,132]{2,1,0:T(2,128)S(1)} %pad_maximum_fusion.5), channel_id=1, source_target_pairs={{1,0},{2,1},{3,2},{4,3},{5,4},{6,5},{7,6},{9,8},{10,9},{11,10},{12... | collective-permute-start | bytes 88712 | tf_op jit(solution)/shard_map/ppermute | solution.py:142

commit v6 on v5

--- a/solution.py
+++ b/solution.py
@@ -183,17 +183,32 @@
     )
     west, east, south, north = exchange(take, sign)
     every = slice(None)
+    n_state = channels * levels
+
+    def split(planes):
+        count = planes.shape[1]
+        return planes[:n_state].reshape(channels, levels, count, planes.shape[2]), planes[n_state:]
+
     middle = jnp.concatenate([west, take(every, every), east], axis=2)
-    padded = jnp.concatenate([south, middle, north], axis=1)
-    n_state = channels * levels
-    state0 = padded[:n_state].reshape(channels, levels, rows + 2 * HALO, cols + 2 * HALO)
-    params_outer = padded[n_state:, 1:-1, 1:-1]
-    state1 = step(state0, params_outer, levels, layer_height)
+    state_mid, params_mid = split(middle)
+    inner = slice(HALO, -HALO)
+    state1_core = step(state_mid, params_mid[:, 1:-1, 1:-1], levels, layer_height)
+    state2_core = step(state1_core, params_mid[:, 2:-2, inner], levels, layer_height)
+
+    state_low, params_low = split(jnp.concatenate([south, middle[:, :HALO]], axis=1))
+    state1_low = step(state_low, params_low[:, 1:-1, 1:-1], levels, layer_height)
     is_bottom = lax.axis_index("lat") == 0
-    first_row = jnp.where(is_bottom, 0.0, state1[:, :, :1, :])
-    state1 = jnp.concatenate([first_row, state1[:, :, 1:, :]], axis=2)
-    params_inner = padded[n_state:, HALO:-HALO, HALO:-HALO]
-    state2 = step(state1, params_inner, levels, layer_height)
+    state1_low = jnp.concatenate(
+        [jnp.where(is_bottom, 0.0, state1_low[:, :, :1]), state1_low[:, :, 1:]], axis=2
+    )
+    state_high, params_high = split(jnp.concatenate([middle[:, -HALO:], north], axis=1))
+    state1_high = step(state_high, params_high[:, 1:-1, 1:-1], levels, layer_height)
+
+    band_low = jnp.concatenate([state1_low, state1_core[:, :, :2]], axis=2)
+    state2_low = step(band_low, params_mid[:, :2, inner], levels, layer_height)
+    band_high = jnp.concatenate([state1_core[:, :, -2:], state1_high], axis=2)
+    state2_high = step(band_high, params_mid[:, -2:, inner], levels, layer_height)
+    state2 = jnp.concatenate([state2_low, state2_core, state2_high], axis=2)
     return (state2[0], state2[1], state2[2], state2[3])
 
 

time: 84.3 us -> 161 us (1.91)
  the two profiles are of different devices: /device:TPU:169 before, /device:TPU:192 now
where the time goes in v6:
time: 161 us; the launch traced here: 158 us
  other arithmetic  53.7 us (33%)
  local copies, waits for them, and re-layouts  52.3 us (32%)
  starting transfers between devices  49.8 us (31%)
  between operations  1.94 us (1%)
    ppermute x1, starting transfers between devices, exchange(): south = lax.ppermute(top_band, 'lat', north_pairs)  25.4 us
    unnamed x157, local copies, waits for them, and re-layouts  23.3 us
    ppermute x1, starting transfers between devices, exchange(): east = lax.ppermute(take(every, slice(0, h)), 'lon', west_pairs)  16.6 us
    unnamed x22, other arithmetic  12.3 us
    another operation x24, other arithmetic, pressure(): return jnp.cumsum(layer_mass, axis=0) - 0.5 * layer_mass  6.31 us
    slice x4, local copies, waits for them, and re-layouts, take(): parts += [s[None, rs, cs].astype(jnp.float32) for s in surfaces]  6.15 us
    mul x9, other arithmetic, mix_vertically(): diapycnal_diffusivity * (water_share[1:] * water_share[:-1]) * contrast  6.13 us
    mul x10, other arithmetic, advance(): updated = water_share * (fields + TIME_STEP * tendency)  5.8 us
  transfers between devices with their start and end apart: 7, of which 0 were waited for; matrix products, arithmetic and copies ran while one was open for 48% of the time, Pallas kernels for 0%

profile of v6, /device:TPU:192, one launch (start us, length us, event | category | flops | bytes accessed | tf_op | source)
XLA Modules:
  0.0 157.8 jit_solution(16234359871098250837)
XLA Ops:
  0.7 1.4 constant_dynamic-update-slice_fusion.21
  16.4 1.5 fusion.340
  21.6 1.5 fusion.337
  23.1 1.5 fusion.336
  24.6 1.6 fusion.335
  26.2 1.6 fusion.334
  36.3 1.9 %collective-permute-start = (f32[28,96,2]{1,2,0:T(2,128)S(1)}, f32[28,96,2]{1,2,0:T(2,128)S(1)}, u32[]{:S(2)}, u32[]{:S(2)}) collective-permute-start(f32[28,96,2]{1,2,0:T(2,128)S(1)} %constant_dynamic-update-slice_fusion), channel_id=1, source_target_pairs={{0,8},{8,16},{16,24},{24,32},{32,40},{40,48},{48,56},{56,64},{64,7... | collective-permute-start | bytes 64520 | tf_op jit(solution)/shard_map/ppermute | solution.py:118
  42.6 16.6 %collective-permute-start.1 = (f32[28,96,2]{1,2,0:T(2,128)S(1)}, f32[28,96,2]{1,2,0:T(2,128)S(1)}, u32[]{:S(2)}, u32[]{:S(2)}) collective-permute-start(f32[28,96,2]{1,2,0:T(2,128)S(1)} %constant_dynamic-update-slice_fusion.22), channel_id=1, source_target_pairs={{8,0},{16,8},{24,16},{32,24},{40,32},{48,40},{56,48},{64,56},{72,6... | collective-permute-start | bytes 64520 | tf_op jit(solution)/shard_map/ppermute | solution.py:119
  71.0 1.5 rev.9
  72.5 1.5 rev.11
  75.1 1.5 maximum_bitcast_fusion.4
  76.6 2.6 %pad_maximum_fusion = f32[28,96,132]{2,1,0:T(8,128)S(1)} fusion(f32[28,96,2]{2,1,0:T(8,128)S(1)} %copy.42, f32[28,96,128]{2,1,0:T(8,128)} %constant_dynamic-update-slice_fusion.33, f32[28,96,2]{2,1,0:T(8,128)S(1)} %copy.41), kind=kLoop, calls=%fused_computation | loop fusion | flops 709632 | bytes 2838528 | tf_op jit(solution)/shard_map/concatenate | solution.py:192
  84.6 1.4 slice_bitcast_fusion.20
  86.7 2.5 %divide_add_fusion = f32[4,4,94,130]{3,2,1,0:T(8,128)S(1)} fusion(f32[4,3,94,130]{3,2,1,0:T(8,128)S(1)} %fusion.4, f32[5,4,96,132]{3,2,1,0:T(8,128)S(1)} %bitcast.258, f32[4]{0:T(128)S(1)} %mul.1838, f32[94,130]{1,0:T(8,128)S(1)} %get-tuple-element.178, f32[4,94,130]{2,1,0:T(8,128)S(1)} %get-tuple-element.61, f32[4,94,130]{2,1,0:T(8,128)S(1)} %get-tuple-element.62, ...), kind=kLoop, calls=%fused_computation.4 | loop fusion | flops 5083520 | bytes 6696576 | tf_op jit(solution)/shard_map/add | solution.py:66
  94.9 1.6 %copy.40 = f32[28,2,2]{2,1,0:T(2,128)} copy(f32[28,2,2]{1,2,0:T(2,128)} %get-tuple-element.165) | data formatting | bytes 896 | tf_op jit(solution)/shard_map/slice | solution.py:139
  96.5 1.6 %copy.44 = f32[28,2,2]{2,1,0:T(2,128)} copy(f32[28,2,2]{1,2,0:T(2,128)} %get-tuple-element.166) | data formatting | bytes 896 | tf_op jit(solution)/shard_map/slice | solution.py:140
  98.1 1.5 fusion.338
  99.6 1.6 %copy.39 = f32[28,2,2]{2,1,0:T(2,128)} copy(f32[28,2,2]{1,2,0:T(2,128)} %get-tuple-element.163) | data formatting | bytes 896 | tf_op jit(solution)/shard_map/slice | solution.py:139
  101.3 1.6 %copy.43 = f32[28,2,2]{2,1,0:T(2,128)} copy(f32[28,2,2]{1,2,0:T(2,128)} %get-tuple-element.164) | data formatting | bytes 896 | tf_op jit(solution)/shard_map/slice | solution.py:140
  102.9 1.7 %pad_maximum_fusion.14 = f32[28,2,132]{2,1,0:T(2,128)} fusion(f32[28,2,2]{2,1,0:T(2,128)} %copy.44, f32[28,2,128]{2,1,0:T(2,128)} %copy-done.42, f32[28,2,2]{2,1,0:T(2,128)} %copy.43), kind=kLoop, calls=%fused_computation.268 | loop fusion | flops 14784 | bytes 59136 | tf_op jit(solution)/shard_map/concatenate | solution.py:140
  104.6 2.0 %collective-permute-start.6 = (f32[28,2,132]{2,1,0:T(2,128)}, f32[28,2,132]{2,1,0:T(2,128)}, u32[]{:S(2)}, u32[]{:S(2)}) collective-permute-start(f32[28,2,132]{2,1,0:T(2,128)} %pad_maximum_fusion.14), channel_id=1, source_target_pairs={{1,0},{2,1},{3,2},{4,3},{5,4},{6,5},{7,6},{9,8},{10,9},{11,10},{12... | collective-permute-start | bytes 88712 | tf_op jit(solution)/shard_map/ppermute | solution.py:142
  106.6 1.6 pad_maximum_fusion.12
  108.2 25.4 %collective-permute-start.2 = (f32[28,2,132]{2,1,0:T(2,128)}, f32[28,2,132]{2,1,0:T(2,128)}, u32[]{:S(2)}, u32[]{:S(2)}) collective-permute-start(f32[28,2,132]{2,1,0:T(2,128)} %pad_maximum_fusion.12), channel_id=1, source_target_pairs={{0,1},{1,2},{2,3},{3,4},{4,5},{5,6},{6,7},{8,9},{9,10},{10,11},{11... | collective-permute-start | bytes 88712 | tf_op jit(solution)/shard_map/ppermute | solution.py:141
  139.8 1.5 rev.10
  (293 shorter events, 77.2 us)
Async XLA Ops:
  0.6 28.2 %copy-start.11 = (f32[4,96,128]{2,1,0:T(8,128)S(1)}, f32[4,96,128]{2,1,0:T(8,128)}, u32[]{:S(2)}) copy-start(f32[4,96,128]{2,1,0:T(8,128)} %param.13) | copy-start | bytes 589828
  0.6 28.3 %copy-start.12 = (f32[4,96,128]{2,1,0:T(8,128)S(1)}, f32[4,96,128]{2,1,0:T(8,128)}, u32[]{:S(2)}) copy-start(f32[4,96,128]{2,1,0:T(8,128)} %param.14) | copy-start | bytes 589828
  15.2 124.6 %collective-permute-start.4 = (f32[28,2,128]{2,1,0:T(2,128)}, f32[28,2,128]{2,1,0:T(2,128)}, u32[]{:S(2)}, u32[]{:S(2)}) collective-permute-start(f32[28,2,128]{2,1,0:T(2,128)} %get-tuple-element.95), channel_id=1, source_target_pairs={{7,511},{15,503},{23,495},{31,487},{39,479},{47,471},{55,463},{63,... | collective-permute-start | bytes 86024 | tf_op jit(solution)/shard_map/ppermute | solution.py:124
  18.0 53.0 %collective-permute-start.3 = (f32[28,2,2]{2,1,0:T(2,128)}, f32[28,2,2]{2,1,0:T(2,128)}, u32[]{:S(2)}, u32[]{:S(2)}) collective-permute-start(f32[28,2,2]{2,1,0:T(2,128)} %get-tuple-element.167), channel_id=1, source_target_pairs={{7,7},{15,511},{23,503},{31,495},{39,487},{47,479},{55,471},{63,46... | collective-permute-start | bytes 1352 | tf_op jit(solution)/shard_map/ppermute | solution.py:125
  19.2 53.2 %collective-permute-start.5 = (f32[28,2,2]{2,1,0:T(2,128)}, f32[28,2,2]{2,1,0:T(2,128)}, u32[]{:S(2)}, u32[]{:S(2)}) collective-permute-start(f32[28,2,2]{2,1,0:T(2,128)} %get-tuple-element.168), channel_id=1, source_target_pairs={{7,503},{15,495},{23,487},{31,479},{39,471},{47,463},{55,455},{63,... | collective-permute-start | bytes 1352 | tf_op jit(solution)/shard_map/ppermute | solution.py:128
  29.9 29.3 %copy-start.21 = (s32[96,128]{1,0:T(8,128)S(1)}, s32[96,128]{1,0:T(8,128)}, u32[]{:S(2)}) copy-start(s32[96,128]{1,0:T(8,128)} %param.18) | copy-start | bytes 147460
  29.9 29.3 %copy-start.19 = (f32[96,128]{1,0:T(8,128)S(1)}, f32[96,128]{1,0:T(8,128)}, u32[]{:S(2)}) copy-start(f32[96,128]{1,0:T(8,128)} %param.21) | copy-start | bytes 147460
  31.8 28.7 %copy-start.17 = (f32[96,128]{1,0:T(8,128)S(1)}, f32[96,128]{1,0:T(8,128)}, u32[]{:S(2)}) copy-start(f32[96,128]{1,0:T(8,128)} %param.19) | copy-start | bytes 147460
  33.6 28.2 %copy-start.20 = (f32[96,128]{1,0:T(8,128)S(1)}, f32[96,128]{1,0:T(8,128)}, u32[]{:S(2)}) copy-start(f32[96,128]{1,0:T(8,128)} %param.22) | copy-start | bytes 147460
  36.3 37.7 %collective-permute-start = (f32[28,96,2]{1,2,0:T(2,128)S(1)}, f32[28,96,2]{1,2,0:T(2,128)S(1)}, u32[]{:S(2)}, u32[]{:S(2)}) collective-permute-start(f32[28,96,2]{1,2,0:T(2,128)S(1)} %constant_dynamic-update-slice_fusion), channel_id=1, source_target_pairs={{0,8},{8,16},{16,24},{24,32},{32,40},{40,48},{48,56},{56,64},{64,7... | collective-permute-start | bytes 64520 | tf_op jit(solution)/shard_map/ppermute | solution.py:118
  42.6 32.0 %collective-permute-start.1 = (f32[28,96,2]{1,2,0:T(2,128)S(1)}, f32[28,96,2]{1,2,0:T(2,128)S(1)}, u32[]{:S(2)}, u32[]{:S(2)}) collective-permute-start(f32[28,96,2]{1,2,0:T(2,128)S(1)} %constant_dynamic-update-slice_fusion.22), channel_id=1, source_target_pairs={{8,0},{16,8},{24,16},{32,24},{40,32},{48,40},{56,48},{64,56},{72,6... | collective-permute-start | bytes 64520 | tf_op jit(solution)/shard_map/ppermute | solution.py:119
  102.9 32.1 %copy-start.22 = (f32[4,92,128]{2,1,0:T(8,128)S(1)}, f32[4,92,128]{2,1,0:T(8,128)}, u32[]{:S(2)}) copy-start(f32[4,92,128]{2,1,0:T(8,128)} %get-tuple-element.55) | copy-start | bytes 565252
  102.9 32.1 %copy-start.23 = (f32[4,92,128]{2,1,0:T(8,128)S(1)}, f32[4,92,128]{2,1,0:T(8,128)}, u32[]{:S(2)}) copy-start(f32[4,92,128]{2,1,0:T(8,128)} %get-tuple-element.56) | copy-start | bytes 565252
  102.9 32.1 %copy-start.24 = (f32[4,92,128]{2,1,0:T(8,128)S(1)}, f32[4,92,128]{2,1,0:T(8,128)}, u32[]{:S(2)}) copy-start(f32[4,92,128]{2,1,0:T(8,128)} %get-tuple-element.57) | copy-start | bytes 565252
  102.9 32.1 %copy-start.25 = (f32[4,92,128]{2,1,0:T(8,128)S(1)}, f32[4,92,128]{2,1,0:T(8,128)}, u32[]{:S(2)}) copy-start(f32[4,92,128]{2,1,0:T(8,128)} %get-tuple-element.59) | copy-start | bytes 565252
  102.9 32.1 %copy-start.26 = (f32[4,92,128]{2,1,0:T(8,128)S(1)}, f32[4,92,128]{2,1,0:T(8,128)}, u32[]{:S(2)}) copy-start(f32[4,92,128]{2,1,0:T(8,128)} %get-tuple-element.68) | copy-start | bytes 565252
  102.9 32.1 %copy-start.27 = (f32[4,92,128]{2,1,0:T(8,128)S(1)}, f32[4,92,128]{2,1,0:T(8,128)}, u32[]{:S(2)}) copy-start(f32[4,92,128]{2,1,0:T(8,128)} %get-tuple-element.69) | copy-start | bytes 565252
  102.9 32.1 %copy-start.31 = (f32[92,128]{1,0:T(8,128)S(1)}, f32[92,128]{1,0:T(8,128)}, u32[]{:S(2)}) copy-start(f32[92,128]{1,0:T(8,128)} %get-tuple-element.135) | copy-start | bytes 141316
  102.9 32.1 %copy-start.32 = (f32[92,128]{1,0:T(8,128)S(1)}, f32[92,128]{1,0:T(8,128)}, u32[]{:S(2)}) copy-start(f32[92,128]{1,0:T(8,128)} %get-tuple-element.137) | copy-start | bytes 141316
  102.9 32.1 %copy-start.38 = (f32[92,128]{1,0:T(8,128)S(1)}, f32[92,128]{1,0:T(8,128)}, u32[]{:S(2)}) copy-start(f32[92,128]{1,0:T(8,128)} %get-tuple-element.136) | copy-start | bytes 141316
  102.9 32.1 %copy-start.39 = (f32[92,128]{1,0:T(8,128)S(1)}, f32[92,128]{1,0:T(8,128)}, u32[]{:S(2)}) copy-start(f32[92,128]{1,0:T(8,128)} %get-tuple-element.138) | copy-start | bytes 141316
  102.9 32.1 %copy-start.40 = (f32[92,128]{1,0:T(8,128)S(1)}, f32[92,128]{1,0:T(8,128)}, u32[]{:S(2)}) copy-start(f32[92,128]{1,0:T(8,128)} %get-tuple-element.186) | copy-start | bytes 141316
  104.6 37.7 %collective-permute-start.6 = (f32[28,2,132]{2,1,0:T(2,128)}, f32[28,2,132]{2,1,0:T(2,128)}, u32[]{:S(2)}, u32[]{:S(2)}) collective-permute-start(f32[28,2,132]{2,1,0:T(2,128)} %pad_maximum_fusion.14), channel_id=1, source_target_pairs={{1,0},{2,1},{3,2},{4,3},{5,4},{6,5},{7,6},{9,8},{10,9},{11,10},{12... | collective-permute-start | bytes 88712 | tf_op jit(solution)/shard_map/ppermute | solution.py:142
  108.2 36.0 %collective-permute-start.2 = (f32[28,2,132]{2,1,0:T(2,128)}, f32[28,2,132]{2,1,0:T(2,128)}, u32[]{:S(2)}, u32[]{:S(2)}) collective-permute-start(f32[28,2,132]{2,1,0:T(2,128)} %pad_maximum_fusion.12), channel_id=1, source_target_pairs={{0,1},{1,2},{2,3},{3,4},{4,5},{5,6},{6,7},{8,9},{9,10},{10,11},{11... | collective-permute-start | bytes 88712 | tf_op jit(solution)/shard_map/ppermute | solution.py:141
  (42 other events, 116.0 us)

commit v7 on v5

--- a/solution.py
+++ b/solution.py
@@ -12,7 +12,10 @@
 
 def pressure(temp_part, salt_part, layer_height):
     layer_mass = (CONTRACTION * salt_part - EXPANSION * temp_part) * layer_height[:, None, None]
-    return jnp.cumsum(layer_mass, axis=0) - 0.5 * layer_mass
+    running = [layer_mass[0]]
+    for level in range(1, layer_mass.shape[0]):
+        running.append(running[-1] + layer_mass[level])
+    return jnp.stack(running) - 0.5 * layer_mass
 
 
 def mix_vertically(fields, water_share, diapycnal_diffusivity, layer_height):
@@ -37,6 +40,7 @@
     horizontal_eddy_coefficient,
     diapycnal_diffusivity,
     layer_height,
+    pressures,
 ):
     water_share = central[4]
     fields = central[:4]
@@ -56,10 +60,7 @@
         zonal * (eastern[:4] - western[:4]) * (0.5 / zonal_spacing)
         + merid * (northern[:4] - southern[:4]) * (0.5 / meridional_spacing)
     )
-    pressure_east = pressure(eastern[0], eastern[1], layer_height)
-    pressure_west = pressure(western[0], western[1], layer_height)
-    pressure_north = pressure(northern[0], northern[1], layer_height)
-    pressure_south = pressure(southern[0], southern[1], layer_height)
+    pressure_east, pressure_west, pressure_north, pressure_south = pressures
     gradient_x = -(pressure_east - pressure_west) * (0.5 / zonal_spacing)
     gradient_y = -(pressure_north - pressure_south) * (0.5 / meridional_spacing)
     mixing = mix_vertically(fields, water_share, diapycnal_diffusivity, layer_height)
@@ -86,6 +87,13 @@
     at_bottom = (
         lax.broadcasted_iota(jnp.int32, (levels, 1, 1), 0).astype(jnp.float32) == floor_index[None]
     ).astype(jnp.float32)
+    column = pressure(state[0], state[1], layer_height)
+    pressures = (
+        column[:, 1:-1, 2:],
+        column[:, 1:-1, :-2],
+        column[:, 2:, 1:-1],
+        column[:, :-2, 1:-1],
+    )
     return advance(
         state[:, :, 1:-1, 1:-1],
         state[:, :, 1:-1, 2:],
@@ -99,6 +107,7 @@
         params[4],
         params[5:8],
         layer_height,
+        pressures,
     )
 
 

time: 84.3 us -> 121 us (1.44)
  the two profiles are of different devices: /device:TPU:169 before, /device:TPU:192 now
where the time goes in v7:
time: 121 us; the launch traced here: 119 us
  starting transfers between devices  50 us (41%)
  local copies, waits for them, and re-layouts  37.9 us (31%)
  other arithmetic  29.5 us (24%)
  between operations  1.23 us (1%)
    ppermute x1, starting transfers between devices, exchange(): south = lax.ppermute(top_band, 'lat', north_pairs)  25.4 us
    unnamed x68, local copies, waits for them, and re-layouts  20.3 us
    ppermute x1, starting transfers between devices, exchange(): east = lax.ppermute(take(every, slice(0, h)), 'lon', west_pairs)  16.7 us
    unnamed x22, other arithmetic  8.92 us
    slice x4, local copies, waits for them, and re-layouts, take(): parts += [s[None, rs, cs].astype(jnp.float32) for s in surfaces]  6.29 us
    add x2, other arithmetic, advance(): tendency = advection + diffusion + mixing  4.06 us
    mul x4, other arithmetic, mix_vertically(): diapycnal_diffusivity * (water_share[1:] * water_share[:-1]) * contrast  2.57 us
    concatenate x1, other arithmetic, shards(): padded = jnp.concatenate([south, middle, north], axis=1)  2.57 us
  transfers between devices with their start and end apart: 7, of which 0 were waited for; matrix products, arithmetic and copies ran while one was open for 35% of the time, Pallas kernels for 0%

profile of v7, /device:TPU:192, one launch (start us, length us, event | category | flops | bytes accessed | tf_op | source)
XLA Modules:
  0.0 118.7 jit_solution(18288397941330561539)
XLA Ops:
  8.9 1.3 %collective-permute-start.4 = (f32[28,2,128]{2,1,0:T(2,128)S(1)}, f32[28,2,128]{2,1,0:T(2,128)}, u32[]{:S(2)}, u32[]{:S(2)}) collective-permute-start(f32[28,2,128]{2,1,0:T(2,128)S(1)} %get-tuple-element.64), channel_id=1, source_target_pairs={{7,511},{15,503},{23,495},{31,487},{39,479},{47,471},{55,463},{63,... | collective-permute-start | bytes 86024 | tf_op jit(solution)/shard_map/ppermute | solution.py:133
  10.9 1.3 %collective-permute-start.3 = (f32[28,2,2]{2,1,0:T(2,128)}, f32[28,2,2]{2,1,0:T(2,128)}, u32[]{:S(2)}, u32[]{:S(2)}) collective-permute-start(f32[28,2,2]{2,1,0:T(2,128)} %get-tuple-element.98), channel_id=1, source_target_pairs={{7,7},{15,511},{23,503},{31,495},{39,487},{47,479},{55,471},{63,46... | collective-permute-start | bytes 1352 | tf_op jit(solution)/shard_map/ppermute | solution.py:134
  12.2 1.3 %collective-permute-start.5 = (f32[28,2,2]{2,1,0:T(2,128)}, f32[28,2,2]{2,1,0:T(2,128)}, u32[]{:S(2)}, u32[]{:S(2)}) collective-permute-start(f32[28,2,2]{2,1,0:T(2,128)} %get-tuple-element.99), channel_id=1, source_target_pairs={{7,503},{15,495},{23,487},{31,479},{39,471},{47,463},{55,455},{63,... | collective-permute-start | bytes 1352 | tf_op jit(solution)/shard_map/ppermute | solution.py:137
  13.4 1.6 %slice_convert_fusion.1 = (f32[96,2]{1,0:T(8,128)}, f32[96,2]{1,0:T(8,128)S(1)}) fusion(s32[96,128]{1,0:T(8,128)} %param.18), kind=kLoop, calls=%fused_computation.170 | loop fusion | flops 384 | bytes 3072 | tf_op jit(solution)/shard_map/convert_element_type | solution.py:183
  15.0 1.6 %fusion.59 = (f32[96,2]{1,0:T(8,128)}, f32[96,2]{1,0:T(8,128)S(1)}) fusion(f32[96,128]{1,0:T(8,128)} %param.19), kind=kLoop, calls=%fused_computation.186 | loop fusion | bytes 3072 | tf_op jit(solution)/shard_map/slice | solution.py:183
  16.6 1.6 %fusion.58 = (f32[96,2]{1,0:T(8,128)}, f32[96,2]{1,0:T(8,128)S(1)}) fusion(f32[96,128]{1,0:T(8,128)} %param.20), kind=kLoop, calls=%fused_computation.185 | loop fusion | bytes 3072 | tf_op jit(solution)/shard_map/slice | solution.py:183
  18.2 1.6 %fusion.57 = (f32[96,2]{1,0:T(8,128)}, f32[96,2]{1,0:T(8,128)}) fusion(f32[96,128]{1,0:T(8,128)} %param.21), kind=kLoop, calls=%fused_computation.184 | loop fusion | bytes 3072 | tf_op jit(solution)/shard_map/slice | solution.py:183
  19.7 1.6 %fusion.56 = (f32[96,2]{1,0:T(8,128)}, f32[96,2]{1,0:T(8,128)}) fusion(f32[96,128]{1,0:T(8,128)} %param.22), kind=kLoop, calls=%fused_computation.183 | loop fusion | bytes 3072 | tf_op jit(solution)/shard_map/slice | solution.py:183
  21.3 1.1 fusion.54
  23.5 1.5 %copy.67 = f32[96,2]{0,1:T(2,128)} copy(f32[96,2]{1,0:T(8,128)} %get-tuple-element.92) | data formatting | bytes 1536
  24.9 1.4 %copy.51 = f32[96,2]{0,1:T(2,128)} copy(f32[96,2]{1,0:T(8,128)} %get-tuple-element.90) | data formatting | bytes 1536
  26.4 1.4 %copy.52 = f32[96,2]{0,1:T(2,128)} copy(f32[96,2]{1,0:T(8,128)} %get-tuple-element.88) | data formatting | bytes 1536
  27.8 1.4 %copy.53 = f32[96,2]{0,1:T(2,128)} copy(f32[96,2]{1,0:T(8,128)} %get-tuple-element.86) | data formatting | bytes 1536
  29.2 1.4 %copy.54 = f32[96,2]{0,1:T(2,128)} copy(f32[96,2]{1,0:T(8,128)} %get-tuple-element.84) | data formatting | bytes 1536
  36.1 1.9 %collective-permute-start = (f32[28,96,2]{1,2,0:T(2,128)S(1)}, f32[28,96,2]{1,2,0:T(2,128)S(1)}, u32[]{:S(2)}, u32[]{:S(2)}) collective-permute-start(f32[28,96,2]{1,2,0:T(2,128)S(1)} %constant_dynamic-update-slice_fusion), channel_id=1, source_target_pairs={{0,8},{8,16},{16,24},{24,32},{32,40},{40,48},{48,56},{56,64},{64,7... | collective-permute-start | bytes 64520 | tf_op jit(solution)/shard_map/ppermute | solution.py:127
  40.8 16.7 %collective-permute-start.1 = (f32[28,96,2]{1,2,0:T(2,128)S(1)}, f32[28,96,2]{1,2,0:T(2,128)S(1)}, u32[]{:S(2)}, u32[]{:S(2)}) collective-permute-start(f32[28,96,2]{1,2,0:T(2,128)S(1)} %constant_dynamic-update-slice_fusion.22), channel_id=1, source_target_pairs={{8,0},{16,8},{24,16},{32,24},{40,32},{48,40},{56,48},{64,56},{72,6... | collective-permute-start | bytes 64520 | tf_op jit(solution)/shard_map/ppermute | solution.py:128
  69.5 2.1 %collective-permute-start.6 = (f32[28,2,132]{2,1,0:T(2,128)}, f32[28,2,132]{2,1,0:T(2,128)}, u32[]{:S(2)}, u32[]{:S(2)}) collective-permute-start(f32[28,2,132]{2,1,0:T(2,128)} %pad_maximum_fusion.5), channel_id=1, source_target_pairs={{1,0},{2,1},{3,2},{4,3},{5,4},{6,5},{7,6},{9,8},{10,9},{11,10},{12... | collective-permute-start | bytes 88712 | tf_op jit(solution)/shard_map/ppermute | solution.py:151
  72.4 25.4 %collective-permute-start.2 = (f32[28,2,132]{2,1,0:T(2,128)}, f32[28,2,132]{2,1,0:T(2,128)S(1)}, u32[]{:S(2)}, u32[]{:S(2)}) collective-permute-start(f32[28,2,132]{2,1,0:T(2,128)} %pad_maximum_fusion.3), channel_id=1, source_target_pairs={{0,1},{1,2},{2,3},{3,4},{4,5},{5,6},{6,7},{8,9},{9,10},{10,11},{11... | collective-permute-start | bytes 88712 | tf_op jit(solution)/shard_map/ppermute | solution.py:150
  100.9 2.6 %pad_maximum_fusion = f32[28,100,132]{2,1,0:T(8,128)S(1)} fusion(f32[28,2,132]{2,1,0:T(2,128)S(1)} %fusion.48, f32[28,96,2]{2,1,0:T(8,128)S(1)} %copy.42, f32[28,96,128]{2,1,0:T(8,128)} %constant_dynamic-update-slice_fusion.33, f32[28,96,2]{2,1,0:T(8,128)S(1)} %copy.41, f32[28,2,132]{2,1,0:T(2,128)S(1)} %collective-permute-done.2), kind=kLoop, calls=%fused_computation | loop fusion | flops 1478400 | bytes 2956800 | tf_op jit(solution)/shard_map/concatenate | solution.py:196
  104.5 1.4 %fusion.22 = f32[4,100,132]{2,1,0:T(8,128)S(1)} fusion(f32[28,2,132]{2,1,0:T(2,128)S(1)} %fusion.48, f32[28,2,132]{2,1,0:T(2,128)S(1)} %collective-permute-done.2, f32[28,96,2]{2,1,0:T(8,128)S(1)} %copy.42, f32[28,96,128]{2,1,0:T(8,128)} %constant_dynamic-update-slice_fusion.33, f32[28,96,2]{2,1,0:T(8,128)S(1)} %copy.41, f32[4]{0:T(128)S(1)} %copy-done.11), kind=kLoop, calls=%fused_computation.39 | loop fusion | flops 633600 | bytes 1689616 | tf_op jit(solution)/shard_map/mul | solution.py:14
  106.0 1.3 %fusion.29 = f32[3,98,130]{2,1,0:T(8,128)S(1)} fusion(f32[5,4,100,132]{3,2,1,0:T(8,128)S(1)} %bitcast.165, f32[28,2,132]{2,1,0:T(2,128)S(1)} %fusion.48, f32[28,2,132]{2,1,0:T(2,128)S(1)} %collective-permute-done.2, f32[28,96,2]{2,1,0:T(8,128)S(1)} %copy.42, f32[28,96,128]{2,1,0:T(8,128)} %constant_dynamic-update-slice_fusion.33, f32[28,96,2]{2,1,0:T(8,128)S(1)} %copy.41), kind=kLoop, calls=%fused_computation.57 | loop fusion | flops 229320 | bytes 1937040 | tf_op jit(solution)/shard_map/mul | solution.py:23
  109.1 1.1 maximum_bitcast_fusion.1
  110.2 2.8 %divide_add_fusion = f32[4,4,98,130]{3,2,1,0:T(8,128)S(1)} fusion(f32[4,3,98,130]{3,2,1,0:T(8,128)S(1)} %fusion.3, f32[5,4,100,132]{3,2,1,0:T(8,128)S(1)} %bitcast.167, f32[4]{0:T(128)S(1)} %mul.560, f32[98,130]{1,0:T(8,128)S(1)} %get-tuple-element.100, f32[4,98,130]{2,1,0:T(8,128)S(1)} %get-tuple-element.29, f32[4,98,130]{2,1,0:T(8,128)S(1)} %get-tuple-element.30, ...), kind=kLoop, calls=%fused_computation.7 | loop fusion | flops 5299840 | bytes 6981536 | tf_op jit(solution)/shard_map/add | solution.py:67
  115.6 1.3 %divide_add_fusion.1 = f32[4,4,96,128]{3,2,1,0:T(8,128)S(1)} fusion(f32[4,3,96,128]{3,2,1,0:T(8,128)S(1)} %fusion.6, f32[5,4,98,130]{3,2,1,0:T(8,128)S(1)} %fusion, f32[4,4,98,130]{3,2,1,0:T(8,128)S(1)} %fusion.2, f32[4]{0:T(128)S(1)} %mul.560, f32[96,128]{1,0:T(8,128)S(1)} %get-tuple-element.71, f32[4,96,128]{2,1,0:T(8,128)S(1)} %get-tuple-element.26, ...), kind=kLoop, calls=%fused_computation.13 | loop fusion | flops 5111808 | bytes 6733840 | tf_op jit(solution)/shard_map/add | solution.py:67
  (148 shorter events, 40.8 us)
Async XLA Ops:
  0.6 21.8 %copy-start.2 = (f32[4,96,128]{2,1,0:T(8,128)S(1)}, f32[4,96,128]{2,1,0:T(8,128)}, u32[]{:S(2)}) copy-start(f32[4,96,128]{2,1,0:T(8,128)} %param.13) | copy-start | bytes 589828
  0.6 21.9 %copy-start.3 = (f32[4,96,128]{2,1,0:T(8,128)S(1)}, f32[4,96,128]{2,1,0:T(8,128)}, u32[]{:S(2)}) copy-start(f32[4,96,128]{2,1,0:T(8,128)} %param.14) | copy-start | bytes 589828
  2.3 20.4 %copy-start.4 = (f32[4,96,128]{2,1,0:T(8,128)S(1)}, f32[4,96,128]{2,1,0:T(8,128)}, u32[]{:S(2)}) copy-start(f32[4,96,128]{2,1,0:T(8,128)} %param.15) | copy-start | bytes 589828
  8.9 89.9 %collective-permute-start.4 = (f32[28,2,128]{2,1,0:T(2,128)S(1)}, f32[28,2,128]{2,1,0:T(2,128)}, u32[]{:S(2)}, u32[]{:S(2)}) collective-permute-start(f32[28,2,128]{2,1,0:T(2,128)S(1)} %get-tuple-element.64), channel_id=1, source_target_pairs={{7,511},{15,503},{23,495},{31,487},{39,479},{47,471},{55,463},{63,... | collective-permute-start | bytes 86024 | tf_op jit(solution)/shard_map/ppermute | solution.py:133
  10.9 54.7 %collective-permute-start.3 = (f32[28,2,2]{2,1,0:T(2,128)}, f32[28,2,2]{2,1,0:T(2,128)}, u32[]{:S(2)}, u32[]{:S(2)}) collective-permute-start(f32[28,2,2]{2,1,0:T(2,128)} %get-tuple-element.98), channel_id=1, source_target_pairs={{7,7},{15,511},{23,503},{31,495},{39,487},{47,479},{55,471},{63,46... | collective-permute-start | bytes 1352 | tf_op jit(solution)/shard_map/ppermute | solution.py:134
  12.2 54.3 %collective-permute-start.5 = (f32[28,2,2]{2,1,0:T(2,128)}, f32[28,2,2]{2,1,0:T(2,128)}, u32[]{:S(2)}, u32[]{:S(2)}) collective-permute-start(f32[28,2,2]{2,1,0:T(2,128)} %get-tuple-element.99), channel_id=1, source_target_pairs={{7,503},{15,495},{23,487},{31,479},{39,471},{47,463},{55,455},{63,... | collective-permute-start | bytes 1352 | tf_op jit(solution)/shard_map/ppermute | solution.py:137
  18.2 4.6 %copy-start.5 = (f32[4,96,128]{2,1,0:T(8,128)S(1)}, f32[4,96,128]{2,1,0:T(8,128)}, u32[]{:S(2)}) copy-start(f32[4,96,128]{2,1,0:T(8,128)} %param.16) | copy-start | bytes 589828
  22.4 0.9 copy-start
  23.3 34.2 %copy-start.7 = (f32[96,128]{1,0:T(8,128)S(1)}, f32[96,128]{1,0:T(8,128)}, u32[]{:S(2)}) copy-start(f32[96,128]{1,0:T(8,128)} %param.19) | copy-start | bytes 147460
  23.4 34.2 %copy-start.8 = (f32[96,128]{1,0:T(8,128)S(1)}, f32[96,128]{1,0:T(8,128)}, u32[]{:S(2)}) copy-start(f32[96,128]{1,0:T(8,128)} %param.20) | copy-start | bytes 147460
  36.1 32.0 %collective-permute-start = (f32[28,96,2]{1,2,0:T(2,128)S(1)}, f32[28,96,2]{1,2,0:T(2,128)S(1)}, u32[]{:S(2)}, u32[]{:S(2)}) collective-permute-start(f32[28,96,2]{1,2,0:T(2,128)S(1)} %constant_dynamic-update-slice_fusion), channel_id=1, source_target_pairs={{0,8},{8,16},{16,24},{24,32},{32,40},{40,48},{48,56},{56,64},{64,7... | collective-permute-start | bytes 64520 | tf_op jit(solution)/shard_map/ppermute | solution.py:127
  40.5 20.6 %copy-start.9 = (s32[96,128]{1,0:T(8,128)S(1)}, s32[96,128]{1,0:T(8,128)}, u32[]{:S(2)}) copy-start(s32[96,128]{1,0:T(8,128)} %param.18) | copy-start | bytes 147460
  40.6 22.3 %copy-start.10 = (f32[96,128]{1,0:T(8,128)S(1)}, f32[96,128]{1,0:T(8,128)}, u32[]{:S(2)}) copy-start(f32[96,128]{1,0:T(8,128)} %param.21) | copy-start | bytes 147460
  40.8 22.8 %copy-start.6 = (f32[96,128]{1,0:T(8,128)S(1)}, f32[96,128]{1,0:T(8,128)}, u32[]{:S(2)}) copy-start(f32[96,128]{1,0:T(8,128)} %param.22) | copy-start | bytes 147460
  40.8 23.4 %copy-start.1 = (f32[3,96,128]{2,1,0:T(8,128)S(1)}, f32[3,96,128]{2,1,0:T(8,128)}, u32[]{:S(2)}) copy-start(f32[3,96,128]{2,1,0:T(8,128)} %param.23) | copy-start | bytes 442372
  40.8 26.6 %collective-permute-start.1 = (f32[28,96,2]{1,2,0:T(2,128)S(1)}, f32[28,96,2]{1,2,0:T(2,128)S(1)}, u32[]{:S(2)}, u32[]{:S(2)}) collective-permute-start(f32[28,96,2]{1,2,0:T(2,128)S(1)} %constant_dynamic-update-slice_fusion.22), channel_id=1, source_target_pairs={{8,0},{16,8},{24,16},{32,24},{40,32},{48,40},{56,48},{64,56},{72,6... | collective-permute-start | bytes 64520 | tf_op jit(solution)/shard_map/ppermute | solution.py:128
  57.6 7.3 %copy-start.11 = (f32[4]{0:T(128)S(1)}, f32[4]{0:T(128)}, u32[]{:S(2)}) copy-start(f32[4]{0:T(128)} %param.24) | copy-start | bytes 52
  57.6 7.3 %copy-start.13 = (f32[5]{0:T(128)S(1)}, f32[5]{0:T(128)}, u32[]{:S(2)}) copy-start(f32[5]{0:T(128)} %constant.6.clone) | copy-start | bytes 64
  69.5 30.5 %copy-start.12 = (f32[28]{0:T(128)S(1)}, f32[28]{0:T(128)}, u32[]{:S(2)}) copy-start(f32[28]{0:T(128)} %concatenate.63) | copy-start | bytes 340
  69.5 30.4 %collective-permute-start.6 = (f32[28,2,132]{2,1,0:T(2,128)}, f32[28,2,132]{2,1,0:T(2,128)}, u32[]{:S(2)}, u32[]{:S(2)}) collective-permute-start(f32[28,2,132]{2,1,0:T(2,128)} %pad_maximum_fusion.5), channel_id=1, source_target_pairs={{1,0},{2,1},{3,2},{4,3},{5,4},{6,5},{7,6},{9,8},{10,9},{11,10},{12... | collective-permute-start | bytes 88712 | tf_op jit(solution)/shard_map/ppermute | solution.py:151
  72.4 28.5 %collective-permute-start.2 = (f32[28,2,132]{2,1,0:T(2,128)}, f32[28,2,132]{2,1,0:T(2,128)S(1)}, u32[]{:S(2)}, u32[]{:S(2)}) collective-permute-start(f32[28,2,132]{2,1,0:T(2,128)} %pad_maximum_fusion.3), channel_id=1, source_target_pairs={{0,1},{1,2},{2,3},{3,4},{4,5},{5,6},{6,7},{8,9},{9,10},{10,11},{11... | collective-permute-start | bytes 88712 | tf_op jit(solution)/shard_map/ppermute | solution.py:150

commit v8 on v5

--- a/solution.py
+++ b/solution.py
@@ -118,26 +118,20 @@
     west = lax.ppermute(take(every, slice(-h, None)), "lon", east_pairs)
     east = lax.ppermute(take(every, slice(0, h)), "lon", west_pairs)
 
-    axes = ("lon", "lat")
     rows_hi = take(slice(-h, None), every)
     rows_lo = take(slice(0, h), every)
-    mirror = lax.ppermute(rows_hi, axes, fold_pairs(lon_count, lat_count, lambda i: lon_count - 1 - i))
-    mirror_lo = lax.ppermute(
-        rows_hi[:, :, :h], axes, fold_pairs(lon_count, lat_count, lambda i: lon_count - i)
-    )
-    mirror_hi = lax.ppermute(
-        rows_hi[:, :, -h:], axes, fold_pairs(lon_count, lat_count, lambda i: lon_count - 2 - i)
-    )
-    mirrored = jnp.concatenate(
-        [mirror_lo[:, :, ::-1], mirror[:, :, ::-1], mirror_hi[:, :, ::-1]], axis=2
-    )
+    top_band = jnp.concatenate([west[:, -h:, :], rows_hi, east[:, -h:, :]], axis=2)
+    bottom_band = jnp.concatenate([west[:, :h, :], rows_lo, east[:, :h, :]], axis=2)
+
+    mirror = lax.ppermute(
+        top_band, ("lon", "lat"), fold_pairs(lon_count, lat_count, lambda i: lon_count - 1 - i)
+    )
+    mirrored = mirror[:, :, ::-1]
     folded = jnp.concatenate([mirrored[:, 1:2, :], mirrored[:, 0:1, :]], axis=1)
     folded = folded * sign[:, None, None]
 
     north_pairs = [(j, j + 1) for j in range(lat_count - 1)]
     south_pairs = [(j, i) for i, j in north_pairs]
-    top_band = jnp.concatenate([west[:, -h:, :], rows_hi, east[:, -h:, :]], axis=2)
-    bottom_band = jnp.concatenate([west[:, :h, :], rows_lo, east[:, :h, :]], axis=2)
     south = lax.ppermute(top_band, "lat", north_pairs)
     north = lax.ppermute(bottom_band, "lat", south_pairs)
     is_top = lax.axis_index("lat") == lat_count - 1

time: 84.3 us -> 74.1 us (0.88)
  the two profiles are of different devices: /device:TPU:169 before, /device:TPU:192 now
where the time goes in v8:
time: 74.1 us; the launch traced here: 73.7 us
  starting transfers between devices  34.3 us (46%)
  other arithmetic  22.7 us (31%)
  local copies, waits for them, and re-layouts  13.1 us (18%)
  waiting for transfers between devices  2.34 us (3%)
  between operations  1.27 us (2%)
    ppermute x1, starting transfers between devices, exchange(): east = lax.ppermute(take(every, slice(0, h)), 'lon', west_pairs)  16.6 us
    ppermute x1, starting transfers between devices, exchange(): south = lax.ppermute(top_band, 'lat', north_pairs)  13.2 us
    unnamed x70, local copies, waits for them, and re-layouts  5.52 us
    unnamed x22, other arithmetic  4.3 us
    add x2, other arithmetic, advance(): tendency = advection + diffusion + mixing  4.23 us
    another operation x8, other arithmetic, pressure(): return jnp.cumsum(layer_mass, axis=0) - 0.5 * layer_mass  3.4 us
    mul x4, other arithmetic, mix_vertically(): diapycnal_diffusivity * (water_share[1:] * water_share[:-1]) * contrast  2.58 us
    concatenate x1, other arithmetic, shards(): padded = jnp.concatenate([south, middle, north], axis=1)  2.57 us
  transfers between devices with their start and end apart: 5, of which 1 were waited for; matrix products, arithmetic and copies ran while one was open for 17% of the time, Pallas kernels for 0%

profile of v8, /device:TPU:192, one launch (start us, length us, event | category | flops | bytes accessed | tf_op | source)
XLA Modules:
  0.0 73.7 jit_solution(1872258191674221688)
XLA Ops:
  0.7 1.2 %fusion.107 = (s32[4,96,2]{2,1,0:T(8,128)S(1)}, s32[4,96,2]{2,1,0:T(8,128)S(1)}) fusion(s32[4,96,128]{2,1,0:T(8,128)} %param.17), kind=kLoop, calls=%fused_computation.233 | loop fusion | bytes 12288 | tf_op jit(solution)/shard_map/slice | solution.py:166
  1.9 1.1 %fusion.108 = (f32[4,96,2]{2,1,0:T(8,128)S(1)}, f32[4,96,2]{2,1,0:T(8,128)S(1)}) fusion(f32[4,96,128]{2,1,0:T(8,128)} %param.13), kind=kLoop, calls=%fused_computation.234 | loop fusion | bytes 12288 | tf_op jit(solution)/shard_map/slice | solution.py:167
  5.2 1.9 %collective-permute-start = (f32[28,96,2]{1,2,0:T(2,128)S(1)}, f32[28,96,2]{1,2,0:T(2,128)S(1)}, u32[]{:S(2)}, u32[]{:S(2)}) collective-permute-start(f32[28,96,2]{1,2,0:T(2,128)S(1)} %constant_dynamic-update-slice_fusion), channel_id=1, source_target_pairs={{0,8},{8,16},{16,24},{24,32},{32,40},{40,48},{48,56},{56,64},{64,7... | collective-permute-start | bytes 64520 | tf_op jit(solution)/shard_map/ppermute | solution.py:118
  8.3 16.6 %collective-permute-start.1 = (f32[28,96,2]{1,2,0:T(2,128)S(1)}, f32[28,96,2]{1,2,0:T(2,128)S(1)}, u32[]{:S(2)}, u32[]{:S(2)}) collective-permute-start(f32[28,96,2]{1,2,0:T(2,128)S(1)} %constant_dynamic-update-slice_fusion.22), channel_id=1, source_target_pairs={{8,0},{16,8},{24,16},{32,24},{40,32},{48,40},{56,48},{64,56},{72,6... | collective-permute-start | bytes 64520 | tf_op jit(solution)/shard_map/ppermute | solution.py:119
  24.9 0.7 multiply_dynamic-update-slice_fusion.3
  25.6 0.7 multiply_dynamic-update-slice_fusion.2
  26.3 0.7 multiply_dynamic-update-slice_fusion.1
  27.0 0.7 multiply_dynamic-update-slice_fusion
  27.7 0.7 convert_dynamic-update-slice_fusion
  34.2 13.2 %collective-permute-start.2 = (f32[28,2,132]{2,1,0:T(2,128)S(1)}, f32[28,2,132]{2,1,0:T(2,128)S(1)}, u32[]{:S(2)}, u32[]{:S(2)}) collective-permute-start(f32[28,2,132]{2,1,0:T(2,128)S(1)} %pad_maximum_fusion.3), channel_id=1, source_target_pairs={{0,1},{1,2},{2,3},{3,4},{4,5},{5,6},{6,7},{8,9},{9,10},{10,11},{11... | collective-permute-start | bytes 88712 | tf_op jit(solution)/shard_map/ppermute | solution.py:135
  48.1 1.9 %collective-permute-start.4 = (f32[28,2,132]{2,1,0:T(2,128)S(1)}, f32[28,2,132]{2,1,0:T(2,128)}, u32[]{:S(2)}, u32[]{:S(2)}) collective-permute-start(f32[28,2,132]{2,1,0:T(2,128)S(1)} %pad_maximum_fusion.4), channel_id=1, source_target_pairs={{1,0},{2,1},{3,2},{4,3},{5,4},{6,5},{7,6},{9,8},{10,9},{11,10},{12... | collective-permute-start | bytes 88712 | tf_op jit(solution)/shard_map/ppermute | solution.py:136
  52.0 2.3 %collective-permute-done.4 = f32[28,2,132]{2,1,0:T(2,128)} collective-permute-done((f32[28,2,132]{2,1,0:T(2,128)S(1)}, f32[28,2,132]{2,1,0:T(2,128)}, u32[]{:S(2)}, u32[]{:S(2)}) %collective-permute-start.4) | collective-permute-done | bytes 29600 | tf_op jit(solution)/shard_map/ppermute | solution.py:136
  54.3 0.9 %fusion.87 = f32[28,2,132]{2,1,0:T(2,128)S(1)} fusion(f32[28,2,132]{2,1,0:T(2,128)} %collective-permute-done.4, f32[28,1,132]{2,1,0:T(1,128)S(1)} %slice.911, f32[28,1,132]{2,1,0:T(1,128)S(1)} %slice.912, pred[]{:T(512)S(6)} %eq.50, f32[28]{0:T(128)S(1)} %concatenate.59), kind=kLoop, calls=%fused_computation.205 | loop fusion | flops 22176 | bytes 88817 | tf_op jit(solution)/shard_map/jit(_where)/select_n | solution.py:138
  55.2 2.6 %pad_maximum_fusion = f32[28,100,132]{2,1,0:T(8,128)S(1)} fusion(f32[28,2,132]{2,1,0:T(2,128)S(1)} %fusion.87, f32[28,96,2]{2,1,0:T(8,128)S(1)} %copy.42, f32[28,96,128]{2,1,0:T(8,128)} %constant_dynamic-update-slice_fusion.33, f32[28,96,2]{2,1,0:T(8,128)S(1)} %copy.41, f32[28,2,132]{2,1,0:T(2,128)S(1)} %collective-permute-done.2), kind=kLoop, calls=%fused_computation | loop fusion | flops 1478400 | bytes 2956800 | tf_op jit(solution)/shard_map/concatenate | solution.py:181
  58.0 0.7 slice_bitcast_fusion.9
  59.5 1.3 %fusion.44 = f32[3,98,130]{2,1,0:T(8,128)S(1)} fusion(f32[5,4,100,132]{3,2,1,0:T(8,128)S(1)} %bitcast.115, f32[28,2,132]{2,1,0:T(2,128)S(1)} %fusion.87, f32[28,2,132]{2,1,0:T(2,128)S(1)} %collective-permute-done.2, f32[28,96,2]{2,1,0:T(8,128)S(1)} %copy.42, f32[28,96,128]{2,1,0:T(8,128)} %constant_dynamic-update-slice_fusion.33, f32[28,96,2]{2,1,0:T(8,128)S(1)} %copy.41), kind=kLoop, calls=%fused_computation.76 | loop fusion | flops 229320 | bytes 1937040 | tf_op jit(solution)/shard_map/mul | solution.py:20
  60.9 0.7 fusion.3
  61.6 1.0 %divide_bitcast_fusion.1 = (f32[98,130]{1,0:T(8,128)S(1)}, f32[1,98,130]{2,1,0:T(8,128)S(1)}, f32[98,130]{1,0:T(8,128)S(1)}, f32[1,98,130]{2,1,0:T(8,128)S(1)}) fusion(f32[28,2,132]{2,1,0:T(2,128)S(1)} %fusion.87, f32[28,96,2]{2,1,0:T(8,128)S(1)} %copy.42, f32[28,96,128]{2,1,0:T(8,128)} %constant_dynamic-update-slice_fusion.33, f32[28,96,2]{2,1,0:T(8,128)S(1)} %copy.41, ...), kind=kLoop, calls=%fused_computation.190 | loop fusion | flops 127400 | bytes 1682240 | tf_op jit(solution)/shard_map/div | solution.py:56
  62.6 1.1 %maximum_bitcast_fusion.1 = (f32[98,130]{1,0:T(8,128)S(1)}, f32[98,130]{1,0:T(8,128)S(1)}, f32[98,130]{1,0:T(8,128)S(1)}) fusion(f32[28,2,132]{2,1,0:T(2,128)S(1)} %fusion.87, f32[28,2,132]{2,1,0:T(2,128)S(1)} %collective-permute-done.2, f32[28,96,2]{2,1,0:T(8,128)S(1)} %copy.42, f32[28,96,128]{2,1,0:T(8,128)} %constant_dynamic-update-slice_fusion.33, ...), kind=kLoop, calls=%fused_computation.183 | loop fusion | flops 152880 | bytes 1631280 | tf_op jit(solution)/shard_map/mul | solution.py:69
  63.7 3.0 %divide_add_fusion = f32[4,4,98,130]{3,2,1,0:T(8,128)S(1)} fusion(f32[4,3,98,130]{3,2,1,0:T(8,128)S(1)} %fusion.3, f32[5,4,100,132]{3,2,1,0:T(8,128)S(1)} %bitcast.117, f32[4]{0:T(128)S(1)} %mul.694, f32[98,130]{1,0:T(8,128)S(1)} %get-tuple-element.86, f32[4,98,130]{2,1,0:T(8,128)S(1)} %get-tuple-element.19, f32[4,98,130]{2,1,0:T(8,128)S(1)} %get-tuple-element.20, ...), kind=kLoop, calls=%fused_computation.7 | loop fusion | flops 5299840 | bytes 6981536 | tf_op jit(solution)/shard_map/add | solution.py:66
  66.8 0.8 %fusion.25 = f32[1,4,98,130]{3,2,1,0:T(8,128)S(1)} fusion(f32[1,4,98,130]{3,2,1,0:T(8,128)S(1)} %reduce-window_subtract_fusion.2, f32[4,4,98,130]{3,2,1,0:T(8,128)S(1)} %divide_add_fusion, f32[5,4,100,132]{3,2,1,0:T(8,128)S(1)} %bitcast.118, f32[98,130]{1,0:T(8,128)S(1)} %get-tuple-element.9, f32[98,130]{1,0:T(8,128)S(1)} %get-tuple-element.4, ...), kind=kOutput, calls=%fused_computation.44 | output fusion | flops 1121120 | bytes 3932736 | tf_op jit(solution)/shard_map/jit(cumsum)/reduce_window_sum | solution.py:15
  67.6 0.8 %fusion.26 = f32[1,4,98,130]{3,2,1,0:T(8,128)S(1)} fusion(f32[1,4,98,130]{3,2,1,0:T(8,128)S(1)} %reduce-window_subtract_fusion, f32[4,4,98,130]{3,2,1,0:T(8,128)S(1)} %divide_add_fusion, f32[5,4,100,132]{3,2,1,0:T(8,128)S(1)} %bitcast.119, f32[98,130]{1,0:T(8,128)S(1)} %get-tuple-element.11, f32[98,130]{1,0:T(8,128)S(1)} %get-tuple-element.9, ...), kind=kOutput, calls=%fused_computation.45 | output fusion | flops 1121120 | bytes 3932736 | tf_op jit(solution)/shard_map/jit(cumsum)/reduce_window_sum | solution.py:15
  70.4 1.3 %divide_add_fusion.1 = f32[4,4,96,128]{3,2,1,0:T(8,128)S(1)} fusion(f32[4,3,96,128]{3,2,1,0:T(8,128)S(1)} %fusion.24, f32[5,4,98,130]{3,2,1,0:T(8,128)S(1)} %fusion, f32[4,4,98,130]{3,2,1,0:T(8,128)S(1)} %fusion.2, f32[4]{0:T(128)S(1)} %mul.694, f32[96,128]{1,0:T(8,128)S(1)} %get-tuple-element.59, f32[4,96,128]{2,1,0:T(8,128)S(1)} %get-tuple-element.16, ...), kind=kLoop, calls=%fused_computation.39 | loop fusion | flops 5111808 | bytes 6733840 | tf_op jit(solution)/shard_map/add | solution.py:66
  72.8 0.9 %slice_bitcast_fusion.2 = (f32[4,96,128]{2,1,0:T(8,128)}, f32[4,96,128]{2,1,0:T(8,128)}, f32[4,96,128]{2,1,0:T(8,128)}, f32[4,96,128]{2,1,0:T(8,128)}) fusion(f32[4,4,96,128]{3,2,1,0:T(8,128)S(1)} %fusion.23), kind=kLoop, calls=%fused_computation.91 | loop fusion | bytes 1572864 | tf_op jit(solution)/shard_map/squeeze | solution.py:191
  (141 shorter events, 15.6 us)
Async XLA Ops:
  0.6 2.6 %copy-start.3 = (f32[4,96,128]{2,1,0:T(8,128)S(1)}, f32[4,96,128]{2,1,0:T(8,128)}, u32[]{:S(2)}) copy-start(f32[4,96,128]{2,1,0:T(8,128)} %param.14) | copy-start | bytes 589828
  0.6 2.8 %copy-start.4 = (f32[4,96,128]{2,1,0:T(8,128)S(1)}, f32[4,96,128]{2,1,0:T(8,128)}, u32[]{:S(2)}) copy-start(f32[4,96,128]{2,1,0:T(8,128)} %param.15) | copy-start | bytes 589828
  1.8 1.9 %copy-start.5 = (f32[4,96,128]{2,1,0:T(8,128)S(1)}, f32[4,96,128]{2,1,0:T(8,128)}, u32[]{:S(2)}) copy-start(f32[4,96,128]{2,1,0:T(8,128)} %param.16) | copy-start | bytes 589828
  3.1 0.9 %copy-start.10 = (s32[96,128]{1,0:T(8,128)S(1)}, s32[96,128]{1,0:T(8,128)}, u32[]{:S(2)}) copy-start(s32[96,128]{1,0:T(8,128)} %param.18) | copy-start | bytes 147460
  3.1 1.1 %copy-start.8 = (f32[96,128]{1,0:T(8,128)S(1)}, f32[96,128]{1,0:T(8,128)}, u32[]{:S(2)}) copy-start(f32[96,128]{1,0:T(8,128)} %param.19) | copy-start | bytes 147460
  3.2 1.2 %copy-start.9 = (f32[96,128]{1,0:T(8,128)S(1)}, f32[96,128]{1,0:T(8,128)}, u32[]{:S(2)}) copy-start(f32[96,128]{1,0:T(8,128)} %param.20) | copy-start | bytes 147460
  3.2 1.3 %copy-start.6 = (f32[96,128]{1,0:T(8,128)S(1)}, f32[96,128]{1,0:T(8,128)}, u32[]{:S(2)}) copy-start(f32[96,128]{1,0:T(8,128)} %param.21) | copy-start | bytes 147460
  3.4 1.4 %copy-start.7 = (f32[96,128]{1,0:T(8,128)S(1)}, f32[96,128]{1,0:T(8,128)}, u32[]{:S(2)}) copy-start(f32[96,128]{1,0:T(8,128)} %param.22) | copy-start | bytes 147460
  3.4 1.5 %copy-start.1 = (f32[3,96,128]{2,1,0:T(8,128)S(1)}, f32[3,96,128]{2,1,0:T(8,128)}, u32[]{:S(2)}) copy-start(f32[3,96,128]{2,1,0:T(8,128)} %param.23) | copy-start | bytes 442372
  4.0 20.8 %copy-start = (s32[4,96,128]{2,1,0:T(8,128)S(1)}, s32[4,96,128]{2,1,0:T(8,128)}, u32[]{:S(2)}) copy-start(s32[4,96,128]{2,1,0:T(8,128)} %param.17) | copy-start | bytes 589828
  4.0 20.8 %copy-start.2 = (f32[4,96,128]{2,1,0:T(8,128)S(1)}, f32[4,96,128]{2,1,0:T(8,128)}, u32[]{:S(2)}) copy-start(f32[4,96,128]{2,1,0:T(8,128)} %param.13) | copy-start | bytes 589828
  5.2 27.4 %collective-permute-start = (f32[28,96,2]{1,2,0:T(2,128)S(1)}, f32[28,96,2]{1,2,0:T(2,128)S(1)}, u32[]{:S(2)}, u32[]{:S(2)}) collective-permute-start(f32[28,96,2]{1,2,0:T(2,128)S(1)} %constant_dynamic-update-slice_fusion), channel_id=1, source_target_pairs={{0,8},{8,16},{16,24},{24,32},{32,40},{40,48},{48,56},{56,64},{64,7... | collective-permute-start | bytes 64520 | tf_op jit(solution)/shard_map/ppermute | solution.py:118
  8.3 24.7 %collective-permute-start.1 = (f32[28,96,2]{1,2,0:T(2,128)S(1)}, f32[28,96,2]{1,2,0:T(2,128)S(1)}, u32[]{:S(2)}, u32[]{:S(2)}) collective-permute-start(f32[28,96,2]{1,2,0:T(2,128)S(1)} %constant_dynamic-update-slice_fusion.22), channel_id=1, source_target_pairs={{8,0},{16,8},{24,16},{32,24},{40,32},{48,40},{56,48},{64,56},{72,6... | collective-permute-start | bytes 64520 | tf_op jit(solution)/shard_map/ppermute | solution.py:119
  25.6 6.8 %copy-start.12 = (f32[5]{0:T(128)S(1)}, f32[5]{0:T(128)}, u32[]{:S(2)}) copy-start(f32[5]{0:T(128)} %constant.46.clone) | copy-start | bytes 64
  25.6 6.9 %copy-start.11 = (f32[4]{0:T(128)S(1)}, f32[4]{0:T(128)}, u32[]{:S(2)}) copy-start(f32[4]{0:T(128)} %param.24) | copy-start | bytes 52
  33.5 17.5 %collective-permute-start.3 = (f32[28,2,132]{2,1,0:T(2,128)S(1)}, f32[28,2,132]{2,1,0:T(2,128)S(1)}, u32[]{:S(2)}, u32[]{:S(2)}) collective-permute-start(f32[28,2,132]{2,1,0:T(2,128)S(1)} %pad_maximum_fusion.3), channel_id=1, source_target_pairs={{7,511},{15,503},{23,495},{31,487},{39,479},{47,471},{55,463},{63,... | collective-permute-start | bytes 88712 | tf_op jit(solution)/shard_map/ppermute | solution.py:126
  34.2 21.0 %collective-permute-start.2 = (f32[28,2,132]{2,1,0:T(2,128)S(1)}, f32[28,2,132]{2,1,0:T(2,128)S(1)}, u32[]{:S(2)}, u32[]{:S(2)}) collective-permute-start(f32[28,2,132]{2,1,0:T(2,128)S(1)} %pad_maximum_fusion.3), channel_id=1, source_target_pairs={{0,1},{1,2},{2,3},{3,4},{4,5},{5,6},{6,7},{8,9},{9,10},{10,11},{11... | collective-permute-start | bytes 88712 | tf_op jit(solution)/shard_map/ppermute | solution.py:135
  48.1 6.2 %collective-permute-start.4 = (f32[28,2,132]{2,1,0:T(2,128)S(1)}, f32[28,2,132]{2,1,0:T(2,128)}, u32[]{:S(2)}, u32[]{:S(2)}) collective-permute-start(f32[28,2,132]{2,1,0:T(2,128)S(1)} %pad_maximum_fusion.4), channel_id=1, source_target_pairs={{1,0},{2,1},{3,2},{4,3},{5,4},{6,5},{7,6},{9,8},{10,9},{11,10},{12... | collective-permute-start | bytes 88712 | tf_op jit(solution)/shard_map/ppermute | solution.py:136

commit v9 on v8

--- a/solution.py
+++ b/solution.py
@@ -2,6 +2,8 @@
 import jax.numpy as jnp
 from jax import lax
 from jax.sharding import PartitionSpec as P
+from jax.experimental import pallas as pl
+from jax.experimental.pallas import tpu as pltpu
 
 TIME_STEP = 0.25
 EXPANSION = 0.2
@@ -176,19 +178,148 @@
         [jnp.repeat(channel_sign, levels), jnp.ones((len(surfaces) + levels - 1,), jnp.float32)]
     )
     west, east, south, north = exchange(take, sign)
-    every = slice(None)
-    middle = jnp.concatenate([west, take(every, every), east], axis=2)
-    padded = jnp.concatenate([south, middle, north], axis=1)
-    n_state = channels * levels
-    state0 = padded[:n_state].reshape(channels, levels, rows + 2 * HALO, cols + 2 * HALO)
-    params_outer = padded[n_state:, 1:-1, 1:-1]
-    state1 = step(state0, params_outer, levels, layer_height)
-    is_bottom = lax.axis_index("lat") == 0
-    first_row = jnp.where(is_bottom, 0.0, state1[:, :, :1, :])
-    state1 = jnp.concatenate([first_row, state1[:, :, 1:, :]], axis=2)
-    params_inner = padded[n_state:, HALO:-HALO, HALO:-HALO]
-    state2 = step(state1, params_inner, levels, layer_height)
-    return (state2[0], state2[1], state2[2], state2[3])
+    block = take(slice(None), slice(None))
+    lanes = 2 * cols
+    gap = lanes - cols - 2 * HALO
+
+    def to_lanes(band):
+        count = band.shape[1]
+        return jnp.concatenate(
+            [
+                band[:, :, HALO:-HALO],
+                band[:, :, -HALO:],
+                jnp.zeros((band.shape[0], count, gap), jnp.float32),
+                band[:, :, :HALO],
+            ],
+            axis=2,
+        )
+
+    middle = jnp.concatenate(
+        [block, east, jnp.zeros((block.shape[0], rows, gap), jnp.float32), west], axis=2
+    )
+    lead = ROW_OFFSET - HALO
+    tail = ROW_PAD - ROW_OFFSET - rows - HALO
+    grid = jnp.concatenate(
+        [
+            jnp.zeros((block.shape[0], lead, lanes), jnp.float32),
+            to_lanes(south),
+            middle,
+            to_lanes(north),
+            jnp.zeros((block.shape[0], tail, lanes), jnp.float32),
+        ],
+        axis=1,
+    )
+    flags = jnp.stack(
+        [(lax.axis_index("lat") == 0).astype(jnp.float32), jnp.float32(0.0)]
+    )
+    out = pl.pallas_call(
+        two_steps_kernel,
+        out_shape=jax.ShapeDtypeStruct((channels - 1, levels, rows, cols), jnp.float32),
+        in_specs=[
+            pl.BlockSpec(memory_space=pltpu.SMEM),
+            pl.BlockSpec(memory_space=pltpu.SMEM),
+            pl.BlockSpec(memory_space=pltpu.VMEM),
+        ],
+        out_specs=pl.BlockSpec(memory_space=pltpu.VMEM),
+    )(layer_height, flags, grid)
+    return (out[0], out[1], out[2], out[3])
+
+
+ROW_OFFSET = 8
+ROW_PAD = 112
+
+
+def two_steps_kernel(height_ref, flag_ref, grid_ref, out_ref):
+    levels = out_ref.shape[1]
+    rows, cols = out_ref.shape[2], out_ref.shape[3]
+    count, width = grid_ref.shape[1], grid_ref.shape[2]
+    lane = lax.broadcasted_iota(jnp.int32, (count, width), 1)
+    sub = lax.broadcasted_iota(jnp.int32, (count, width), 0)
+    lane_fwd = pltpu.roll(lane, 1, 1) == (lane + width - 1) % width
+    sub_fwd = pltpu.roll(sub, 1, 0) == (sub + count - 1) % count
+
+    def east_of(x):
+        return jnp.where(lane_fwd, pltpu.roll(x, width - 1, 1), pltpu.roll(x, 1, 1))
+
+    def west_of(x):
+        return jnp.where(lane_fwd, pltpu.roll(x, 1, 1), pltpu.roll(x, width - 1, 1))
+
+    def north_of(x):
+        return jnp.where(sub_fwd, pltpu.roll(x, count - 1, 0), pltpu.roll(x, 1, 0))
+
+    def south_of(x):
+        return jnp.where(sub_fwd, pltpu.roll(x, 1, 0), pltpu.roll(x, count - 1, 0))
+
+    n_state = 5 * levels
+    floor_index = grid_ref[n_state]
+    zonal_spacing = grid_ref[n_state + 1]
+    meridional_spacing = grid_ref[n_state + 2]
+    rotation = grid_ref[n_state + 3]
+    eddy = grid_ref[n_state + 4]
+    diapycnal = [grid_ref[n_state + 5 + k] for k in range(levels - 1)]
+    heights = [height_ref[k] for k in range(levels)]
+    zonal_sq = zonal_spacing * zonal_spacing
+    merid_sq = meridional_spacing * meridional_spacing
+    half_zonal = 0.5 / zonal_spacing
+    half_merid = 0.5 / meridional_spacing
+    at_bottom = [(floor_index == float(k)).astype(jnp.float32) for k in range(levels)]
+
+    def one_step(state):
+        wet = state[4]
+        fields = state[:4]
+        pressure_column = []
+        running = None
+        for k in range(levels):
+            mass = (CONTRACTION * fields[1][k] - EXPANSION * fields[0][k]) * heights[k]
+            running = mass if running is None else running + mass
+            pressure_column.append(running - 0.5 * mass)
+        fluxes = []
+        for c in range(4):
+            fluxes.append(
+                [
+                    diapycnal[k] * (wet[k + 1] * wet[k]) * (fields[c][k + 1] - fields[c][k])
+                    for k in range(levels - 1)
+                ]
+            )
+        new_state = [[None] * levels for _ in range(5)]
+        for k in range(levels):
+            w = wet[k]
+            w_e, w_w, w_n, w_s = east_of(w), west_of(w), north_of(w), south_of(w)
+            weight_east, weight_west = w * w_e, w * w_w
+            weight_north, weight_south = w * w_n, w * w_s
+            u = fields[2][k]
+            v = fields[3][k]
+            p = pressure_column[k]
+            gradient_x = -(east_of(p) - west_of(p)) * half_zonal
+            gradient_y = -(north_of(p) - south_of(p)) * half_merid
+            for c in range(4):
+                f = fields[c][k]
+                f_e, f_w, f_n, f_s = east_of(f), west_of(f), north_of(f), south_of(f)
+                diffusion = eddy * (
+                    (weight_east * (f_e - f) + weight_west * (f_w - f)) / zonal_sq
+                    + (weight_north * (f_n - f) + weight_south * (f_s - f)) / merid_sq
+                )
+                advection = -(u * (f_e - f_w) * half_zonal + v * (f_n - f_s) * half_merid)
+                below = fluxes[c][k] if k < levels - 1 else 0.0
+                above = fluxes[c][k - 1] if k > 0 else 0.0
+                mixing = (below - above) / (heights[k] * heights[k])
+                tendency = advection + diffusion + mixing
+                if c == 2:
+                    tendency = tendency + rotation * v + gradient_x - BOTTOM_DRAG * at_bottom[k] * u
+                if c == 3:
+                    tendency = tendency - rotation * u + gradient_y - BOTTOM_DRAG * at_bottom[k] * v
+                new_state[c][k] = w * (f + TIME_STEP * tendency)
+            new_state[4][k] = w
+        return new_state
+
+    state0 = [[grid_ref[c * levels + k] for k in range(levels)] for c in range(5)]
+    state1 = one_step(state0)
+    clear = jnp.logical_and(sub == ROW_OFFSET - 1, flag_ref[0] > 0.5)
+    state1 = [[jnp.where(clear, 0.0, x) for x in channel] for channel in state1]
+    state2 = one_step(state1)
+    for c in range(4):
+        for k in range(levels):
+            out_ref[c, k] = state2[c][k][ROW_OFFSET : ROW_OFFSET + rows, :cols]
 
 
 def solution(mesh):

time: 74.1 us -> 71.1 us (0.960)
  the two profiles are of different devices: /device:TPU:192 before, /device:TPU:224 now
where the time goes in v9:
time: 71.1 us; the launch traced here: 70.8 us
  starting transfers between devices  33.7 us (47%)
  local copies, waits for them, and re-layouts  19.2 us (27%)
  other arithmetic  8.19 us (12%)
  Pallas kernels  8.1 us (11%)
  between operations  1.14 us (2%)
    ppermute x1, starting transfers between devices, exchange(): east = lax.ppermute(take(every, slice(0, h)), 'lon', west_pairs)  16.6 us
    ppermute x1, starting transfers between devices, exchange(): lax.ppermute(top_band, ('lon', 'lat'), fold_pairs(lon_count, lat_count, l...  9.32 us
    pallas_call x1, Pallas kernels, shards(): pl.pallas_call(two_steps_kernel, out_shape=jax.ShapeDtypeStruct((channels...  8.1 us
    concatenate x1, local copies, waits for them, and re-layouts, shards(): jnp.concatenate([jnp.zeros((block.shape[0], lead, lanes), jnp.float32), t...  6.17 us
    unnamed x72, local copies, waits for them, and re-layouts  5.52 us
    ppermute x1, starting transfers between devices, exchange(): north = lax.ppermute(bottom_band, 'lat', south_pairs)  4.55 us
    unnamed x22, other arithmetic  4.29 us
    concatenate x1, other arithmetic, shards(): jnp.concatenate([block, east, jnp.zeros((block.shape[0], rows, gap), jnp....  2.68 us
  transfers between devices with their start and end apart: 5, of which 1 were waited for; matrix products, arithmetic and copies ran while one was open for 20% of the time, Pallas kernels for 0%

profile of v9, /device:TPU:224, one launch (start us, length us, event | category | flops | bytes accessed | tf_op | source)
XLA Modules:
  0.0 70.8 jit_solution(16665740432422391164)
XLA Ops:
  0.7 1.2 %fusion.6 = (s32[4,96,2]{2,1,0:T(8,128)S(1)}, s32[4,96,2]{2,1,0:T(8,128)S(1)}) fusion(s32[4,96,128]{2,1,0:T(8,128)} %param.17), kind=kLoop, calls=%fused_computation.74 | loop fusion | bytes 12288 | tf_op jit(solution)/shard_map/slice | solution.py:168
  1.9 1.2 %fusion.7 = (f32[4,96,2]{2,1,0:T(8,128)S(1)}, f32[4,96,2]{2,1,0:T(8,128)S(1)}) fusion(f32[4,96,128]{2,1,0:T(8,128)} %param.13), kind=kLoop, calls=%fused_computation.75 | loop fusion | bytes 12288 | tf_op jit(solution)/shard_map/slice | solution.py:169
  5.2 1.9 %collective-permute-start = (f32[28,96,2]{1,2,0:T(2,128)S(1)}, f32[28,96,2]{1,2,0:T(2,128)S(1)}, u32[]{:S(2)}, u32[]{:S(2)}) collective-permute-start(f32[28,96,2]{1,2,0:T(2,128)S(1)} %constant_dynamic-update-slice_fusion), channel_id=1, source_target_pairs={{0,8},{8,16},{16,24},{24,32},{32,40},{40,48},{48,56},{56,64},{64,7... | collective-permute-start | bytes 64520 | tf_op jit(solution)/shard_map/ppermute | solution.py:120
  8.3 16.6 %collective-permute-start.1 = (f32[28,96,2]{1,2,0:T(2,128)S(1)}, f32[28,96,2]{1,2,0:T(2,128)S(1)}, u32[]{:S(2)}, u32[]{:S(2)}) collective-permute-start(f32[28,96,2]{1,2,0:T(2,128)S(1)} %constant_dynamic-update-slice_fusion.22), channel_id=1, source_target_pairs={{8,0},{16,8},{24,16},{32,24},{40,32},{48,40},{56,48},{64,56},{72,6... | collective-permute-start | bytes 64520 | tf_op jit(solution)/shard_map/ppermute | solution.py:121
  24.9 0.7 multiply_dynamic-update-slice_fusion.3
  25.6 0.7 multiply_dynamic-update-slice_fusion.2
  26.3 0.7 multiply_dynamic-update-slice_fusion.1
  27.0 0.7 multiply_dynamic-update-slice_fusion
  27.7 0.7 convert_dynamic-update-slice_fusion
  28.4 0.6 constant_dynamic-update-slice_fusion.38
  29.0 0.6 constant_dynamic-update-slice_fusion.37
  29.6 0.6 constant_dynamic-update-slice_fusion.36
  30.2 0.6 constant_dynamic-update-slice_fusion.35
  30.9 0.6 constant_dynamic-update-slice_fusion.34
  31.5 0.7 constant_dynamic-update-slice_fusion.33
  32.3 0.6 add_convert_fusion.flag_ref
  34.4 9.3 %collective-permute-start.3 = (f32[28,2,132]{2,1,0:T(2,128)S(1)}, f32[28,2,132]{2,1,0:T(2,128)S(1)}, u32[]{:S(2)}, u32[]{:S(2)}) collective-permute-start(f32[28,2,132]{2,1,0:T(2,128)S(1)} %pad_maximum_fusion.1), channel_id=1, source_target_pairs={{7,511},{15,503},{23,495},{31,487},{39,479},{47,471},{55,463},{63,... | collective-permute-start | bytes 88712 | tf_op jit(solution)/shard_map/ppermute | solution.py:128
  43.7 1.3 %collective-permute-start.2 = (f32[28,2,132]{2,1,0:T(2,128)S(1)}, f32[28,2,132]{2,1,0:T(2,128)S(1)}, u32[]{:S(2)}, u32[]{:S(2)}) collective-permute-start(f32[28,2,132]{2,1,0:T(2,128)S(1)} %pad_maximum_fusion.1), channel_id=1, source_target_pairs={{0,1},{1,2},{2,3},{3,4},{4,5},{5,6},{6,7},{8,9},{9,10},{10,11},{11... | collective-permute-start | bytes 88712 | tf_op jit(solution)/shard_map/ppermute | solution.py:137
  45.2 4.5 %collective-permute-start.4 = (f32[28,2,132]{2,1,0:T(2,128)S(1)}, f32[28,2,132]{2,1,0:T(2,128)S(1)}, u32[]{:S(2)}, u32[]{:S(2)}) collective-permute-start(f32[28,2,132]{2,1,0:T(2,128)S(1)} %pad_maximum_fusion.3), channel_id=1, source_target_pairs={{1,0},{2,1},{3,2},{4,3},{5,4},{6,5},{7,6},{9,8},{10,9},{11,10},{12... | collective-permute-start | bytes 88712 | tf_op jit(solution)/shard_map/ppermute | solution.py:138
  49.7 2.7 %pad_maximum_fusion = f32[28,96,256]{2,1,0:T(8,128)S(1)} fusion(f32[28,96,2]{2,1,0:T(8,128)} %copy-done.1, f32[28,96,2]{2,1,0:T(8,128)} %copy-done.2, f32[28,96,128]{2,1,0:T(8,128)} %constant_dynamic-update-slice_fusion.33, f32[256]{0:T(256)S(1)} %pad.14.clone), kind=kLoop, calls=%fused_computation | loop fusion | flops 2064384 | bytes 4172800 | tf_op jit(solution)/shard_map/concatenate | solution.py:197
  52.4 0.5 collective-permute-done.3
  54.4 6.2 %concatenate.53.grid_ref = f32[28,112,256]{2,1,0:T(8,128)} concatenate(f32[28,6,256]{2,1,0:T(8,128)S(1)} %broadcast.10, f32[28,2,256]{2,1,0:T(2,128)S(1)} %get-tuple-element.59, f32[28,96,256]{2,1,0:T(8,128)S(1)} %pad_maximum_fusion, f32[28,2,256]{2,1,0:T(2,128)S(1)} %get-tuple-element.58, f32[28,6,256]{2,1,0:T(8,128)S(1)} %broadcast.10), dimensions={1} | concatenate | bytes 6422528 | tf_op jit(solution)/shard_map/concatenate | solution.py:202
  60.6 8.1 %shard_map.156 = f32[4,4,96,128]{3,2,1,0:T(8,128)} custom-call(f32[4]{0:T(128)} %height_ref.1, f32[2]{0:T(128)} %add_convert_fusion.flag_ref, f32[28,112,256]{2,1,0:T(8,128)} %concatenate.53.grid_ref), custom_call_target="tpu_custom_call" | custom-call | tf_op jit(solution)/shard_map/pallas_call | solution.py:215
  68.7 2.1 %slice_bitcast_fusion = (f32[4,96,128]{2,1,0:T(8,128)}, f32[4,96,128]{2,1,0:T(8,128)}, f32[4,96,128]{2,1,0:T(8,128)}, f32[4,96,128]{2,1,0:T(8,128)}) fusion(f32[4,4,96,128]{3,2,1,0:T(8,128)} %shard_map.156), kind=kLoop, calls=%fused_computation.1 | loop fusion | bytes 1572864 | tf_op jit(solution)/shard_map/squeeze | solution.py:225
  (119 shorter events, 6.3 us)
Async XLA Ops:
  0.6 2.6 %copy-start.4 = (f32[4,96,128]{2,1,0:T(8,128)S(1)}, f32[4,96,128]{2,1,0:T(8,128)}, u32[]{:S(2)}) copy-start(f32[4,96,128]{2,1,0:T(8,128)} %param.14) | copy-start | bytes 589828
  0.6 2.9 %copy-start.5 = (f32[4,96,128]{2,1,0:T(8,128)S(1)}, f32[4,96,128]{2,1,0:T(8,128)}, u32[]{:S(2)}) copy-start(f32[4,96,128]{2,1,0:T(8,128)} %param.15) | copy-start | bytes 589828
  1.9 1.8 %copy-start.6 = (f32[4,96,128]{2,1,0:T(8,128)S(1)}, f32[4,96,128]{2,1,0:T(8,128)}, u32[]{:S(2)}) copy-start(f32[4,96,128]{2,1,0:T(8,128)} %param.16) | copy-start | bytes 589828
  3.2 0.8 %copy-start.8 = (s32[96,128]{1,0:T(8,128)S(1)}, s32[96,128]{1,0:T(8,128)}, u32[]{:S(2)}) copy-start(s32[96,128]{1,0:T(8,128)} %param.18) | copy-start | bytes 147460
  3.4 0.8 %copy-start.9 = (f32[96,128]{1,0:T(8,128)S(1)}, f32[96,128]{1,0:T(8,128)}, u32[]{:S(2)}) copy-start(f32[96,128]{1,0:T(8,128)} %param.19) | copy-start | bytes 147460
  3.4 1.0 %copy-start.10 = (f32[96,128]{1,0:T(8,128)S(1)}, f32[96,128]{1,0:T(8,128)}, u32[]{:S(2)}) copy-start(f32[96,128]{1,0:T(8,128)} %param.20) | copy-start | bytes 147460
  3.5 1.0 %copy-start.11 = (f32[96,128]{1,0:T(8,128)S(1)}, f32[96,128]{1,0:T(8,128)}, u32[]{:S(2)}) copy-start(f32[96,128]{1,0:T(8,128)} %param.21) | copy-start | bytes 147460
  3.5 1.2 %copy-start.12 = (f32[96,128]{1,0:T(8,128)S(1)}, f32[96,128]{1,0:T(8,128)}, u32[]{:S(2)}) copy-start(f32[96,128]{1,0:T(8,128)} %param.22) | copy-start | bytes 147460
  3.6 1.3 %copy-start.7 = (f32[3,96,128]{2,1,0:T(8,128)S(1)}, f32[3,96,128]{2,1,0:T(8,128)}, u32[]{:S(2)}) copy-start(f32[3,96,128]{2,1,0:T(8,128)} %param.23) | copy-start | bytes 442372
  4.5 20.3 %copy-start = (s32[4,96,128]{2,1,0:T(8,128)S(1)}, s32[4,96,128]{2,1,0:T(8,128)}, u32[]{:S(2)}) copy-start(s32[4,96,128]{2,1,0:T(8,128)} %param.17) | copy-start | bytes 589828
  4.5 20.3 %copy-start.3 = (f32[4,96,128]{2,1,0:T(8,128)S(1)}, f32[4,96,128]{2,1,0:T(8,128)}, u32[]{:S(2)}) copy-start(f32[4,96,128]{2,1,0:T(8,128)} %param.13) | copy-start | bytes 589828
  5.2 28.0 %collective-permute-start = (f32[28,96,2]{1,2,0:T(2,128)S(1)}, f32[28,96,2]{1,2,0:T(2,128)S(1)}, u32[]{:S(2)}, u32[]{:S(2)}) collective-permute-start(f32[28,96,2]{1,2,0:T(2,128)S(1)} %constant_dynamic-update-slice_fusion), channel_id=1, source_target_pairs={{0,8},{8,16},{16,24},{24,32},{32,40},{40,48},{48,56},{56,64},{64,7... | collective-permute-start | bytes 64520 | tf_op jit(solution)/shard_map/ppermute | solution.py:120
  8.3 25.4 %collective-permute-start.1 = (f32[28,96,2]{1,2,0:T(2,128)S(1)}, f32[28,96,2]{1,2,0:T(2,128)S(1)}, u32[]{:S(2)}, u32[]{:S(2)}) collective-permute-start(f32[28,96,2]{1,2,0:T(2,128)S(1)} %constant_dynamic-update-slice_fusion.22), channel_id=1, source_target_pairs={{8,0},{16,8},{24,16},{32,24},{40,32},{48,40},{56,48},{64,56},{72,6... | collective-permute-start | bytes 64520 | tf_op jit(solution)/shard_map/ppermute | solution.py:121
  26.3 6.6 %copy-start.13 = (f32[5]{0:T(128)S(1)}, f32[5]{0:T(128)}, u32[]{:S(2)}) copy-start(f32[5]{0:T(128)} %constant.6.clone) | copy-start | bytes 64
  33.6 11.5 %copy-start.1 = (f32[28,96,2]{2,1,0:T(8,128)}, f32[28,96,2]{2,1,0:T(8,128)S(1)}, u32[]{:S(2)}) copy-start(f32[28,96,2]{2,1,0:T(8,128)S(1)} %copy.28) | copy-start | bytes 64516
  34.2 11.0 %copy-start.2 = (f32[28,96,2]{2,1,0:T(8,128)}, f32[28,96,2]{2,1,0:T(8,128)S(1)}, u32[]{:S(2)}) copy-start(f32[28,96,2]{2,1,0:T(8,128)S(1)} %copy.40) | copy-start | bytes 64516
  34.4 18.5 %collective-permute-start.3 = (f32[28,2,132]{2,1,0:T(2,128)S(1)}, f32[28,2,132]{2,1,0:T(2,128)S(1)}, u32[]{:S(2)}, u32[]{:S(2)}) collective-permute-start(f32[28,2,132]{2,1,0:T(2,128)S(1)} %pad_maximum_fusion.1), channel_id=1, source_target_pairs={{7,511},{15,503},{23,495},{31,487},{39,479},{47,471},{55,463},{63,... | collective-permute-start | bytes 88712 | tf_op jit(solution)/shard_map/ppermute | solution.py:128
  43.7 10.4 %collective-permute-start.2 = (f32[28,2,132]{2,1,0:T(2,128)S(1)}, f32[28,2,132]{2,1,0:T(2,128)S(1)}, u32[]{:S(2)}, u32[]{:S(2)}) collective-permute-start(f32[28,2,132]{2,1,0:T(2,128)S(1)} %pad_maximum_fusion.1), channel_id=1, source_target_pairs={{0,1},{1,2},{2,3},{3,4},{4,5},{5,6},{6,7},{8,9},{9,10},{10,11},{11... | collective-permute-start | bytes 88712 | tf_op jit(solution)/shard_map/ppermute | solution.py:137
  45.2 8.7 %collective-permute-start.4 = (f32[28,2,132]{2,1,0:T(2,128)S(1)}, f32[28,2,132]{2,1,0:T(2,128)S(1)}, u32[]{:S(2)}, u32[]{:S(2)}) collective-permute-start(f32[28,2,132]{2,1,0:T(2,128)S(1)} %pad_maximum_fusion.3), channel_id=1, source_target_pairs={{1,0},{2,1},{3,2},{4,3},{5,4},{6,5},{7,6},{9,8},{10,9},{11,10},{12... | collective-permute-start | bytes 88712 | tf_op jit(solution)/shard_map/ppermute | solution.py:138

commit v10 on v9

--- a/solution.py
+++ b/solution.py
@@ -212,26 +212,28 @@
     flags = jnp.stack(
         [(lax.axis_index("lat") == 0).astype(jnp.float32), jnp.float32(0.0)]
     )
+    field_shape = jax.ShapeDtypeStruct((levels, rows, cols), jnp.float32)
     out = pl.pallas_call(
         two_steps_kernel,
-        out_shape=jax.ShapeDtypeStruct((channels - 1, levels, rows, cols), jnp.float32),
+        out_shape=[field_shape] * (channels - 1),
         in_specs=[
             pl.BlockSpec(memory_space=pltpu.SMEM),
             pl.BlockSpec(memory_space=pltpu.SMEM),
             pl.BlockSpec(memory_space=pltpu.VMEM),
         ],
-        out_specs=pl.BlockSpec(memory_space=pltpu.VMEM),
+        out_specs=[pl.BlockSpec(memory_space=pltpu.VMEM)] * (channels - 1),
+        compiler_params=pltpu.CompilerParams(allow_input_fusion=[False, False, True]),
     )(layer_height, flags, grid)
-    return (out[0], out[1], out[2], out[3])
+    return tuple(out)
 
 
 ROW_OFFSET = 8
 ROW_PAD = 112
 
 
-def two_steps_kernel(height_ref, flag_ref, grid_ref, out_ref):
-    levels = out_ref.shape[1]
-    rows, cols = out_ref.shape[2], out_ref.shape[3]
+def two_steps_kernel(height_ref, flag_ref, grid_ref, *out_refs):
+    levels = out_refs[0].shape[0]
+    rows, cols = out_refs[0].shape[1], out_refs[0].shape[2]
     count, width = grid_ref.shape[1], grid_ref.shape[2]
     lane = lax.broadcasted_iota(jnp.int32, (count, width), 1)
     sub = lax.broadcasted_iota(jnp.int32, (count, width), 0)
@@ -319,7 +321,7 @@
     state2 = one_step(state1)
     for c in range(4):
         for k in range(levels):
-            out_ref[c, k] = state2[c][k][ROW_OFFSET : ROW_OFFSET + rows, :cols]
+            out_refs[c][k] = state2[c][k][ROW_OFFSET : ROW_OFFSET + rows, :cols]
 
 
 def solution(mesh):

time: 71.1 us -> 68.7 us (0.966)
  the two profiles are of different devices: /device:TPU:224 before, /device:TPU:192 now
where the time goes in v10:
time: 68.7 us; the launch traced here: 68.4 us
  starting transfers between devices  40.3 us (59%)
  local copies, waits for them, and re-layouts  14 us (20%)
  Pallas kernels  7.9 us (11%)
  other arithmetic  4.46 us (6%)
  between operations  1.24 us (2%)
    ppermute x1, starting transfers between devices, exchange(): south = lax.ppermute(top_band, 'lat', north_pairs)  19.2 us
    ppermute x1, starting transfers between devices, exchange(): east = lax.ppermute(take(every, slice(0, h)), 'lon', west_pairs)  16.6 us
    pallas_call x1, Pallas kernels, shards(): pl.pallas_call(two_steps_kernel, out_shape=[field_shape] * (channels - 1)...  7.9 us
    concatenate x1, local copies, waits for them, and re-layouts, shards(): jnp.concatenate([jnp.zeros((block.shape[0], lead, lanes), jnp.float32), t...  6.17 us
    unnamed x74, local copies, waits for them, and re-layouts  3.07 us
    concatenate x1, other arithmetic, shards(): jnp.concatenate([block, east, jnp.zeros((block.shape[0], rows, gap), jnp....  2.69 us
    ppermute x1, starting transfers between devices, exchange(): north = lax.ppermute(bottom_band, 'lat', south_pairs)  1.92 us
    ppermute x1, starting transfers between devices, exchange(): west = lax.ppermute(take(every, slice(-h, None)), 'lon', east_pairs)  1.92 us
  transfers between devices with their start and end apart: 5, of which 1 were waited for; matrix products, arithmetic and copies ran while one was open for 10% of the time, Pallas kernels for 0%

profile of v10, /device:TPU:192, one launch (start us, length us, event | category | flops | bytes accessed | tf_op | source)
XLA Modules:
  0.0 68.4 jit_solution(8288438178001560161)
XLA Ops:
  0.7 1.2 %fusion.6 = (s32[4,96,2]{2,1,0:T(8,128)S(1)}, s32[4,96,2]{2,1,0:T(8,128)S(1)}) fusion(s32[4,96,128]{2,1,0:T(8,128)} %param.17), kind=kLoop, calls=%fused_computation.70 | loop fusion | bytes 12288 | tf_op jit(solution)/shard_map/slice | solution.py:168
  1.9 1.2 %fusion.7 = (f32[4,96,2]{2,1,0:T(8,128)S(1)}, f32[4,96,2]{2,1,0:T(8,128)S(1)}) fusion(f32[4,96,128]{2,1,0:T(8,128)} %param.13), kind=kLoop, calls=%fused_computation.71 | loop fusion | bytes 12288 | tf_op jit(solution)/shard_map/slice | solution.py:169
  3.2 0.1 fusion.5
  3.7 0.1 fusion.3
  4.9 0.1 fusion.8
  5.2 1.9 %collective-permute-start = (f32[28,96,2]{1,2,0:T(2,128)S(1)}, f32[28,96,2]{1,2,0:T(2,128)S(1)}, u32[]{:S(2)}, u32[]{:S(2)}) collective-permute-start(f32[28,96,2]{1,2,0:T(2,128)S(1)} %constant_dynamic-update-slice_fusion), channel_id=1, source_target_pairs={{0,8},{8,16},{16,24},{24,32},{32,40},{40,48},{48,56},{56,64},{64,7... | collective-permute-start | bytes 64520 | tf_op jit(solution)/shard_map/ppermute | solution.py:120
  8.3 16.6 %collective-permute-start.1 = (f32[28,96,2]{1,2,0:T(2,128)S(1)}, f32[28,96,2]{1,2,0:T(2,128)S(1)}, u32[]{:S(2)}, u32[]{:S(2)}) collective-permute-start(f32[28,96,2]{1,2,0:T(2,128)S(1)} %constant_dynamic-update-slice_fusion.22), channel_id=1, source_target_pairs={{8,0},{16,8},{24,16},{32,24},{40,32},{48,40},{56,48},{64,56},{72,6... | collective-permute-start | bytes 64520 | tf_op jit(solution)/shard_map/ppermute | solution.py:121
  25.3 0.8 %add_convert_fusion.flag_ref = f32[2]{0:T(128)} fusion(pred[1]{0:T(512)(128)(4,1)} %constant.9.clone.1, pred[1]{0:T(512)(128)(4,1)} %bitcast), kind=kLoop, calls=%fused_computation.64 | loop fusion | flops 4 | bytes 10 | tf_op jit(solution)/shard_map/stack | solution.py:212
  26.4 0.5 copy.28
  26.9 0.5 copy.40
  27.5 0.2 pad_maximum_fusion.1
  27.6 0.7 collective-permute-start.3
  28.3 19.2 %collective-permute-start.2 = (f32[28,2,132]{2,1,0:T(2,128)S(1)}, f32[28,2,132]{2,1,0:T(2,128)S(1)}, u32[]{:S(2)}, u32[]{:S(2)}) collective-permute-start(f32[28,2,132]{2,1,0:T(2,128)S(1)} %pad_maximum_fusion.1), channel_id=1, source_target_pairs={{0,1},{1,2},{2,3},{3,4},{4,5},{5,6},{6,7},{8,9},{9,10},{10,11},{11... | collective-permute-start | bytes 88712 | tf_op jit(solution)/shard_map/ppermute | solution.py:137
  47.5 0.2 pad_maximum_fusion.3
  47.7 1.9 %collective-permute-start.4 = (f32[28,2,132]{2,1,0:T(2,128)S(1)}, f32[28,2,132]{2,1,0:T(2,128)S(1)}, u32[]{:S(2)}, u32[]{:S(2)}) collective-permute-start(f32[28,2,132]{2,1,0:T(2,128)S(1)} %pad_maximum_fusion.3), channel_id=1, source_target_pairs={{1,0},{2,1},{3,2},{4,3},{5,4},{6,5},{7,6},{9,8},{10,9},{11,10},{12... | collective-permute-start | bytes 88712 | tf_op jit(solution)/shard_map/ppermute | solution.py:138
  49.6 2.7 %pad_maximum_fusion = f32[28,96,256]{2,1,0:T(8,128)S(1)} fusion(f32[28,96,2]{2,1,0:T(8,128)} %copy-done.1, f32[28,96,2]{2,1,0:T(8,128)} %copy-done.2, f32[28,96,128]{2,1,0:T(8,128)} %copy-done.7, f32[256]{0:T(256)S(1)} %pad.14.clone), kind=kLoop, calls=%fused_computation | loop fusion | flops 2064384 | bytes 4172800 | tf_op jit(solution)/shard_map/concatenate | solution.py:197
  52.4 0.3 reverse.2
  52.7 0.1 slice.270
  52.8 0.3 reverse.3
  53.2 0.1 slice.271
  53.3 0.5 collective-permute-done.4
  54.2 0.1 pad_maximum_fusion.4
  54.3 6.2 %concatenate.53.grid_ref = f32[28,112,256]{2,1,0:T(8,128)} concatenate(f32[28,6,256]{2,1,0:T(8,128)S(1)} %broadcast.10, f32[28,2,256]{2,1,0:T(2,128)S(1)} %get-tuple-element.55, f32[28,96,256]{2,1,0:T(8,128)S(1)} %pad_maximum_fusion, f32[28,2,256]{2,1,0:T(2,128)S(1)} %get-tuple-element.54, f32[28,6,256]{2,1,0:T(8,128)S(1)} %broadcast.10), dimensions={1} | concatenate | bytes 6422528 | tf_op jit(solution)/shard_map/concatenate | solution.py:202
  60.5 7.9 %shard_map.156 = (f32[4,96,128]{2,1,0:T(8,128)}, f32[4,96,128]{2,1,0:T(8,128)}, f32[4,96,128]{2,1,0:T(8,128)}, f32[4,96,128]{2,1,0:T(8,128)}) custom-call(f32[4]{0:T(128)} %height_ref.1, f32[2]{0:T(128)} %add_convert_fusion.flag_ref, f32[28,112,256]{2,1,0:T(8,128)} %concatenate.53.grid_ref), custom_call_target="tpu_custom_call" | custom-call | tf_op jit(solution)/shard_map/pallas_call | solution.py:216
  (120 shorter events, 3.8 us)
Async XLA Ops:
  0.6 2.6 %copy-start.4 = (f32[4,96,128]{2,1,0:T(8,128)S(1)}, f32[4,96,128]{2,1,0:T(8,128)}, u32[]{:S(2)}) copy-start(f32[4,96,128]{2,1,0:T(8,128)} %param.14) | copy-start | bytes 589828
  0.6 2.9 %copy-start.5 = (f32[4,96,128]{2,1,0:T(8,128)S(1)}, f32[4,96,128]{2,1,0:T(8,128)}, u32[]{:S(2)}) copy-start(f32[4,96,128]{2,1,0:T(8,128)} %param.15) | copy-start | bytes 589828
  1.9 1.8 %copy-start.6 = (f32[4,96,128]{2,1,0:T(8,128)S(1)}, f32[4,96,128]{2,1,0:T(8,128)}, u32[]{:S(2)}) copy-start(f32[4,96,128]{2,1,0:T(8,128)} %param.16) | copy-start | bytes 589828
  3.2 0.8 %copy-start.9 = (s32[96,128]{1,0:T(8,128)S(1)}, s32[96,128]{1,0:T(8,128)}, u32[]{:S(2)}) copy-start(s32[96,128]{1,0:T(8,128)} %param.18) | copy-start | bytes 147460
  3.4 0.8 %copy-start.10 = (f32[96,128]{1,0:T(8,128)S(1)}, f32[96,128]{1,0:T(8,128)}, u32[]{:S(2)}) copy-start(f32[96,128]{1,0:T(8,128)} %param.19) | copy-start | bytes 147460
  3.4 1.0 %copy-start.11 = (f32[96,128]{1,0:T(8,128)S(1)}, f32[96,128]{1,0:T(8,128)}, u32[]{:S(2)}) copy-start(f32[96,128]{1,0:T(8,128)} %param.20) | copy-start | bytes 147460
  3.5 1.0 %copy-start.12 = (f32[96,128]{1,0:T(8,128)S(1)}, f32[96,128]{1,0:T(8,128)}, u32[]{:S(2)}) copy-start(f32[96,128]{1,0:T(8,128)} %param.21) | copy-start | bytes 147460
  3.5 1.2 %copy-start.13 = (f32[96,128]{1,0:T(8,128)S(1)}, f32[96,128]{1,0:T(8,128)}, u32[]{:S(2)}) copy-start(f32[96,128]{1,0:T(8,128)} %param.22) | copy-start | bytes 147460
  3.6 1.3 %copy-start.8 = (f32[3,96,128]{2,1,0:T(8,128)S(1)}, f32[3,96,128]{2,1,0:T(8,128)}, u32[]{:S(2)}) copy-start(f32[3,96,128]{2,1,0:T(8,128)} %param.23) | copy-start | bytes 442372
  4.5 20.3 %copy-start = (s32[4,96,128]{2,1,0:T(8,128)S(1)}, s32[4,96,128]{2,1,0:T(8,128)}, u32[]{:S(2)}) copy-start(s32[4,96,128]{2,1,0:T(8,128)} %param.17) | copy-start | bytes 589828
  4.5 20.3 %copy-start.3 = (f32[4,96,128]{2,1,0:T(8,128)S(1)}, f32[4,96,128]{2,1,0:T(8,128)}, u32[]{:S(2)}) copy-start(f32[4,96,128]{2,1,0:T(8,128)} %param.13) | copy-start | bytes 589828
  5.2 21.2 %collective-permute-start = (f32[28,96,2]{1,2,0:T(2,128)S(1)}, f32[28,96,2]{1,2,0:T(2,128)S(1)}, u32[]{:S(2)}, u32[]{:S(2)}) collective-permute-start(f32[28,96,2]{1,2,0:T(2,128)S(1)} %constant_dynamic-update-slice_fusion), channel_id=1, source_target_pairs={{0,8},{8,16},{16,24},{24,32},{32,40},{40,48},{48,56},{56,64},{64,7... | collective-permute-start | bytes 64520 | tf_op jit(solution)/shard_map/ppermute | solution.py:120
  8.3 18.7 %collective-permute-start.1 = (f32[28,96,2]{1,2,0:T(2,128)S(1)}, f32[28,96,2]{1,2,0:T(2,128)S(1)}, u32[]{:S(2)}, u32[]{:S(2)}) collective-permute-start(f32[28,96,2]{1,2,0:T(2,128)S(1)} %constant_dynamic-update-slice_fusion.22), channel_id=1, source_target_pairs={{8,0},{16,8},{24,16},{32,24},{40,32},{48,40},{56,48},{64,56},{72,6... | collective-permute-start | bytes 64520 | tf_op jit(solution)/shard_map/ppermute | solution.py:121
  25.0 1.2 %copy-start.14 = (f32[5]{0:T(128)S(1)}, f32[5]{0:T(128)}, u32[]{:S(2)}) copy-start(f32[5]{0:T(128)} %constant.6.clone) | copy-start | bytes 64
  25.2 1.3 %copy-start.7 = (f32[28,96,128]{2,1,0:T(8,128)}, f32[28,96,128]{2,1,0:T(8,128)S(1)}, u32[]{:S(2)}) copy-start(f32[28,96,128]{2,1,0:T(8,128)S(1)} %constant_dynamic-update-slice_fusion.33) | copy-start | bytes 4128772
  26.9 20.8 %copy-start.1 = (f32[28,96,2]{2,1,0:T(8,128)}, f32[28,96,2]{2,1,0:T(8,128)S(1)}, u32[]{:S(2)}) copy-start(f32[28,96,2]{2,1,0:T(8,128)S(1)} %copy.28) | copy-start | bytes 64516
  27.4 20.3 %copy-start.2 = (f32[28,96,2]{2,1,0:T(8,128)}, f32[28,96,2]{2,1,0:T(8,128)S(1)}, u32[]{:S(2)}) copy-start(f32[28,96,2]{2,1,0:T(8,128)S(1)} %copy.40) | copy-start | bytes 64516
  27.6 24.7 %collective-permute-start.3 = (f32[28,2,132]{2,1,0:T(2,128)S(1)}, f32[28,2,132]{2,1,0:T(2,128)S(1)}, u32[]{:S(2)}, u32[]{:S(2)}) collective-permute-start(f32[28,2,132]{2,1,0:T(2,128)S(1)} %pad_maximum_fusion.1), channel_id=1, source_target_pairs={{7,511},{15,503},{23,495},{31,487},{39,479},{47,471},{55,463},{63,... | collective-permute-start | bytes 88712 | tf_op jit(solution)/shard_map/ppermute | solution.py:128
  28.3 25.7 %collective-permute-start.2 = (f32[28,2,132]{2,1,0:T(2,128)S(1)}, f32[28,2,132]{2,1,0:T(2,128)S(1)}, u32[]{:S(2)}, u32[]{:S(2)}) collective-permute-start(f32[28,2,132]{2,1,0:T(2,128)S(1)} %pad_maximum_fusion.1), channel_id=1, source_target_pairs={{0,1},{1,2},{2,3},{3,4},{4,5},{5,6},{6,7},{8,9},{9,10},{10,11},{11... | collective-permute-start | bytes 88712 | tf_op jit(solution)/shard_map/ppermute | solution.py:137
  47.7 6.1 %collective-permute-start.4 = (f32[28,2,132]{2,1,0:T(2,128)S(1)}, f32[28,2,132]{2,1,0:T(2,128)S(1)}, u32[]{:S(2)}, u32[]{:S(2)}) collective-permute-start(f32[28,2,132]{2,1,0:T(2,128)S(1)} %pad_maximum_fusion.3), channel_id=1, source_target_pairs={{1,0},{2,1},{3,2},{4,3},{5,4},{6,5},{7,6},{9,8},{10,9},{11,10},{12... | collective-permute-start | bytes 88712 | tf_op jit(solution)/shard_map/ppermute | solution.py:138

commit v11 on v10

--- a/solution.py
+++ b/solution.py
@@ -199,15 +199,11 @@
     )
     lead = ROW_OFFSET - HALO
     tail = ROW_PAD - ROW_OFFSET - rows - HALO
-    grid = jnp.concatenate(
-        [
-            jnp.zeros((block.shape[0], lead, lanes), jnp.float32),
-            to_lanes(south),
-            middle,
-            to_lanes(north),
-            jnp.zeros((block.shape[0], tail, lanes), jnp.float32),
-        ],
-        axis=1,
+    rim_low = jnp.concatenate(
+        [jnp.zeros((block.shape[0], lead, lanes), jnp.float32), to_lanes(south)], axis=1
+    )
+    rim_high = jnp.concatenate(
+        [to_lanes(north), jnp.zeros((block.shape[0], tail, lanes), jnp.float32)], axis=1
     )
     flags = jnp.stack(
         [(lax.axis_index("lat") == 0).astype(jnp.float32), jnp.float32(0.0)]
@@ -220,10 +216,11 @@
             pl.BlockSpec(memory_space=pltpu.SMEM),
             pl.BlockSpec(memory_space=pltpu.SMEM),
             pl.BlockSpec(memory_space=pltpu.VMEM),
+            pl.BlockSpec(memory_space=pltpu.VMEM),
+            pl.BlockSpec(memory_space=pltpu.VMEM),
         ],
         out_specs=[pl.BlockSpec(memory_space=pltpu.VMEM)] * (channels - 1),
-        compiler_params=pltpu.CompilerParams(allow_input_fusion=[False, False, True]),
-    )(layer_height, flags, grid)
+    )(layer_height, flags, rim_low, middle, rim_high)
     return tuple(out)
 
 
@@ -231,10 +228,15 @@
 ROW_PAD = 112
 
 
-def two_steps_kernel(height_ref, flag_ref, grid_ref, *out_refs):
+def two_steps_kernel(height_ref, flag_ref, low_ref, middle_ref, high_ref, *out_refs):
     levels = out_refs[0].shape[0]
     rows, cols = out_refs[0].shape[1], out_refs[0].shape[2]
-    count, width = grid_ref.shape[1], grid_ref.shape[2]
+    count = low_ref.shape[1] + middle_ref.shape[1] + high_ref.shape[1]
+    width = middle_ref.shape[2]
+
+    def plane(p):
+        return jnp.concatenate([low_ref[p], middle_ref[p], high_ref[p]], axis=0)
+
     lane = lax.broadcasted_iota(jnp.int32, (count, width), 1)
     sub = lax.broadcasted_iota(jnp.int32, (count, width), 0)
     lane_fwd = pltpu.roll(lane, 1, 1) == (lane + width - 1) % width
@@ -253,12 +255,12 @@
         return jnp.where(sub_fwd, pltpu.roll(x, 1, 0), pltpu.roll(x, count - 1, 0))
 
     n_state = 5 * levels
-    floor_index = grid_ref[n_state]
-    zonal_spacing = grid_ref[n_state + 1]
-    meridional_spacing = grid_ref[n_state + 2]
-    rotation = grid_ref[n_state + 3]
-    eddy = grid_ref[n_state + 4]
-    diapycnal = [grid_ref[n_state + 5 + k] for k in range(levels - 1)]
+    floor_index = plane(n_state)
+    zonal_spacing = plane(n_state + 1)
+    meridional_spacing = plane(n_state + 2)
+    rotation = plane(n_state + 3)
+    eddy = plane(n_state + 4)
+    diapycnal = [plane(n_state + 5 + k) for k in range(levels - 1)]
     heights = [height_ref[k] for k in range(levels)]
     zonal_sq = zonal_spacing * zonal_spacing
     merid_sq = meridional_spacing * meridional_spacing
@@ -314,7 +316,7 @@
             new_state[4][k] = w
         return new_state
 
-    state0 = [[grid_ref[c * levels + k] for k in range(levels)] for c in range(5)]
+    state0 = [[plane(c * levels + k) for k in range(levels)] for c in range(5)]
     state1 = one_step(state0)
     clear = jnp.logical_and(sub == ROW_OFFSET - 1, flag_ref[0] > 0.5)
     state1 = [[jnp.where(clear, 0.0, x) for x in channel] for channel in state1]

time: 68.7 us -> 66.9 us (0.974)
  the two profiles are of different devices: /device:TPU:192 before, /device:TPU:224 now
where the time goes in v11:
time: 66.9 us; the launch traced here: 66.6 us
  starting transfers between devices  22.6 us (34%)
  waiting for transfers between devices  20.6 us (31%)
  local copies, waits for them, and re-layouts  9.23 us (14%)
  Pallas kernels  7.82 us (12%)
  other arithmetic  5.21 us (8%)
  between operations  1.19 us (2%)
    ppermute x1, waiting for transfers between devices, exchange(): west = lax.ppermute(take(every, slice(-h, None)), 'lon', east_pairs)  14.1 us
    ppermute x1, starting transfers between devices, exchange(): east = lax.ppermute(take(every, slice(0, h)), 'lon', west_pairs)  12.3 us
    pallas_call x1, Pallas kernels, shards(): pl.pallas_call(two_steps_kernel, out_shape=[field_shape] * (channels - 1)...  7.82 us
    ppermute x1, waiting for transfers between devices, exchange(): lax.ppermute(top_band, ('lon', 'lat'), fold_pairs(lon_count, lat_count, l...  6.53 us
    ppermute x1, starting transfers between devices, exchange(): north = lax.ppermute(bottom_band, 'lat', south_pairs)  4.55 us
    concatenate x1, other arithmetic, shards(): jnp.concatenate([block, east, jnp.zeros((block.shape[0], rows, gap), jnp....  3.39 us
    unnamed x70, local copies, waits for them, and re-layouts  3.06 us
    ppermute x1, starting transfers between devices, exchange(): lax.ppermute(top_band, ('lon', 'lat'), fold_pairs(lon_count, lat_count, l...  2.49 us
  transfers between devices with their start and end apart: 5, of which 2 were waited for; matrix products, arithmetic and copies ran while one was open for 12% of the time, Pallas kernels for 0%

profile of v11, /device:TPU:224, one launch (start us, length us, event | category | flops | bytes accessed | tf_op | source)
XLA Modules:
  0.0 66.6 jit_solution(16630187260766814141)
XLA Ops:
  0.7 1.2 %fusion.7 = (f32[4,96,2]{2,1,0:T(8,128)S(1)}, f32[4,96,2]{2,1,0:T(8,128)S(1)}) fusion(f32[4,96,128]{2,1,0:T(8,128)} %param.13), kind=kLoop, calls=%fused_computation.71 | loop fusion | bytes 12288 | tf_op jit(solution)/shard_map/slice | solution.py:169
  1.9 1.2 %fusion.6 = (s32[4,96,2]{2,1,0:T(8,128)S(1)}, s32[4,96,2]{2,1,0:T(8,128)S(1)}) fusion(s32[4,96,128]{2,1,0:T(8,128)} %param.17), kind=kLoop, calls=%fused_computation.70 | loop fusion | bytes 12288 | tf_op jit(solution)/shard_map/slice | solution.py:168
  3.2 0.1 fusion.5
  3.7 0.1 fusion.3
  5.2 12.3 %collective-permute-start.1 = (f32[28,96,2]{1,2,0:T(2,128)S(1)}, f32[28,96,2]{1,2,0:T(2,128)S(1)}, u32[]{:S(2)}, u32[]{:S(2)}) collective-permute-start(f32[28,96,2]{1,2,0:T(2,128)S(1)} %constant_dynamic-update-slice_fusion.22), channel_id=1, source_target_pairs={{8,0},{16,8},{24,16},{32,24},{40,32},{48,40},{56,48},{64,56},{72,6... | collective-permute-start | bytes 64520 | tf_op jit(solution)/shard_map/ppermute | solution.py:121
  18.7 1.9 %collective-permute-start = (f32[28,96,2]{1,2,0:T(2,128)S(1)}, f32[28,96,2]{1,2,0:T(2,128)S(1)}, u32[]{:S(2)}, u32[]{:S(2)}) collective-permute-start(f32[28,96,2]{1,2,0:T(2,128)S(1)} %constant_dynamic-update-slice_fusion), channel_id=1, source_target_pairs={{0,8},{8,16},{16,24},{24,32},{32,40},{40,48},{48,56},{56,64},{64,7... | collective-permute-start | bytes 64520 | tf_op jit(solution)/shard_map/ppermute | solution.py:120
  21.1 0.9 %add_convert_fusion.flag_ref = f32[2]{0:T(128)} fusion(pred[1]{0:T(512)(128)(4,1)} %constant.9.clone.1, pred[1]{0:T(512)(128)(4,1)} %bitcast), kind=kLoop, calls=%fused_computation.64 | loop fusion | flops 4 | bytes 10 | tf_op jit(solution)/shard_map/stack | solution.py:208
  22.2 0.5 copy.40
  22.7 14.1 %collective-permute-done = f32[28,96,2]{1,2,0:T(2,128)S(1)} collective-permute-done((f32[28,96,2]{1,2,0:T(2,128)S(1)}, f32[28,96,2]{1,2,0:T(2,128)S(1)}, u32[]{:S(2)}, u32[]{:S(2)}) %collective-permute-start) | collective-permute-done | bytes 21536 | tf_op jit(solution)/shard_map/ppermute | solution.py:120
  36.8 0.5 copy.28
  37.3 0.2 pad_maximum_fusion.1
  37.4 2.5 %collective-permute-start.3 = (f32[28,2,132]{2,1,0:T(2,128)S(1)}, f32[28,2,132]{2,1,0:T(2,128)S(1)}, u32[]{:S(2)}, u32[]{:S(2)}) collective-permute-start(f32[28,2,132]{2,1,0:T(2,128)S(1)} %pad_maximum_fusion.1), channel_id=1, source_target_pairs={{7,511},{15,503},{23,495},{31,487},{39,479},{47,471},{55,463},{63,... | collective-permute-start | bytes 88712 | tf_op jit(solution)/shard_map/ppermute | solution.py:128
  39.9 1.3 %collective-permute-start.2 = (f32[28,2,132]{2,1,0:T(2,128)S(1)}, f32[28,2,132]{2,1,0:T(2,128)S(1)}, u32[]{:S(2)}, u32[]{:S(2)}) collective-permute-start(f32[28,2,132]{2,1,0:T(2,128)S(1)} %pad_maximum_fusion.1), channel_id=1, source_target_pairs={{0,1},{1,2},{2,3},{3,4},{4,5},{5,6},{6,7},{8,9},{9,10},{10,11},{11... | collective-permute-start | bytes 88712 | tf_op jit(solution)/shard_map/ppermute | solution.py:137
  41.2 0.2 pad_maximum_fusion.3
  41.4 4.5 %collective-permute-start.4 = (f32[28,2,132]{2,1,0:T(2,128)S(1)}, f32[28,2,132]{2,1,0:T(2,128)S(1)}, u32[]{:S(2)}, u32[]{:S(2)}) collective-permute-start(f32[28,2,132]{2,1,0:T(2,128)S(1)} %pad_maximum_fusion.3), channel_id=1, source_target_pairs={{1,0},{2,1},{3,2},{4,3},{5,4},{6,5},{7,6},{9,8},{10,9},{11,10},{12... | collective-permute-start | bytes 88712 | tf_op jit(solution)/shard_map/ppermute | solution.py:138
  46.0 3.4 %pad_maximum_fusion.middle_ref = f32[28,96,256]{2,1,0:T(8,128)} fusion(f32[28,96,2]{2,1,0:T(8,128)S(1)} %copy.28, f32[28,96,2]{2,1,0:T(8,128)S(1)} %copy.40, f32[28,96,128]{2,1,0:T(8,128)} %copy-done.5, f32[256]{0:T(256)S(1)} %pad.16.clone), kind=kLoop, calls=%fused_computation | loop fusion | flops 2064384 | bytes 4172800 | tf_op jit(solution)/shard_map/concatenate | solution.py:197
  49.3 6.5 %collective-permute-done.3 = f32[28,2,132]{2,1,0:T(2,128)S(1)} collective-permute-done((f32[28,2,132]{2,1,0:T(2,128)S(1)}, f32[28,2,132]{2,1,0:T(2,128)S(1)}, u32[]{:S(2)}, u32[]{:S(2)}) %collective-permute-start.3) | collective-permute-done | bytes 29600 | tf_op jit(solution)/shard_map/ppermute | solution.py:128
  55.9 0.3 reverse.2
  56.2 0.1 slice.270
  56.4 0.3 reverse.3
  57.2 0.1 pad_maximum_fusion.4
  57.4 0.7 %concatenate.49.low_ref = f32[28,8,256]{2,1,0:T(8,128)} pad(f32[28,2,256]{2,1,0:T(2,128)S(1)} %get-tuple-element.55, f32[]{:T(128)} %constant.3.clone.1), padding=0_0x6_0x0_0 | pad | bytes 286724 | tf_op jit(solution)/shard_map/concatenate | solution.py:202
  58.1 0.7 %concatenate.57.high_ref = f32[28,8,256]{2,1,0:T(8,128)} pad(f32[28,2,256]{2,1,0:T(2,128)S(1)} %get-tuple-element.54, f32[]{:T(128)} %constant.3.clone.1), padding=0_0x0_6x0_0 | pad | bytes 286724 | tf_op jit(solution)/shard_map/concatenate | solution.py:205
  58.8 7.8 %shard_map.156 = (f32[4,96,128]{2,1,0:T(8,128)}, f32[4,96,128]{2,1,0:T(8,128)}, f32[4,96,128]{2,1,0:T(8,128)}, f32[4,96,128]{2,1,0:T(8,128)}) custom-call(f32[4]{0:T(128)} %height_ref.1, f32[2]{0:T(128)} %add_convert_fusion.flag_ref, f32[28,8,256]{2,1,0:T(8,128)} %concatenate.49.low_ref, f32[28,96,256]{2,1,0:T(8,128)} %pad_maximum_fusion.middle_ref, ...), custom_call_target="tpu_custom_call" | custom-call | tf_op jit(solution)/shard_map/pallas_call | solution.py:212
  (116 shorter events, 4.0 us)
Async XLA Ops:
  0.6 2.6 %copy-start.2 = (f32[4,96,128]{2,1,0:T(8,128)S(1)}, f32[4,96,128]{2,1,0:T(8,128)}, u32[]{:S(2)}) copy-start(f32[4,96,128]{2,1,0:T(8,128)} %param.14) | copy-start | bytes 589828
  0.6 2.9 %copy-start.3 = (f32[4,96,128]{2,1,0:T(8,128)S(1)}, f32[4,96,128]{2,1,0:T(8,128)}, u32[]{:S(2)}) copy-start(f32[4,96,128]{2,1,0:T(8,128)} %param.15) | copy-start | bytes 589828
  1.9 1.8 %copy-start.4 = (f32[4,96,128]{2,1,0:T(8,128)S(1)}, f32[4,96,128]{2,1,0:T(8,128)}, u32[]{:S(2)}) copy-start(f32[4,96,128]{2,1,0:T(8,128)} %param.16) | copy-start | bytes 589828
  3.2 0.8 %copy-start.7 = (s32[96,128]{1,0:T(8,128)S(1)}, s32[96,128]{1,0:T(8,128)}, u32[]{:S(2)}) copy-start(s32[96,128]{1,0:T(8,128)} %param.18) | copy-start | bytes 147460
  3.4 0.8 %copy-start.8 = (f32[96,128]{1,0:T(8,128)S(1)}, f32[96,128]{1,0:T(8,128)}, u32[]{:S(2)}) copy-start(f32[96,128]{1,0:T(8,128)} %param.19) | copy-start | bytes 147460
  3.4 1.0 %copy-start.9 = (f32[96,128]{1,0:T(8,128)S(1)}, f32[96,128]{1,0:T(8,128)}, u32[]{:S(2)}) copy-start(f32[96,128]{1,0:T(8,128)} %param.20) | copy-start | bytes 147460
  3.5 1.0 %copy-start.10 = (f32[96,128]{1,0:T(8,128)S(1)}, f32[96,128]{1,0:T(8,128)}, u32[]{:S(2)}) copy-start(f32[96,128]{1,0:T(8,128)} %param.21) | copy-start | bytes 147460
  3.5 1.2 %copy-start.11 = (f32[96,128]{1,0:T(8,128)S(1)}, f32[96,128]{1,0:T(8,128)}, u32[]{:S(2)}) copy-start(f32[96,128]{1,0:T(8,128)} %param.22) | copy-start | bytes 147460
  3.6 1.2 %copy-start.6 = (f32[3,96,128]{2,1,0:T(8,128)S(1)}, f32[3,96,128]{2,1,0:T(8,128)}, u32[]{:S(2)}) copy-start(f32[3,96,128]{2,1,0:T(8,128)} %param.23) | copy-start | bytes 442372
  4.5 16.0 %copy-start = (s32[4,96,128]{2,1,0:T(8,128)S(1)}, s32[4,96,128]{2,1,0:T(8,128)}, u32[]{:S(2)}) copy-start(s32[4,96,128]{2,1,0:T(8,128)} %param.17) | copy-start | bytes 589828
  4.5 16.1 %copy-start.1 = (f32[4,96,128]{2,1,0:T(8,128)S(1)}, f32[4,96,128]{2,1,0:T(8,128)}, u32[]{:S(2)}) copy-start(f32[4,96,128]{2,1,0:T(8,128)} %param.13) | copy-start | bytes 589828
  5.2 17.0 %collective-permute-start.1 = (f32[28,96,2]{1,2,0:T(2,128)S(1)}, f32[28,96,2]{1,2,0:T(2,128)S(1)}, u32[]{:S(2)}, u32[]{:S(2)}) collective-permute-start(f32[28,96,2]{1,2,0:T(2,128)S(1)} %constant_dynamic-update-slice_fusion.22), channel_id=1, source_target_pairs={{8,0},{16,8},{24,16},{32,24},{40,32},{48,40},{56,48},{64,56},{72,6... | collective-permute-start | bytes 64520 | tf_op jit(solution)/shard_map/ppermute | solution.py:121
  18.7 18.1 %collective-permute-start = (f32[28,96,2]{1,2,0:T(2,128)S(1)}, f32[28,96,2]{1,2,0:T(2,128)S(1)}, u32[]{:S(2)}, u32[]{:S(2)}) collective-permute-start(f32[28,96,2]{1,2,0:T(2,128)S(1)} %constant_dynamic-update-slice_fusion), channel_id=1, source_target_pairs={{0,8},{8,16},{16,24},{24,32},{32,40},{40,48},{48,56},{56,64},{64,7... | collective-permute-start | bytes 64520 | tf_op jit(solution)/shard_map/ppermute | solution.py:120
  20.7 1.2 %copy-start.12 = (f32[5]{0:T(128)S(1)}, f32[5]{0:T(128)}, u32[]{:S(2)}) copy-start(f32[5]{0:T(128)} %constant.6.clone) | copy-start | bytes 64
  20.9 1.3 %copy-start.5 = (f32[28,96,128]{2,1,0:T(8,128)}, f32[28,96,128]{2,1,0:T(8,128)S(1)}, u32[]{:S(2)}) copy-start(f32[28,96,128]{2,1,0:T(8,128)S(1)} %constant_dynamic-update-slice_fusion.33) | copy-start | bytes 4128772
  37.4 18.4 %collective-permute-start.3 = (f32[28,2,132]{2,1,0:T(2,128)S(1)}, f32[28,2,132]{2,1,0:T(2,128)S(1)}, u32[]{:S(2)}, u32[]{:S(2)}) collective-permute-start(f32[28,2,132]{2,1,0:T(2,128)S(1)} %pad_maximum_fusion.1), channel_id=1, source_target_pairs={{7,511},{15,503},{23,495},{31,487},{39,479},{47,471},{55,463},{63,... | collective-permute-start | bytes 88712 | tf_op jit(solution)/shard_map/ppermute | solution.py:128
  39.9 17.1 %collective-permute-start.2 = (f32[28,2,132]{2,1,0:T(2,128)S(1)}, f32[28,2,132]{2,1,0:T(2,128)S(1)}, u32[]{:S(2)}, u32[]{:S(2)}) collective-permute-start(f32[28,2,132]{2,1,0:T(2,128)S(1)} %pad_maximum_fusion.1), channel_id=1, source_target_pairs={{0,1},{1,2},{2,3},{3,4},{4,5},{5,6},{6,7},{8,9},{9,10},{10,11},{11... | collective-permute-start | bytes 88712 | tf_op jit(solution)/shard_map/ppermute | solution.py:137
  41.4 15.4 %collective-permute-start.4 = (f32[28,2,132]{2,1,0:T(2,128)S(1)}, f32[28,2,132]{2,1,0:T(2,128)S(1)}, u32[]{:S(2)}, u32[]{:S(2)}) collective-permute-start(f32[28,2,132]{2,1,0:T(2,128)S(1)} %pad_maximum_fusion.3), channel_id=1, source_target_pairs={{1,0},{2,1},{3,2},{4,3},{5,4},{6,5},{7,6},{9,8},{10,9},{11,10},{12... | collective-permute-start | bytes 88712 | tf_op jit(solution)/shard_map/ppermute | solution.py:138

commit v12 on v11

--- a/solution.py
+++ b/solution.py
@@ -237,22 +237,19 @@
     def plane(p):
         return jnp.concatenate([low_ref[p], middle_ref[p], high_ref[p]], axis=0)
 
-    lane = lax.broadcasted_iota(jnp.int32, (count, width), 1)
     sub = lax.broadcasted_iota(jnp.int32, (count, width), 0)
-    lane_fwd = pltpu.roll(lane, 1, 1) == (lane + width - 1) % width
-    sub_fwd = pltpu.roll(sub, 1, 0) == (sub + count - 1) % count
 
     def east_of(x):
-        return jnp.where(lane_fwd, pltpu.roll(x, width - 1, 1), pltpu.roll(x, 1, 1))
+        return pltpu.roll(x, width - 1, 1)
 
     def west_of(x):
-        return jnp.where(lane_fwd, pltpu.roll(x, 1, 1), pltpu.roll(x, width - 1, 1))
+        return pltpu.roll(x, 1, 1)
 
     def north_of(x):
-        return jnp.where(sub_fwd, pltpu.roll(x, count - 1, 0), pltpu.roll(x, 1, 0))
+        return pltpu.roll(x, count - 1, 0)
 
     def south_of(x):
-        return jnp.where(sub_fwd, pltpu.roll(x, 1, 0), pltpu.roll(x, count - 1, 0))
+        return pltpu.roll(x, 1, 0)
 
     n_state = 5 * levels
     floor_index = plane(n_state)
@@ -262,8 +259,9 @@
     eddy = plane(n_state + 4)
     diapycnal = [plane(n_state + 5 + k) for k in range(levels - 1)]
     heights = [height_ref[k] for k in range(levels)]
-    zonal_sq = zonal_spacing * zonal_spacing
-    merid_sq = meridional_spacing * meridional_spacing
+    inv_zonal_sq = 1.0 / (zonal_spacing * zonal_spacing)
+    inv_merid_sq = 1.0 / (meridional_spacing * meridional_spacing)
+    inv_height_sq = [1.0 / (h * h) for h in heights]
     half_zonal = 0.5 / zonal_spacing
     half_merid = 0.5 / meridional_spacing
     at_bottom = [(floor_index == float(k)).astype(jnp.float32) for k in range(levels)]
@@ -300,13 +298,13 @@
                 f = fields[c][k]
                 f_e, f_w, f_n, f_s = east_of(f), west_of(f), north_of(f), south_of(f)
                 diffusion = eddy * (
-                    (weight_east * (f_e - f) + weight_west * (f_w - f)) / zonal_sq
-                    + (weight_north * (f_n - f) + weight_south * (f_s - f)) / merid_sq
+                    (weight_east * (f_e - f) + weight_west * (f_w - f)) * inv_zonal_sq
+                    + (weight_north * (f_n - f) + weight_south * (f_s - f)) * inv_merid_sq
                 )
                 advection = -(u * (f_e - f_w) * half_zonal + v * (f_n - f_s) * half_merid)
                 below = fluxes[c][k] if k < levels - 1 else 0.0
                 above = fluxes[c][k - 1] if k > 0 else 0.0
-                mixing = (below - above) / (heights[k] * heights[k])
+                mixing = (below - above) * inv_height_sq[k]
                 tendency = advection + diffusion + mixing
                 if c == 2:
                     tendency = tendency + rotation * v + gradient_x - BOTTOM_DRAG * at_bottom[k] * u

time: 66.9 us -> 66.4 us (level)
  no operation moved by 1% of the time
where the time goes in v12:
time: 66.4 us; the launch traced here: 66.1 us
  starting transfers between devices  22.6 us (34%)
  waiting for transfers between devices  20.6 us (31%)
  local copies, waits for them, and re-layouts  9.23 us (14%)
  Pallas kernels  7.3 us (11%)
  other arithmetic  5.21 us (8%)
  between operations  1.19 us (2%)
    ppermute x1, waiting for transfers between devices, exchange(): west = lax.ppermute(take(every, slice(-h, None)), 'lon', east_pairs)  14.1 us
    ppermute x1, starting transfers between devices, exchange(): east = lax.ppermute(take(every, slice(0, h)), 'lon', west_pairs)  12.3 us
    pallas_call x1, Pallas kernels, shards(): pl.pallas_call(two_steps_kernel, out_shape=[field_shape] * (channels - 1)...  7.3 us
    ppermute x1, waiting for transfers between devices, exchange(): lax.ppermute(top_band, ('lon', 'lat'), fold_pairs(lon_count, lat_count, l...  6.53 us
    ppermute x1, starting transfers between devices, exchange(): north = lax.ppermute(bottom_band, 'lat', south_pairs)  4.55 us
    concatenate x1, other arithmetic, shards(): jnp.concatenate([block, east, jnp.zeros((block.shape[0], rows, gap), jnp....  3.39 us
    unnamed x70, local copies, waits for them, and re-layouts  3.06 us
    ppermute x1, starting transfers between devices, exchange(): lax.ppermute(top_band, ('lon', 'lat'), fold_pairs(lon_count, lat_count, l...  2.49 us
  transfers between devices with their start and end apart: 5, of which 2 were waited for; matrix products, arithmetic and copies ran while one was open for 12% of the time, Pallas kernels for 0%

profile of v12, /device:TPU:224, one launch (start us, length us, event | category | flops | bytes accessed | tf_op | source)
XLA Modules:
  0.0 66.1 jit_solution(7179204020164278844)
XLA Ops:
  0.7 1.2 %fusion.7 = (f32[4,96,2]{2,1,0:T(8,128)S(1)}, f32[4,96,2]{2,1,0:T(8,128)S(1)}) fusion(f32[4,96,128]{2,1,0:T(8,128)} %param.13), kind=kLoop, calls=%fused_computation.71 | loop fusion | bytes 12288 | tf_op jit(solution)/shard_map/slice | solution.py:169
  1.9 1.2 %fusion.6 = (s32[4,96,2]{2,1,0:T(8,128)S(1)}, s32[4,96,2]{2,1,0:T(8,128)S(1)}) fusion(s32[4,96,128]{2,1,0:T(8,128)} %param.17), kind=kLoop, calls=%fused_computation.70 | loop fusion | bytes 12288 | tf_op jit(solution)/shard_map/slice | solution.py:168
  3.2 0.1 fusion.5
  3.7 0.1 fusion.3
  5.2 12.3 %collective-permute-start.1 = (f32[28,96,2]{1,2,0:T(2,128)S(1)}, f32[28,96,2]{1,2,0:T(2,128)S(1)}, u32[]{:S(2)}, u32[]{:S(2)}) collective-permute-start(f32[28,96,2]{1,2,0:T(2,128)S(1)} %constant_dynamic-update-slice_fusion.22), channel_id=1, source_target_pairs={{8,0},{16,8},{24,16},{32,24},{40,32},{48,40},{56,48},{64,56},{72,6... | collective-permute-start | bytes 64520 | tf_op jit(solution)/shard_map/ppermute | solution.py:121
  18.7 1.9 %collective-permute-start = (f32[28,96,2]{1,2,0:T(2,128)S(1)}, f32[28,96,2]{1,2,0:T(2,128)S(1)}, u32[]{:S(2)}, u32[]{:S(2)}) collective-permute-start(f32[28,96,2]{1,2,0:T(2,128)S(1)} %constant_dynamic-update-slice_fusion), channel_id=1, source_target_pairs={{0,8},{8,16},{16,24},{24,32},{32,40},{40,48},{48,56},{56,64},{64,7... | collective-permute-start | bytes 64520 | tf_op jit(solution)/shard_map/ppermute | solution.py:120
  21.1 0.9 %add_convert_fusion.flag_ref = f32[2]{0:T(128)} fusion(pred[1]{0:T(512)(128)(4,1)} %constant.9.clone.1, pred[1]{0:T(512)(128)(4,1)} %bitcast), kind=kLoop, calls=%fused_computation.64 | loop fusion | flops 4 | bytes 10 | tf_op jit(solution)/shard_map/stack | solution.py:208
  22.2 0.5 copy.40
  22.7 14.1 %collective-permute-done = f32[28,96,2]{1,2,0:T(2,128)S(1)} collective-permute-done((f32[28,96,2]{1,2,0:T(2,128)S(1)}, f32[28,96,2]{1,2,0:T(2,128)S(1)}, u32[]{:S(2)}, u32[]{:S(2)}) %collective-permute-start) | collective-permute-done | bytes 21536 | tf_op jit(solution)/shard_map/ppermute | solution.py:120
  36.8 0.5 copy.28
  37.3 0.2 pad_maximum_fusion.1
  37.4 2.5 %collective-permute-start.3 = (f32[28,2,132]{2,1,0:T(2,128)S(1)}, f32[28,2,132]{2,1,0:T(2,128)S(1)}, u32[]{:S(2)}, u32[]{:S(2)}) collective-permute-start(f32[28,2,132]{2,1,0:T(2,128)S(1)} %pad_maximum_fusion.1), channel_id=1, source_target_pairs={{7,511},{15,503},{23,495},{31,487},{39,479},{47,471},{55,463},{63,... | collective-permute-start | bytes 88712 | tf_op jit(solution)/shard_map/ppermute | solution.py:128
  39.9 1.3 %collective-permute-start.2 = (f32[28,2,132]{2,1,0:T(2,128)S(1)}, f32[28,2,132]{2,1,0:T(2,128)S(1)}, u32[]{:S(2)}, u32[]{:S(2)}) collective-permute-start(f32[28,2,132]{2,1,0:T(2,128)S(1)} %pad_maximum_fusion.1), channel_id=1, source_target_pairs={{0,1},{1,2},{2,3},{3,4},{4,5},{5,6},{6,7},{8,9},{9,10},{10,11},{11... | collective-permute-start | bytes 88712 | tf_op jit(solution)/shard_map/ppermute | solution.py:137
  41.2 0.2 pad_maximum_fusion.3
  41.4 4.5 %collective-permute-start.4 = (f32[28,2,132]{2,1,0:T(2,128)S(1)}, f32[28,2,132]{2,1,0:T(2,128)S(1)}, u32[]{:S(2)}, u32[]{:S(2)}) collective-permute-start(f32[28,2,132]{2,1,0:T(2,128)S(1)} %pad_maximum_fusion.3), channel_id=1, source_target_pairs={{1,0},{2,1},{3,2},{4,3},{5,4},{6,5},{7,6},{9,8},{10,9},{11,10},{12... | collective-permute-start | bytes 88712 | tf_op jit(solution)/shard_map/ppermute | solution.py:138
  46.0 3.4 %pad_maximum_fusion.middle_ref = f32[28,96,256]{2,1,0:T(8,128)} fusion(f32[28,96,2]{2,1,0:T(8,128)S(1)} %copy.28, f32[28,96,2]{2,1,0:T(8,128)S(1)} %copy.40, f32[28,96,128]{2,1,0:T(8,128)} %copy-done.5, f32[256]{0:T(256)S(1)} %pad.16.clone), kind=kLoop, calls=%fused_computation | loop fusion | flops 2064384 | bytes 4172800 | tf_op jit(solution)/shard_map/concatenate | solution.py:197
  49.3 6.5 %collective-permute-done.3 = f32[28,2,132]{2,1,0:T(2,128)S(1)} collective-permute-done((f32[28,2,132]{2,1,0:T(2,128)S(1)}, f32[28,2,132]{2,1,0:T(2,128)S(1)}, u32[]{:S(2)}, u32[]{:S(2)}) %collective-permute-start.3) | collective-permute-done | bytes 29600 | tf_op jit(solution)/shard_map/ppermute | solution.py:128
  55.9 0.3 reverse.2
  56.2 0.1 slice.270
  56.4 0.3 reverse.3
  57.2 0.1 pad_maximum_fusion.4
  57.4 0.7 %concatenate.49.low_ref = f32[28,8,256]{2,1,0:T(8,128)} pad(f32[28,2,256]{2,1,0:T(2,128)S(1)} %get-tuple-element.55, f32[]{:T(128)} %constant.3.clone.1), padding=0_0x6_0x0_0 | pad | bytes 286724 | tf_op jit(solution)/shard_map/concatenate | solution.py:202
  58.1 0.7 %concatenate.57.high_ref = f32[28,8,256]{2,1,0:T(8,128)} pad(f32[28,2,256]{2,1,0:T(2,128)S(1)} %get-tuple-element.54, f32[]{:T(128)} %constant.3.clone.1), padding=0_0x0_6x0_0 | pad | bytes 286724 | tf_op jit(solution)/shard_map/concatenate | solution.py:205
  58.8 7.3 %shard_map.156 = (f32[4,96,128]{2,1,0:T(8,128)}, f32[4,96,128]{2,1,0:T(8,128)}, f32[4,96,128]{2,1,0:T(8,128)}, f32[4,96,128]{2,1,0:T(8,128)}) custom-call(f32[4]{0:T(128)} %height_ref.1, f32[2]{0:T(128)} %add_convert_fusion.flag_ref, f32[28,8,256]{2,1,0:T(8,128)} %concatenate.49.low_ref, f32[28,96,256]{2,1,0:T(8,128)} %pad_maximum_fusion.middle_ref, ...), custom_call_target="tpu_custom_call" | custom-call | tf_op jit(solution)/shard_map/pallas_call | solution.py:212
  (116 shorter events, 4.0 us)
Async XLA Ops:
  0.6 2.6 %copy-start.2 = (f32[4,96,128]{2,1,0:T(8,128)S(1)}, f32[4,96,128]{2,1,0:T(8,128)}, u32[]{:S(2)}) copy-start(f32[4,96,128]{2,1,0:T(8,128)} %param.14) | copy-start | bytes 589828
  0.6 2.9 %copy-start.3 = (f32[4,96,128]{2,1,0:T(8,128)S(1)}, f32[4,96,128]{2,1,0:T(8,128)}, u32[]{:S(2)}) copy-start(f32[4,96,128]{2,1,0:T(8,128)} %param.15) | copy-start | bytes 589828
  1.9 1.8 %copy-start.4 = (f32[4,96,128]{2,1,0:T(8,128)S(1)}, f32[4,96,128]{2,1,0:T(8,128)}, u32[]{:S(2)}) copy-start(f32[4,96,128]{2,1,0:T(8,128)} %param.16) | copy-start | bytes 589828
  3.2 0.8 %copy-start.7 = (s32[96,128]{1,0:T(8,128)S(1)}, s32[96,128]{1,0:T(8,128)}, u32[]{:S(2)}) copy-start(s32[96,128]{1,0:T(8,128)} %param.18) | copy-start | bytes 147460
  3.4 0.8 %copy-start.8 = (f32[96,128]{1,0:T(8,128)S(1)}, f32[96,128]{1,0:T(8,128)}, u32[]{:S(2)}) copy-start(f32[96,128]{1,0:T(8,128)} %param.19) | copy-start | bytes 147460
  3.4 1.0 %copy-start.9 = (f32[96,128]{1,0:T(8,128)S(1)}, f32[96,128]{1,0:T(8,128)}, u32[]{:S(2)}) copy-start(f32[96,128]{1,0:T(8,128)} %param.20) | copy-start | bytes 147460
  3.5 1.0 %copy-start.10 = (f32[96,128]{1,0:T(8,128)S(1)}, f32[96,128]{1,0:T(8,128)}, u32[]{:S(2)}) copy-start(f32[96,128]{1,0:T(8,128)} %param.21) | copy-start | bytes 147460
  3.5 1.2 %copy-start.11 = (f32[96,128]{1,0:T(8,128)S(1)}, f32[96,128]{1,0:T(8,128)}, u32[]{:S(2)}) copy-start(f32[96,128]{1,0:T(8,128)} %param.22) | copy-start | bytes 147460
  3.6 1.2 %copy-start.6 = (f32[3,96,128]{2,1,0:T(8,128)S(1)}, f32[3,96,128]{2,1,0:T(8,128)}, u32[]{:S(2)}) copy-start(f32[3,96,128]{2,1,0:T(8,128)} %param.23) | copy-start | bytes 442372
  4.5 16.0 %copy-start = (s32[4,96,128]{2,1,0:T(8,128)S(1)}, s32[4,96,128]{2,1,0:T(8,128)}, u32[]{:S(2)}) copy-start(s32[4,96,128]{2,1,0:T(8,128)} %param.17) | copy-start | bytes 589828
  4.5 16.1 %copy-start.1 = (f32[4,96,128]{2,1,0:T(8,128)S(1)}, f32[4,96,128]{2,1,0:T(8,128)}, u32[]{:S(2)}) copy-start(f32[4,96,128]{2,1,0:T(8,128)} %param.13) | copy-start | bytes 589828
  5.2 17.0 %collective-permute-start.1 = (f32[28,96,2]{1,2,0:T(2,128)S(1)}, f32[28,96,2]{1,2,0:T(2,128)S(1)}, u32[]{:S(2)}, u32[]{:S(2)}) collective-permute-start(f32[28,96,2]{1,2,0:T(2,128)S(1)} %constant_dynamic-update-slice_fusion.22), channel_id=1, source_target_pairs={{8,0},{16,8},{24,16},{32,24},{40,32},{48,40},{56,48},{64,56},{72,6... | collective-permute-start | bytes 64520 | tf_op jit(solution)/shard_map/ppermute | solution.py:121
  18.7 18.1 %collective-permute-start = (f32[28,96,2]{1,2,0:T(2,128)S(1)}, f32[28,96,2]{1,2,0:T(2,128)S(1)}, u32[]{:S(2)}, u32[]{:S(2)}) collective-permute-start(f32[28,96,2]{1,2,0:T(2,128)S(1)} %constant_dynamic-update-slice_fusion), channel_id=1, source_target_pairs={{0,8},{8,16},{16,24},{24,32},{32,40},{40,48},{48,56},{56,64},{64,7... | collective-permute-start | bytes 64520 | tf_op jit(solution)/shard_map/ppermute | solution.py:120
  20.7 1.2 %copy-start.12 = (f32[5]{0:T(128)S(1)}, f32[5]{0:T(128)}, u32[]{:S(2)}) copy-start(f32[5]{0:T(128)} %constant.6.clone) | copy-start | bytes 64
  20.9 1.3 %copy-start.5 = (f32[28,96,128]{2,1,0:T(8,128)}, f32[28,96,128]{2,1,0:T(8,128)S(1)}, u32[]{:S(2)}) copy-start(f32[28,96,128]{2,1,0:T(8,128)S(1)} %constant_dynamic-update-slice_fusion.33) | copy-start | bytes 4128772
  37.4 18.4 %collective-permute-start.3 = (f32[28,2,132]{2,1,0:T(2,128)S(1)}, f32[28,2,132]{2,1,0:T(2,128)S(1)}, u32[]{:S(2)}, u32[]{:S(2)}) collective-permute-start(f32[28,2,132]{2,1,0:T(2,128)S(1)} %pad_maximum_fusion.1), channel_id=1, source_target_pairs={{7,511},{15,503},{23,495},{31,487},{39,479},{47,471},{55,463},{63,... | collective-permute-start | bytes 88712 | tf_op jit(solution)/shard_map/ppermute | solution.py:128
  39.9 17.1 %collective-permute-start.2 = (f32[28,2,132]{2,1,0:T(2,128)S(1)}, f32[28,2,132]{2,1,0:T(2,128)S(1)}, u32[]{:S(2)}, u32[]{:S(2)}) collective-permute-start(f32[28,2,132]{2,1,0:T(2,128)S(1)} %pad_maximum_fusion.1), channel_id=1, source_target_pairs={{0,1},{1,2},{2,3},{3,4},{4,5},{5,6},{6,7},{8,9},{9,10},{10,11},{11... | collective-permute-start | bytes 88712 | tf_op jit(solution)/shard_map/ppermute | solution.py:137
  41.4 15.4 %collective-permute-start.4 = (f32[28,2,132]{2,1,0:T(2,128)S(1)}, f32[28,2,132]{2,1,0:T(2,128)S(1)}, u32[]{:S(2)}, u32[]{:S(2)}) collective-permute-start(f32[28,2,132]{2,1,0:T(2,128)S(1)} %pad_maximum_fusion.3), channel_id=1, source_target_pairs={{1,0},{2,1},{3,2},{4,3},{5,4},{6,5},{7,6},{9,8},{10,9},{11,10},{12... | collective-permute-start | bytes 88712 | tf_op jit(solution)/shard_map/ppermute | solution.py:138

commit v13 on v12

--- a/solution.py
+++ b/solution.py
@@ -266,7 +266,7 @@
     half_merid = 0.5 / meridional_spacing
     at_bottom = [(floor_index == float(k)).astype(jnp.float32) for k in range(levels)]
 
-    def one_step(state):
+    def one_step(state, win):
         wet = state[4]
         fields = state[:4]
         pressure_column = []
@@ -275,53 +275,62 @@
             mass = (CONTRACTION * fields[1][k] - EXPANSION * fields[0][k]) * heights[k]
             running = mass if running is None else running + mass
             pressure_column.append(running - 0.5 * mass)
+        wet_c = [win(x) for x in wet]
+        fields_c = [[win(x) for x in channel] for channel in fields]
         fluxes = []
         for c in range(4):
             fluxes.append(
                 [
-                    diapycnal[k] * (wet[k + 1] * wet[k]) * (fields[c][k + 1] - fields[c][k])
+                    win(diapycnal[k])
+                    * (wet_c[k + 1] * wet_c[k])
+                    * (fields_c[c][k + 1] - fields_c[c][k])
                     for k in range(levels - 1)
                 ]
             )
+        inv_zonal_sq_c, inv_merid_sq_c = win(inv_zonal_sq), win(inv_merid_sq)
+        half_zonal_c, half_merid_c = win(half_zonal), win(half_merid)
+        eddy_c, rotation_c = win(eddy), win(rotation)
         new_state = [[None] * levels for _ in range(5)]
         for k in range(levels):
-            w = wet[k]
-            w_e, w_w, w_n, w_s = east_of(w), west_of(w), north_of(w), south_of(w)
-            weight_east, weight_west = w * w_e, w * w_w
-            weight_north, weight_south = w * w_n, w * w_s
-            u = fields[2][k]
-            v = fields[3][k]
+            w = wet_c[k]
+            weight_east, weight_west = w * win(east_of(wet[k])), w * win(west_of(wet[k]))
+            weight_north, weight_south = w * win(north_of(wet[k])), w * win(south_of(wet[k]))
+            u = fields_c[2][k]
+            v = fields_c[3][k]
             p = pressure_column[k]
-            gradient_x = -(east_of(p) - west_of(p)) * half_zonal
-            gradient_y = -(north_of(p) - south_of(p)) * half_merid
+            gradient_x = -(win(east_of(p)) - win(west_of(p))) * half_zonal_c
+            gradient_y = -(win(north_of(p)) - win(south_of(p))) * half_merid_c
+            bottom = win(at_bottom[k])
             for c in range(4):
-                f = fields[c][k]
-                f_e, f_w, f_n, f_s = east_of(f), west_of(f), north_of(f), south_of(f)
-                diffusion = eddy * (
-                    (weight_east * (f_e - f) + weight_west * (f_w - f)) * inv_zonal_sq
-                    + (weight_north * (f_n - f) + weight_south * (f_s - f)) * inv_merid_sq
+                full = fields[c][k]
+                f = fields_c[c][k]
+                f_e, f_w = win(east_of(full)), win(west_of(full))
+                f_n, f_s = win(north_of(full)), win(south_of(full))
+                diffusion = eddy_c * (
+                    (weight_east * (f_e - f) + weight_west * (f_w - f)) * inv_zonal_sq_c
+                    + (weight_north * (f_n - f) + weight_south * (f_s - f)) * inv_merid_sq_c
                 )
-                advection = -(u * (f_e - f_w) * half_zonal + v * (f_n - f_s) * half_merid)
+                advection = -(u * (f_e - f_w) * half_zonal_c + v * (f_n - f_s) * half_merid_c)
                 below = fluxes[c][k] if k < levels - 1 else 0.0
                 above = fluxes[c][k - 1] if k > 0 else 0.0
                 mixing = (below - above) * inv_height_sq[k]
                 tendency = advection + diffusion + mixing
                 if c == 2:
-                    tendency = tendency + rotation * v + gradient_x - BOTTOM_DRAG * at_bottom[k] * u
+                    tendency = tendency + rotation_c * v + gradient_x - BOTTOM_DRAG * bottom * u
                 if c == 3:
-                    tendency = tendency - rotation * u + gradient_y - BOTTOM_DRAG * at_bottom[k] * v
+                    tendency = tendency - rotation_c * u + gradient_y - BOTTOM_DRAG * bottom * v
                 new_state[c][k] = w * (f + TIME_STEP * tendency)
             new_state[4][k] = w
         return new_state
 
     state0 = [[plane(c * levels + k) for k in range(levels)] for c in range(5)]
-    state1 = one_step(state0)
+    state1 = one_step(state0, lambda x: x)
     clear = jnp.logical_and(sub == ROW_OFFSET - 1, flag_ref[0] > 0.5)
     state1 = [[jnp.where(clear, 0.0, x) for x in channel] for channel in state1]
-    state2 = one_step(state1)
+    state2 = one_step(state1, lambda x: x[ROW_OFFSET : ROW_OFFSET + rows, :cols])
     for c in range(4):
         for k in range(levels):
-            out_refs[c][k] = state2[c][k][ROW_OFFSET : ROW_OFFSET + rows, :cols]
+            out_refs[c][k] = state2[c][k]
 
 
 def solution(mesh):

time: 66.4 us -> 66.4 us (level)
  no operation moved by 1% of the time
where the time goes in v13:
time: 66.4 us; the launch traced here: 66.1 us
  starting transfers between devices  22.6 us (34%)
  waiting for transfers between devices  20.6 us (31%)
  local copies, waits for them, and re-layouts  9.23 us (14%)
  Pallas kernels  7.29 us (11%)
  other arithmetic  5.21 us (8%)
  between operations  1.19 us (2%)
    ppermute x1, waiting for transfers between devices, exchange(): west = lax.ppermute(take(every, slice(-h, None)), 'lon', east_pairs)  14.1 us
    ppermute x1, starting transfers between devices, exchange(): east = lax.ppermute(take(every, slice(0, h)), 'lon', west_pairs)  12.3 us
    pallas_call x1, Pallas kernels, shards(): pl.pallas_call(two_steps_kernel, out_shape=[field_shape] * (channels - 1)...  7.29 us
    ppermute x1, waiting for transfers between devices, exchange(): lax.ppermute(top_band, ('lon', 'lat'), fold_pairs(lon_count, lat_count, l...  6.53 us
    ppermute x1, starting transfers between devices, exchange(): north = lax.ppermute(bottom_band, 'lat', south_pairs)  4.55 us
    concatenate x1, other arithmetic, shards(): jnp.concatenate([block, east, jnp.zeros((block.shape[0], rows, gap), jnp....  3.39 us
    unnamed x70, local copies, waits for them, and re-layouts  3.06 us
    ppermute x1, starting transfers between devices, exchange(): lax.ppermute(top_band, ('lon', 'lat'), fold_pairs(lon_count, lat_count, l...  2.49 us
  transfers between devices with their start and end apart: 5, of which 2 were waited for; matrix products, arithmetic and copies ran while one was open for 12% of the time, Pallas kernels for 0%

profile of v13, /device:TPU:224, one launch (start us, length us, event | category | flops | bytes accessed | tf_op | source)
XLA Modules:
  0.0 66.1 jit_solution(11231578539703559020)
XLA Ops:
  0.7 1.2 %fusion.7 = (f32[4,96,2]{2,1,0:T(8,128)S(1)}, f32[4,96,2]{2,1,0:T(8,128)S(1)}) fusion(f32[4,96,128]{2,1,0:T(8,128)} %param.13), kind=kLoop, calls=%fused_computation.71 | loop fusion | bytes 12288 | tf_op jit(solution)/shard_map/slice | solution.py:169
  1.9 1.2 %fusion.6 = (s32[4,96,2]{2,1,0:T(8,128)S(1)}, s32[4,96,2]{2,1,0:T(8,128)S(1)}) fusion(s32[4,96,128]{2,1,0:T(8,128)} %param.17), kind=kLoop, calls=%fused_computation.70 | loop fusion | bytes 12288 | tf_op jit(solution)/shard_map/slice | solution.py:168
  3.2 0.1 fusion.5
  3.7 0.1 fusion.3
  5.2 12.3 %collective-permute-start.1 = (f32[28,96,2]{1,2,0:T(2,128)S(1)}, f32[28,96,2]{1,2,0:T(2,128)S(1)}, u32[]{:S(2)}, u32[]{:S(2)}) collective-permute-start(f32[28,96,2]{1,2,0:T(2,128)S(1)} %constant_dynamic-update-slice_fusion.22), channel_id=1, source_target_pairs={{8,0},{16,8},{24,16},{32,24},{40,32},{48,40},{56,48},{64,56},{72,6... | collective-permute-start | bytes 64520 | tf_op jit(solution)/shard_map/ppermute | solution.py:121
  18.7 1.9 %collective-permute-start = (f32[28,96,2]{1,2,0:T(2,128)S(1)}, f32[28,96,2]{1,2,0:T(2,128)S(1)}, u32[]{:S(2)}, u32[]{:S(2)}) collective-permute-start(f32[28,96,2]{1,2,0:T(2,128)S(1)} %constant_dynamic-update-slice_fusion), channel_id=1, source_target_pairs={{0,8},{8,16},{16,24},{24,32},{32,40},{40,48},{48,56},{56,64},{64,7... | collective-permute-start | bytes 64520 | tf_op jit(solution)/shard_map/ppermute | solution.py:120
  21.1 0.9 %add_convert_fusion.flag_ref = f32[2]{0:T(128)} fusion(pred[1]{0:T(512)(128)(4,1)} %constant.9.clone.1, pred[1]{0:T(512)(128)(4,1)} %bitcast), kind=kLoop, calls=%fused_computation.64 | loop fusion | flops 4 | bytes 10 | tf_op jit(solution)/shard_map/stack | solution.py:208
  22.2 0.5 copy.40
  22.7 14.1 %collective-permute-done = f32[28,96,2]{1,2,0:T(2,128)S(1)} collective-permute-done((f32[28,96,2]{1,2,0:T(2,128)S(1)}, f32[28,96,2]{1,2,0:T(2,128)S(1)}, u32[]{:S(2)}, u32[]{:S(2)}) %collective-permute-start) | collective-permute-done | bytes 21536 | tf_op jit(solution)/shard_map/ppermute | solution.py:120
  36.8 0.5 copy.28
  37.3 0.2 pad_maximum_fusion.1
  37.4 2.5 %collective-permute-start.3 = (f32[28,2,132]{2,1,0:T(2,128)S(1)}, f32[28,2,132]{2,1,0:T(2,128)S(1)}, u32[]{:S(2)}, u32[]{:S(2)}) collective-permute-start(f32[28,2,132]{2,1,0:T(2,128)S(1)} %pad_maximum_fusion.1), channel_id=1, source_target_pairs={{7,511},{15,503},{23,495},{31,487},{39,479},{47,471},{55,463},{63,... | collective-permute-start | bytes 88712 | tf_op jit(solution)/shard_map/ppermute | solution.py:128
  39.9 1.3 %collective-permute-start.2 = (f32[28,2,132]{2,1,0:T(2,128)S(1)}, f32[28,2,132]{2,1,0:T(2,128)S(1)}, u32[]{:S(2)}, u32[]{:S(2)}) collective-permute-start(f32[28,2,132]{2,1,0:T(2,128)S(1)} %pad_maximum_fusion.1), channel_id=1, source_target_pairs={{0,1},{1,2},{2,3},{3,4},{4,5},{5,6},{6,7},{8,9},{9,10},{10,11},{11... | collective-permute-start | bytes 88712 | tf_op jit(solution)/shard_map/ppermute | solution.py:137
  41.2 0.2 pad_maximum_fusion.3
  41.4 4.5 %collective-permute-start.4 = (f32[28,2,132]{2,1,0:T(2,128)S(1)}, f32[28,2,132]{2,1,0:T(2,128)S(1)}, u32[]{:S(2)}, u32[]{:S(2)}) collective-permute-start(f32[28,2,132]{2,1,0:T(2,128)S(1)} %pad_maximum_fusion.3), channel_id=1, source_target_pairs={{1,0},{2,1},{3,2},{4,3},{5,4},{6,5},{7,6},{9,8},{10,9},{11,10},{12... | collective-permute-start | bytes 88712 | tf_op jit(solution)/shard_map/ppermute | solution.py:138
  46.0 3.4 %pad_maximum_fusion.middle_ref = f32[28,96,256]{2,1,0:T(8,128)} fusion(f32[28,96,2]{2,1,0:T(8,128)S(1)} %copy.28, f32[28,96,2]{2,1,0:T(8,128)S(1)} %copy.40, f32[28,96,128]{2,1,0:T(8,128)} %copy-done.5, f32[256]{0:T(256)S(1)} %pad.16.clone), kind=kLoop, calls=%fused_computation | loop fusion | flops 2064384 | bytes 4172800 | tf_op jit(solution)/shard_map/concatenate | solution.py:197
  49.3 6.5 %collective-permute-done.3 = f32[28,2,132]{2,1,0:T(2,128)S(1)} collective-permute-done((f32[28,2,132]{2,1,0:T(2,128)S(1)}, f32[28,2,132]{2,1,0:T(2,128)S(1)}, u32[]{:S(2)}, u32[]{:S(2)}) %collective-permute-start.3) | collective-permute-done | bytes 29600 | tf_op jit(solution)/shard_map/ppermute | solution.py:128
  55.9 0.3 reverse.2
  56.2 0.1 slice.270
  56.4 0.3 reverse.3
  57.2 0.1 pad_maximum_fusion.4
  57.4 0.7 %concatenate.49.low_ref = f32[28,8,256]{2,1,0:T(8,128)} pad(f32[28,2,256]{2,1,0:T(2,128)S(1)} %get-tuple-element.55, f32[]{:T(128)} %constant.3.clone.1), padding=0_0x6_0x0_0 | pad | bytes 286724 | tf_op jit(solution)/shard_map/concatenate | solution.py:202
  58.1 0.7 %concatenate.57.high_ref = f32[28,8,256]{2,1,0:T(8,128)} pad(f32[28,2,256]{2,1,0:T(2,128)S(1)} %get-tuple-element.54, f32[]{:T(128)} %constant.3.clone.1), padding=0_0x0_6x0_0 | pad | bytes 286724 | tf_op jit(solution)/shard_map/concatenate | solution.py:205
  58.8 7.3 %shard_map.156 = (f32[4,96,128]{2,1,0:T(8,128)}, f32[4,96,128]{2,1,0:T(8,128)}, f32[4,96,128]{2,1,0:T(8,128)}, f32[4,96,128]{2,1,0:T(8,128)}) custom-call(f32[4]{0:T(128)} %height_ref.1, f32[2]{0:T(128)} %add_convert_fusion.flag_ref, f32[28,8,256]{2,1,0:T(8,128)} %concatenate.49.low_ref, f32[28,96,256]{2,1,0:T(8,128)} %pad_maximum_fusion.middle_ref, ...), custom_call_target="tpu_custom_call" | custom-call | tf_op jit(solution)/shard_map/pallas_call | solution.py:212
  (116 shorter events, 4.0 us)
Async XLA Ops:
  0.6 2.6 %copy-start.2 = (f32[4,96,128]{2,1,0:T(8,128)S(1)}, f32[4,96,128]{2,1,0:T(8,128)}, u32[]{:S(2)}) copy-start(f32[4,96,128]{2,1,0:T(8,128)} %param.14) | copy-start | bytes 589828
  0.6 2.9 %copy-start.3 = (f32[4,96,128]{2,1,0:T(8,128)S(1)}, f32[4,96,128]{2,1,0:T(8,128)}, u32[]{:S(2)}) copy-start(f32[4,96,128]{2,1,0:T(8,128)} %param.15) | copy-start | bytes 589828
  1.9 1.8 %copy-start.4 = (f32[4,96,128]{2,1,0:T(8,128)S(1)}, f32[4,96,128]{2,1,0:T(8,128)}, u32[]{:S(2)}) copy-start(f32[4,96,128]{2,1,0:T(8,128)} %param.16) | copy-start | bytes 589828
  3.2 0.8 %copy-start.7 = (s32[96,128]{1,0:T(8,128)S(1)}, s32[96,128]{1,0:T(8,128)}, u32[]{:S(2)}) copy-start(s32[96,128]{1,0:T(8,128)} %param.18) | copy-start | bytes 147460
  3.4 0.8 %copy-start.8 = (f32[96,128]{1,0:T(8,128)S(1)}, f32[96,128]{1,0:T(8,128)}, u32[]{:S(2)}) copy-start(f32[96,128]{1,0:T(8,128)} %param.19) | copy-start | bytes 147460
  3.4 1.0 %copy-start.9 = (f32[96,128]{1,0:T(8,128)S(1)}, f32[96,128]{1,0:T(8,128)}, u32[]{:S(2)}) copy-start(f32[96,128]{1,0:T(8,128)} %param.20) | copy-start | bytes 147460
  3.5 1.0 %copy-start.10 = (f32[96,128]{1,0:T(8,128)S(1)}, f32[96,128]{1,0:T(8,128)}, u32[]{:S(2)}) copy-start(f32[96,128]{1,0:T(8,128)} %param.21) | copy-start | bytes 147460
  3.5 1.2 %copy-start.11 = (f32[96,128]{1,0:T(8,128)S(1)}, f32[96,128]{1,0:T(8,128)}, u32[]{:S(2)}) copy-start(f32[96,128]{1,0:T(8,128)} %param.22) | copy-start | bytes 147460
  3.6 1.2 %copy-start.6 = (f32[3,96,128]{2,1,0:T(8,128)S(1)}, f32[3,96,128]{2,1,0:T(8,128)}, u32[]{:S(2)}) copy-start(f32[3,96,128]{2,1,0:T(8,128)} %param.23) | copy-start | bytes 442372
  4.5 16.0 %copy-start = (s32[4,96,128]{2,1,0:T(8,128)S(1)}, s32[4,96,128]{2,1,0:T(8,128)}, u32[]{:S(2)}) copy-start(s32[4,96,128]{2,1,0:T(8,128)} %param.17) | copy-start | bytes 589828
  4.5 16.1 %copy-start.1 = (f32[4,96,128]{2,1,0:T(8,128)S(1)}, f32[4,96,128]{2,1,0:T(8,128)}, u32[]{:S(2)}) copy-start(f32[4,96,128]{2,1,0:T(8,128)} %param.13) | copy-start | bytes 589828
  5.2 17.0 %collective-permute-start.1 = (f32[28,96,2]{1,2,0:T(2,128)S(1)}, f32[28,96,2]{1,2,0:T(2,128)S(1)}, u32[]{:S(2)}, u32[]{:S(2)}) collective-permute-start(f32[28,96,2]{1,2,0:T(2,128)S(1)} %constant_dynamic-update-slice_fusion.22), channel_id=1, source_target_pairs={{8,0},{16,8},{24,16},{32,24},{40,32},{48,40},{56,48},{64,56},{72,6... | collective-permute-start | bytes 64520 | tf_op jit(solution)/shard_map/ppermute | solution.py:121
  18.7 18.1 %collective-permute-start = (f32[28,96,2]{1,2,0:T(2,128)S(1)}, f32[28,96,2]{1,2,0:T(2,128)S(1)}, u32[]{:S(2)}, u32[]{:S(2)}) collective-permute-start(f32[28,96,2]{1,2,0:T(2,128)S(1)} %constant_dynamic-update-slice_fusion), channel_id=1, source_target_pairs={{0,8},{8,16},{16,24},{24,32},{32,40},{40,48},{48,56},{56,64},{64,7... | collective-permute-start | bytes 64520 | tf_op jit(solution)/shard_map/ppermute | solution.py:120
  20.7 1.2 %copy-start.12 = (f32[5]{0:T(128)S(1)}, f32[5]{0:T(128)}, u32[]{:S(2)}) copy-start(f32[5]{0:T(128)} %constant.6.clone) | copy-start | bytes 64
  20.9 1.3 %copy-start.5 = (f32[28,96,128]{2,1,0:T(8,128)}, f32[28,96,128]{2,1,0:T(8,128)S(1)}, u32[]{:S(2)}) copy-start(f32[28,96,128]{2,1,0:T(8,128)S(1)} %constant_dynamic-update-slice_fusion.33) | copy-start | bytes 4128772
  37.4 18.4 %collective-permute-start.3 = (f32[28,2,132]{2,1,0:T(2,128)S(1)}, f32[28,2,132]{2,1,0:T(2,128)S(1)}, u32[]{:S(2)}, u32[]{:S(2)}) collective-permute-start(f32[28,2,132]{2,1,0:T(2,128)S(1)} %pad_maximum_fusion.1), channel_id=1, source_target_pairs={{7,511},{15,503},{23,495},{31,487},{39,479},{47,471},{55,463},{63,... | collective-permute-start | bytes 88712 | tf_op jit(solution)/shard_map/ppermute | solution.py:128
  39.9 17.1 %collective-permute-start.2 = (f32[28,2,132]{2,1,0:T(2,128)S(1)}, f32[28,2,132]{2,1,0:T(2,128)S(1)}, u32[]{:S(2)}, u32[]{:S(2)}) collective-permute-start(f32[28,2,132]{2,1,0:T(2,128)S(1)} %pad_maximum_fusion.1), channel_id=1, source_target_pairs={{0,1},{1,2},{2,3},{3,4},{4,5},{5,6},{6,7},{8,9},{9,10},{10,11},{11... | collective-permute-start | bytes 88712 | tf_op jit(solution)/shard_map/ppermute | solution.py:137
  41.4 15.4 %collective-permute-start.4 = (f32[28,2,132]{2,1,0:T(2,128)S(1)}, f32[28,2,132]{2,1,0:T(2,128)S(1)}, u32[]{:S(2)}, u32[]{:S(2)}) collective-permute-start(f32[28,2,132]{2,1,0:T(2,128)S(1)} %pad_maximum_fusion.3), channel_id=1, source_target_pairs={{1,0},{2,1},{3,2},{4,3},{5,4},{6,5},{7,6},{9,8},{10,9},{11,10},{12... | collective-permute-start | bytes 88712 | tf_op jit(solution)/shard_map/ppermute | solution.py:138

commit v14 on v13

--- a/solution.py
+++ b/solution.py
@@ -109,16 +109,32 @@
     return [(i * lat_count + top, (target_of(i) % lon_count) * lat_count + top) for i in range(lon_count)]
 
 
+def swap_edges(axis, size, low_edge, high_edge, periodic):
+    if size % 2:
+        up = [(i, (i + 1) % size) for i in range(size if periodic else size - 1)]
+        down = [(j, i) for i, j in up]
+        return lax.ppermute(high_edge, axis, up), lax.ppermute(low_edge, axis, down)
+    even = lax.axis_index(axis) % 2 == 0
+    inner = []
+    for i in range(0, size, 2):
+        inner += [(i, i + 1), (i + 1, i)]
+    outer = []
+    for i in range(1, size if periodic else size - 1, 2):
+        outer += [(i, (i + 1) % size), ((i + 1) % size, i)]
+    from_inner = lax.ppermute(jnp.where(even, high_edge, low_edge), axis, inner)
+    from_outer = lax.ppermute(jnp.where(even, low_edge, high_edge), axis, outer)
+    from_lower = jnp.where(even, from_outer, from_inner)
+    from_upper = jnp.where(even, from_inner, from_outer)
+    return from_lower, from_upper
+
+
 def exchange(take, sign):
     lon_count = lax.axis_size("lon")
     lat_count = lax.axis_size("lat")
     h = HALO
     every = slice(None)
 
-    east_pairs = [(i, (i + 1) % lon_count) for i in range(lon_count)]
-    west_pairs = [(j, i) for i, j in east_pairs]
-    west = lax.ppermute(take(every, slice(-h, None)), "lon", east_pairs)
-    east = lax.ppermute(take(every, slice(0, h)), "lon", west_pairs)
+    west, east = swap_edges("lon", lon_count, take(every, slice(0, h)), take(every, slice(-h, None)), True)
 
     rows_hi = take(slice(-h, None), every)
     rows_lo = take(slice(0, h), every)
@@ -132,10 +148,7 @@
     folded = jnp.concatenate([mirrored[:, 1:2, :], mirrored[:, 0:1, :]], axis=1)
     folded = folded * sign[:, None, None]
 
-    north_pairs = [(j, j + 1) for j in range(lat_count - 1)]
-    south_pairs = [(j, i) for i, j in north_pairs]
-    south = lax.ppermute(top_band, "lat", north_pairs)
-    north = lax.ppermute(bottom_band, "lat", south_pairs)
+    south, north = swap_edges("lat", lat_count, bottom_band, top_band, False)
     is_top = lax.axis_index("lat") == lat_count - 1
     north = jnp.where(is_top, folded, north)
     return west, east, south, north

time: 66.4 us -> 76 us (1.14)
  waiting for transfers between devices: 20.6 us -> 2.89 us
  local copies, waits for them, and re-layouts: 9.23 us -> 24.4 us
  starting transfers between devices: 22.6 us -> 29.2 us
  other arithmetic: 5.21 us -> 10.3 us
    ppermute x4, waiting for transfers between devices: 14.1 us -> 0.91 us  [the longest x2 0.9 us: swap_edges(): from_outer = lax.ppermute(jnp.where(even, low_edge, high_edge), axis, outer)]
    ppermute x1, starting transfers between devices: 2.49 us -> 12.3 us  [exchange(): lax.ppermute(top_band, ('lon', 'lat'), fold_pairs(lon_count, lat_count, l...]
    unnamed x70 -> x96, local copies, waits for them, and re-layouts: 3.06 us -> 7.72 us
    ppermute x1, waiting for transfers between devices: 6.53 us -> 1.98 us  [exchange(): lax.ppermute(top_band, ('lon', 'lat'), fold_pairs(lon_count, lat_count, l...]
    select_n x0 -> x2, local copies, waits for them, and re-layouts: none -> 3.48 us  [the longest x1 2.43 us: swap_edges(): from_outer = lax.ppermute(jnp.where(even, low_edge, high_edge), axis, outer)]
    concatenate x4 -> x6, local copies, waits for them, and re-layouts: 0.04 us -> 3.42 us  [take(): return jnp.concatenate(parts, axis=0)]
    select_n x0 -> x4, other arithmetic: none -> 3.34 us  [the longest x2 2.86 us: swap_edges(): from_outer = lax.ppermute(jnp.where(even, low_edge, high_edge), axis, outer)]
    ppermute x4, starting transfers between devices: 20.1 us -> 16.9 us  [the longest x2 13 us: swap_edges(): from_outer = lax.ppermute(jnp.where(even, low_edge, high_edge), axis, outer)]
  transfers between devices with their start and end apart: 5 -> 5, of which waited for: 2 -> 2; matrix products, arithmetic and copies ran while one was open for 12% -> 9% of each run, Pallas kernels for 0% -> 0%
where the time goes in v14:
time: 76 us; the launch traced here: 75.4 us
  starting transfers between devices  29.2 us (38%)
  local copies, waits for them, and re-layouts  24.4 us (32%)
  other arithmetic  10.3 us (14%)
  Pallas kernels  7.29 us (10%)
  waiting for transfers between devices  2.89 us (4%)
  between operations  1.28 us (2%)
    ppermute x2, starting transfers between devices, swap_edges(): from_outer = lax.ppermute(jnp.where(even, low_edge, high_edge), axis, outer)  13 us
    ppermute x1, starting transfers between devices, exchange(): lax.ppermute(top_band, ('lon', 'lat'), fold_pairs(lon_count, lat_count, l...  12.3 us
    unnamed x96, local copies, waits for them, and re-layouts  7.72 us
    pallas_call x1, Pallas kernels, shards(): pl.pallas_call(two_steps_kernel, out_shape=[field_shape] * (channels - 1)...  7.29 us
    ppermute x2, starting transfers between devices, swap_edges(): from_inner = lax.ppermute(jnp.where(even, high_edge, low_edge), axis, inner)  3.96 us
    concatenate x6, local copies, waits for them, and re-layouts, take(): return jnp.concatenate(parts, axis=0)  3.42 us
    unnamed x22, other arithmetic  3.25 us
    select_n x2, other arithmetic, swap_edges(): from_outer = lax.ppermute(jnp.where(even, low_edge, high_edge), axis, outer)  2.86 us
  transfers between devices with their start and end apart: 5, of which 2 were waited for; matrix products, arithmetic and copies ran while one was open for 9% of the time, Pallas kernels for 0%

profile of v14, /device:TPU:224, one launch (start us, length us, event | category | flops | bytes accessed | tf_op | source)
XLA Modules:
  0.0 75.4 jit_solution(5067322388599786960)
XLA Ops:
  0.7 1.2 %fusion.6 = (s32[4,96,2]{2,1,0:T(8,128)S(1)}, s32[4,96,2]{2,1,0:T(8,128)S(1)}) fusion(s32[4,96,128]{2,1,0:T(8,128)} %param.17), kind=kLoop, calls=%fused_computation.77 | loop fusion | bytes 12288 | tf_op jit(solution)/shard_map/slice | solution.py:181
  2.0 1.2 %fusion.7 = (f32[4,96,2]{2,1,0:T(8,128)S(1)}, f32[4,96,2]{2,1,0:T(8,128)S(1)}) fusion(f32[4,96,128]{2,1,0:T(8,128)} %param.13), kind=kLoop, calls=%fused_computation.78 | loop fusion | bytes 12288 | tf_op jit(solution)/shard_map/slice | solution.py:182
  7.7 0.6 fusion.13
  8.4 0.6 fusion.12
  14.2 1.2 %copy.40 = f32[28,96,2]{2,1,0:T(8,128)S(1)} copy(f32[28,96,2]{1,2,0:T(2,128)} %constant_dynamic-update-slice_fusion.11) | data formatting | bytes 43008 | tf_op jit(solution)/shard_map/concatenate | solution.py:185
  16.2 0.9 %copy.56 = f32[96,2]{0,1:T(2,128)S(1)} copy(f32[96,2]{1,0:T(8,128)} %get-tuple-element.56) | data formatting | bytes 1536
  17.4 1.6 %copy.39 = f32[28,96,2]{2,1,0:T(8,128)} copy(f32[28,96,2]{1,2,0:T(2,128)S(1)} %constant_dynamic-update-slice_fusion) | data formatting | bytes 43008 | tf_op jit(solution)/shard_map/concatenate | solution.py:185
  19.0 2.7 %broadcast_select_fusion.3 = (f32[28,96,2]{2,1,0:T(8,128)}, f32[28,96,2]{2,1,0:T(8,128)S(1)}) fusion(f32[28,96,2]{2,1,0:T(8,128)} %copy.39, f32[28,96,2]{2,1,0:T(8,128)S(1)} %copy.40, pred[]{:T(512)S(6)} %eq.17), kind=kLoop, calls=%fused_computation.4 | loop fusion | flops 10752 | bytes 86017 | tf_op jit(solution)/shard_map/jit(_where)/select_n | solution.py:125
  21.7 2.4 %copy.41 = f32[28,96,2]{1,2,0:T(2,128)} copy(f32[28,96,2]{2,1,0:T(8,128)} %get-tuple-element.8) | data formatting | bytes 43008 | tf_op jit(solution)/shard_map/jit(_where)/select_n | solution.py:125
  24.2 12.3 %collective-permute-start = (f32[28,96,2]{1,2,0:T(2,128)}, f32[28,96,2]{1,2,0:T(2,128)}, u32[]{:S(2)}, u32[]{:S(2)}) collective-permute-start(f32[28,96,2]{1,2,0:T(2,128)} %copy.41), channel_id=1, source_target_pairs={{8,16},{16,8},{24,32},{32,24},{40,48},{48,40},{56,64},{64,56},{72,... | collective-permute-start | bytes 64520 | tf_op jit(solution)/shard_map/ppermute | solution.py:125
  36.5 1.0 %copy.44 = f32[28,96,2]{1,2,0:T(2,128)} copy(f32[28,96,2]{2,1,0:T(8,128)S(1)} %get-tuple-element.9) | data formatting | bytes 43008 | tf_op jit(solution)/shard_map/jit(_where)/select_n | solution.py:124
  37.5 2.0 %collective-permute-start.1 = (f32[28,96,2]{1,2,0:T(2,128)}, f32[28,96,2]{1,2,0:T(2,128)}, u32[]{:S(2)}, u32[]{:S(2)}) collective-permute-start(f32[28,96,2]{1,2,0:T(2,128)} %copy.44), channel_id=1, source_target_pairs={{0,8},{8,0},{16,24},{24,16},{32,40},{40,32},{48,56},{56,48},{64,72... | collective-permute-start | bytes 64520 | tf_op jit(solution)/shard_map/ppermute | solution.py:124
  40.7 0.8 %add_convert_fusion.flag_ref = f32[2]{0:T(128)} fusion(pred[1]{0:T(512)(128)(4,1)} %constant.32.clone.1, pred[1]{0:T(512)(128)(4,1)} %bitcast), kind=kLoop, calls=%fused_computation.71 | loop fusion | flops 4 | bytes 10 | tf_op jit(solution)/shard_map/stack | solution.py:221
  41.7 0.9 %collective-permute-done = f32[28,96,2]{1,2,0:T(2,128)} collective-permute-done((f32[28,96,2]{1,2,0:T(2,128)}, f32[28,96,2]{1,2,0:T(2,128)}, u32[]{:S(2)}, u32[]{:S(2)}) %collective-permute-start) | collective-permute-done | bytes 21536 | tf_op jit(solution)/shard_map/ppermute | solution.py:125
  42.6 1.2 %copy.45 = f32[28,96,2]{2,1,0:T(8,128)S(1)} copy(f32[28,96,2]{1,2,0:T(2,128)} %collective-permute-done) | data formatting | bytes 43008 | tf_op jit(solution)/shard_map/ppermute | solution.py:125
  43.8 1.2 %copy.46 = f32[28,96,2]{2,1,0:T(8,128)S(1)} copy(f32[28,96,2]{1,2,0:T(2,128)} %collective-permute-done.1) | data formatting | bytes 43008 | tf_op jit(solution)/shard_map/ppermute | solution.py:124
  46.2 12.3 %collective-permute-start.4 = (f32[28,2,132]{2,1,0:T(2,128)S(1)}, f32[28,2,132]{2,1,0:T(2,128)S(1)}, u32[]{:S(2)}, u32[]{:S(2)}) collective-permute-start(f32[28,2,132]{2,1,0:T(2,128)S(1)} %get-tuple-element.5), channel_id=1, source_target_pairs={{7,511},{15,503},{23,495},{31,487},{39,479},{47,471},{55,463},{63,... | collective-permute-start | bytes 88712 | tf_op jit(solution)/shard_map/ppermute | solution.py:144
  58.5 0.7 collective-permute-start.2
  59.2 1.9 %collective-permute-start.3 = (f32[28,2,132]{2,1,0:T(2,128)S(1)}, f32[28,2,132]{2,1,0:T(2,128)S(1)}, u32[]{:S(2)}, u32[]{:S(2)}) collective-permute-start(f32[28,2,132]{2,1,0:T(2,128)S(1)} %get-tuple-element.4), channel_id=1, source_target_pairs={{0,1},{1,0},{2,3},{3,2},{4,5},{5,4},{6,7},{7,6},{8,9},{9,8},{10,11... | collective-permute-start | bytes 88712 | tf_op jit(solution)/shard_map/ppermute | solution.py:124
  61.1 2.0 %pad_maximum_fusion.middle_ref = f32[28,96,256]{2,1,0:T(8,128)} fusion(f32[28,96,2]{2,1,0:T(8,128)S(1)} %get-tuple-element.6, f32[28,96,2]{2,1,0:T(8,128)S(1)} %get-tuple-element.7, f32[28,96,128]{2,1,0:T(8,128)S(1)} %copy-done.6, f32[256]{0:T(256)S(1)} %pad.13.clone), kind=kLoop, calls=%fused_computation | loop fusion | flops 2064384 | bytes 4172800 | tf_op jit(solution)/shard_map/concatenate | solution.py:210
  63.2 2.0 %collective-permute-done.4 = f32[28,2,132]{2,1,0:T(2,128)S(1)} collective-permute-done((f32[28,2,132]{2,1,0:T(2,128)S(1)}, f32[28,2,132]{2,1,0:T(2,128)S(1)}, u32[]{:S(2)}, u32[]{:S(2)}) %collective-permute-start.4) | collective-permute-done | bytes 29600 | tf_op jit(solution)/shard_map/ppermute | solution.py:144
  66.7 0.7 concatenate.51.low_ref
  67.4 0.7 concatenate.57.high_ref
  68.1 7.3 %shard_map.156 = (f32[4,96,128]{2,1,0:T(8,128)}, f32[4,96,128]{2,1,0:T(8,128)}, f32[4,96,128]{2,1,0:T(8,128)}, f32[4,96,128]{2,1,0:T(8,128)}) custom-call(f32[4]{0:T(128)} %height_ref.1, f32[2]{0:T(128)} %add_convert_fusion.flag_ref, f32[28,8,256]{2,1,0:T(8,128)} %concatenate.51.low_ref, f32[28,96,256]{2,1,0:T(8,128)} %pad_maximum_fusion.middle_ref, ...), custom_call_target="tpu_custom_call" | custom-call | tf_op jit(solution)/shard_map/pallas_call | solution.py:225
  (147 shorter events, 14.6 us)
Async XLA Ops:
  0.6 2.6 %copy-start.2 = (f32[4,96,128]{2,1,0:T(8,128)S(1)}, f32[4,96,128]{2,1,0:T(8,128)}, u32[]{:S(2)}) copy-start(f32[4,96,128]{2,1,0:T(8,128)} %param.14) | copy-start | bytes 589828
  0.7 2.9 %copy-start.3 = (f32[4,96,128]{2,1,0:T(8,128)S(1)}, f32[4,96,128]{2,1,0:T(8,128)}, u32[]{:S(2)}) copy-start(f32[4,96,128]{2,1,0:T(8,128)} %param.15) | copy-start | bytes 589828
  3.3 3.7 %copy-start.8 = (s32[96,128]{1,0:T(8,128)S(1)}, s32[96,128]{1,0:T(8,128)}, u32[]{:S(2)}) copy-start(s32[96,128]{1,0:T(8,128)} %param.18) | copy-start | bytes 147460
  3.4 4.3 %copy-start.9 = (f32[96,128]{1,0:T(8,128)S(1)}, f32[96,128]{1,0:T(8,128)}, u32[]{:S(2)}) copy-start(f32[96,128]{1,0:T(8,128)} %param.19) | copy-start | bytes 147460
  3.4 5.0 %copy-start.11 = (f32[96,128]{1,0:T(8,128)S(1)}, f32[96,128]{1,0:T(8,128)}, u32[]{:S(2)}) copy-start(f32[96,128]{1,0:T(8,128)} %param.20) | copy-start | bytes 147460
  3.5 5.6 %copy-start.13 = (f32[96,128]{1,0:T(8,128)S(1)}, f32[96,128]{1,0:T(8,128)}, u32[]{:S(2)}) copy-start(f32[96,128]{1,0:T(8,128)} %param.21) | copy-start | bytes 147460
  3.5 6.3 %copy-start.15 = (f32[96,128]{1,0:T(8,128)S(1)}, f32[96,128]{1,0:T(8,128)}, u32[]{:S(2)}) copy-start(f32[96,128]{1,0:T(8,128)} %param.22) | copy-start | bytes 147460
  3.6 6.9 %copy-start.7 = (f32[3,96,128]{2,1,0:T(8,128)S(1)}, f32[3,96,128]{2,1,0:T(8,128)}, u32[]{:S(2)}) copy-start(f32[3,96,128]{2,1,0:T(8,128)} %param.23) | copy-start | bytes 442372
  10.6 5.4 %copy-start.17 = (f32[96,2]{1,0:T(8,128)S(1)}, f32[96,2]{1,0:T(8,128)}, u32[]{:S(2)}) copy-start(f32[96,2]{1,0:T(8,128)} %get-tuple-element.60) | copy-start | bytes 2308
  10.6 5.5 %copy-start.18 = (f32[96,2]{1,0:T(8,128)S(1)}, f32[96,2]{1,0:T(8,128)}, u32[]{:S(2)}) copy-start(f32[96,2]{1,0:T(8,128)} %get-tuple-element.58) | copy-start | bytes 2308
  10.7 6.3 %copy-start.19 = (f32[96,2]{1,0:T(8,128)S(1)}, f32[96,2]{1,0:T(8,128)}, u32[]{:S(2)}) copy-start(f32[96,2]{1,0:T(8,128)} %get-tuple-element.54) | copy-start | bytes 2308
  10.7 6.4 %copy-start.20 = (f32[96,2]{1,0:T(8,128)S(1)}, f32[96,2]{1,0:T(8,128)}, u32[]{:S(2)}) copy-start(f32[96,2]{1,0:T(8,128)} %get-tuple-element.52) | copy-start | bytes 2308
  21.7 17.8 %copy-start = (s32[4,96,128]{2,1,0:T(8,128)S(1)}, s32[4,96,128]{2,1,0:T(8,128)}, u32[]{:S(2)}) copy-start(s32[4,96,128]{2,1,0:T(8,128)} %param.17) | copy-start | bytes 589828
  21.7 17.8 %copy-start.1 = (f32[4,96,128]{2,1,0:T(8,128)S(1)}, f32[4,96,128]{2,1,0:T(8,128)}, u32[]{:S(2)}) copy-start(f32[4,96,128]{2,1,0:T(8,128)} %param.13) | copy-start | bytes 589828
  24.2 18.4 %collective-permute-start = (f32[28,96,2]{1,2,0:T(2,128)}, f32[28,96,2]{1,2,0:T(2,128)}, u32[]{:S(2)}, u32[]{:S(2)}) collective-permute-start(f32[28,96,2]{1,2,0:T(2,128)} %copy.41), channel_id=1, source_target_pairs={{8,16},{16,8},{24,32},{32,24},{40,48},{48,40},{56,64},{64,56},{72,... | collective-permute-start | bytes 64520 | tf_op jit(solution)/shard_map/ppermute | solution.py:125
  37.5 2.3 %copy-start.10 = (f32[96,128]{1,0:T(8,128)S(1)}, f32[96,128]{1,0:T(8,128)}, u32[]{:S(2)}) copy-start(f32[96,128]{1,0:T(8,128)} %param.19) | copy-start | bytes 147460
  37.5 2.3 %copy-start.12 = (f32[96,128]{1,0:T(8,128)S(1)}, f32[96,128]{1,0:T(8,128)}, u32[]{:S(2)}) copy-start(f32[96,128]{1,0:T(8,128)} %param.20) | copy-start | bytes 147460
  37.5 6.3 %collective-permute-start.1 = (f32[28,96,2]{1,2,0:T(2,128)}, f32[28,96,2]{1,2,0:T(2,128)}, u32[]{:S(2)}, u32[]{:S(2)}) collective-permute-start(f32[28,96,2]{1,2,0:T(2,128)} %copy.44), channel_id=1, source_target_pairs={{0,8},{8,0},{16,24},{24,16},{32,40},{40,32},{48,56},{56,48},{64,72... | collective-permute-start | bytes 64520 | tf_op jit(solution)/shard_map/ppermute | solution.py:124
  40.6 3.2 %copy-start.21 = (f32[28,2,128]{2,1,0:T(2,128)}, f32[28,2,128]{2,1,0:T(2,128)S(1)}, u32[]{:S(2)}) copy-start(f32[28,2,128]{2,1,0:T(2,128)S(1)} %get-tuple-element.35) | copy-start | bytes 86020
  40.7 3.1 %copy-start.23 = (f32[28,2,128]{2,1,0:T(2,128)}, f32[28,2,128]{2,1,0:T(2,128)S(1)}, u32[]{:S(2)}) copy-start(f32[28,2,128]{2,1,0:T(2,128)S(1)} %get-tuple-element.34) | copy-start | bytes 86020
  45.0 16.1 %copy-start.6 = (f32[28,96,128]{2,1,0:T(8,128)S(1)}, f32[28,96,128]{2,1,0:T(8,128)}, u32[]{:S(2)}) copy-start(f32[28,96,128]{2,1,0:T(8,128)} %copy-done.5) | copy-start | bytes 4128772
  46.2 18.9 %collective-permute-start.4 = (f32[28,2,132]{2,1,0:T(2,128)S(1)}, f32[28,2,132]{2,1,0:T(2,128)S(1)}, u32[]{:S(2)}, u32[]{:S(2)}) collective-permute-start(f32[28,2,132]{2,1,0:T(2,128)S(1)} %get-tuple-element.5), channel_id=1, source_target_pairs={{7,511},{15,503},{23,495},{31,487},{39,479},{47,471},{55,463},{63,... | collective-permute-start | bytes 88712 | tf_op jit(solution)/shard_map/ppermute | solution.py:144
  58.5 7.6 %collective-permute-start.2 = (f32[28,2,132]{2,1,0:T(2,128)S(1)}, f32[28,2,132]{2,1,0:T(2,128)S(1)}, u32[]{:S(2)}, u32[]{:S(2)}) collective-permute-start(f32[28,2,132]{2,1,0:T(2,128)S(1)} %broadcast_select_fusion.6), channel_id=1, source_target_pairs={{1,2},{2,1},{3,4},{4,3},{5,6},{6,5},{9,10},{10,9},{11,12},{12,11},... | collective-permute-start | bytes 88712 | tf_op jit(solution)/shard_map/ppermute | solution.py:125
  59.2 6.9 %collective-permute-start.3 = (f32[28,2,132]{2,1,0:T(2,128)S(1)}, f32[28,2,132]{2,1,0:T(2,128)S(1)}, u32[]{:S(2)}, u32[]{:S(2)}) collective-permute-start(f32[28,2,132]{2,1,0:T(2,128)S(1)} %get-tuple-element.4), channel_id=1, source_target_pairs={{0,1},{1,0},{2,3},{3,2},{4,5},{5,4},{6,7},{7,6},{8,9},{9,8},{10,11... | collective-permute-start | bytes 88712 | tf_op jit(solution)/shard_map/ppermute | solution.py:124
  (7 other events, 7.9 us)

commit v15 on v13

--- a/solution.py
+++ b/solution.py
@@ -109,16 +109,30 @@
     return [(i * lat_count + top, (target_of(i) % lon_count) * lat_count + top) for i in range(lon_count)]
 
 
-def exchange(take, sign):
+def exchange(take, take_edge, take_edge_size, sign):
     lon_count = lax.axis_size("lon")
     lat_count = lax.axis_size("lat")
     h = HALO
     every = slice(None)
 
-    east_pairs = [(i, (i + 1) % lon_count) for i in range(lon_count)]
-    west_pairs = [(j, i) for i, j in east_pairs]
-    west = lax.ppermute(take(every, slice(-h, None)), "lon", east_pairs)
-    east = lax.ppermute(take(every, slice(0, h)), "lon", west_pairs)
+    if lon_count % 2:
+        east_pairs = [(i, (i + 1) % lon_count) for i in range(lon_count)]
+        west_pairs = [(j, i) for i, j in east_pairs]
+        west = lax.ppermute(take(every, slice(-h, None)), "lon", east_pairs)
+        east = lax.ppermute(take(every, slice(0, h)), "lon", west_pairs)
+    else:
+        even = lax.axis_index("lon") % 2 == 0
+        high = take_edge_size() - h
+        inner = []
+        for i in range(0, lon_count, 2):
+            inner += [(i, i + 1), (i + 1, i)]
+        outer = []
+        for i in range(1, lon_count, 2):
+            outer += [(i, (i + 1) % lon_count), ((i + 1) % lon_count, i)]
+        from_inner = lax.ppermute(take_edge(jnp.where(even, high, 0)), "lon", inner)
+        from_outer = lax.ppermute(take_edge(jnp.where(even, 0, high)), "lon", outer)
+        west = jnp.where(even, from_outer, from_inner)
+        east = jnp.where(even, from_inner, from_outer)
 
     rows_hi = take(slice(-h, None), every)
     rows_lo = take(slice(0, h), every)
@@ -171,13 +185,23 @@
         parts.append(diapycnal_diffusivity[:, rs, cs])
         return jnp.concatenate(parts, axis=0)
 
+    def take_edge(start):
+        def cut(a):
+            return lax.dynamic_slice_in_dim(a, start, HALO, axis=a.ndim - 1)
+
+        wet = cut(water_indicator).astype(jnp.float32)
+        parts = [cut(f) * wet for f in fields] + [wet]
+        parts += [cut(s)[None].astype(jnp.float32) for s in surfaces]
+        parts.append(cut(diapycnal_diffusivity))
+        return jnp.concatenate(parts, axis=0)
+
     channels = len(fields) + 1
     levels, rows, cols = potential_heat.shape
     channel_sign = jnp.array([1.0, 1.0, -1.0, -1.0, 1.0], jnp.float32)
     sign = jnp.concatenate(
         [jnp.repeat(channel_sign, levels), jnp.ones((len(surfaces) + levels - 1,), jnp.float32)]
     )
-    west, east, south, north = exchange(take, sign)
+    west, east, south, north = exchange(take, take_edge, lambda: cols, sign)
     block = take(slice(None), slice(None))
     lanes = 2 * cols
     gap = lanes - cols - 2 * HALO

time: 66.4 us -> 59.6 us (0.90)
  waiting for transfers between devices: 20.6 us -> 0.01 us
  starting transfers between devices: 22.6 us -> 30 us
  other arithmetic: 5.21 us -> 9.25 us
  local copies, waits for them, and re-layouts: 9.23 us -> 11.6 us
    ppermute x2, waiting for transfers between devices: 14.1 us -> 0.01 us  [the longest x1 0.01 us: exchange(): from_inner = lax.ppermute(take_edge(jnp.where(even, high, 0)), 'lon', inner)]
    ppermute x1, starting transfers between devices: 2.49 us -> 9.27 us  [exchange(): lax.ppermute(top_band, ('lon', 'lat'), fold_pairs(lon_count, lat_count, l...]
    ppermute x1, waiting for transfers between devices: 6.53 us -> 0.01 us  [exchange(): lax.ppermute(top_band, ('lon', 'lat'), fold_pairs(lon_count, lat_count, l...]
    unnamed x22, other arithmetic: 0.32 us -> 4.31 us
    slice x10 -> x0, local copies, waits for them, and re-layouts: 3.19 us -> none  [the longest x4 1.54 us: take(): parts = [f[:, rs, cs] * wet for f in fields] + [wet]]
    dynamic_slice x0 -> x14, local copies, waits for them, and re-layouts: none -> 3.02 us  [cut(): return lax.dynamic_slice_in_dim(a, start, HALO, axis=a.ndim - 1)]
    unnamed x70 -> x60, local copies, waits for them, and re-layouts: 3.06 us -> 4.93 us
  transfers between devices with their start and end apart: 5 -> 5, of which waited for: 2 -> 0; matrix products, arithmetic and copies ran while one was open for 12% -> 25% of each run, Pallas kernels for 0% -> 0%
where the time goes in v15:
time: 59.6 us; the launch traced here: 59.3 us
  starting transfers between devices  30 us (50%)
  local copies, waits for them, and re-layouts  11.6 us (19%)
  other arithmetic  9.25 us (16%)
  Pallas kernels  7.29 us (12%)
  between operations  1.13 us (2%)
    ppermute x1, starting transfers between devices, exchange(): from_outer = lax.ppermute(take_edge(jnp.where(even, 0, high)), 'lon', outer)  13 us
    ppermute x1, starting transfers between devices, exchange(): lax.ppermute(top_band, ('lon', 'lat'), fold_pairs(lon_count, lat_count, l...  9.27 us
    pallas_call x1, Pallas kernels, shards(): pl.pallas_call(two_steps_kernel, out_shape=[field_shape] * (channels - 1)...  7.29 us
    unnamed x60, local copies, waits for them, and re-layouts  4.93 us
    ppermute x1, starting transfers between devices, exchange(): north = lax.ppermute(bottom_band, 'lat', south_pairs)  4.55 us
    unnamed x22, other arithmetic  4.31 us
    concatenate x1, other arithmetic, shards(): jnp.concatenate([block, east, jnp.zeros((block.shape[0], rows, gap), jnp....  3.39 us
    dynamic_slice x14, local copies, waits for them, and re-layouts, cut(): return lax.dynamic_slice_in_dim(a, start, HALO, axis=a.ndim - 1)  3.02 us
  transfers between devices with their start and end apart: 5, of which 0 were waited for; matrix products, arithmetic and copies ran while one was open for 25% of the time, Pallas kernels for 0%

profile of v15, /device:TPU:224, one launch (start us, length us, event | category | flops | bytes accessed | tf_op | source)
XLA Modules:
  0.0 59.3 jit_solution(7943530605440131806)
XLA Ops:
  0.7 1.6 %constant_dynamic-slice_fusion.17 = (f32[4,96,2]{2,1,0:T(8,128)S(1)}, f32[4,96,2]{2,1,0:T(8,128)S(1)}, f32[4,96,2]{2,1,0:T(8,128)S(1)}, f32[4,96,2]{2,1,0:T(8,128)S(1)}) fusion(f32[4,96,128]{2,1,0:T(8,128)} %param.14, s32[]{:T(128)S(6)} %select_n.58, s32[]{:T(128)S(6)} %select_n.59, f32[4,96,128]{2,1,0:T(8,128)} %param.13), kind=kLoop, calls=%fused_computation.83 | loop fusion | bytes 24584 | tf_op jit(solution)/shard_map/dynamic_slice | solution.py:190
  4.5 1.9 %collective-permute-start.1 = (f32[28,96,2]{1,2,0:T(2,128)S(1)}, f32[28,96,2]{1,2,0:T(2,128)S(1)}, u32[]{:S(2)}, u32[]{:S(2)}) collective-permute-start(f32[28,96,2]{1,2,0:T(2,128)S(1)} %constant_dynamic-update-slice_fusion.11), channel_id=1, source_target_pairs={{0,8},{8,0},{16,24},{24,16},{32,40},{40,32},{48,56},{56,48},{64,72... | collective-permute-start | bytes 64520 | tf_op jit(solution)/shard_map/ppermute | solution.py:132
  7.6 13.0 %collective-permute-start = (f32[28,96,2]{1,2,0:T(2,128)S(1)}, f32[28,96,2]{1,2,0:T(2,128)S(1)}, u32[]{:S(2)}, u32[]{:S(2)}) collective-permute-start(f32[28,96,2]{1,2,0:T(2,128)S(1)} %constant_dynamic-update-slice_fusion), channel_id=1, source_target_pairs={{8,16},{16,8},{24,32},{32,24},{40,48},{48,40},{56,64},{64,56},{72,... | collective-permute-start | bytes 64520 | tf_op jit(solution)/shard_map/ppermute | solution.py:133
  20.6 0.7 %multiply_dynamic-update-slice_fusion.3 = f32[28,96,128]{2,1,0:T(8,128)} fusion(f32[4,96,128]{2,1,0:T(8,128)S(1)} %copy-done.1, s32[4,96,128]{2,1,0:T(8,128)S(1)} %copy-done), kind=kLoop, calls=%fused_computation.6 | loop fusion | flops 98303 | bytes 589824
  21.3 0.7 %multiply_dynamic-update-slice_fusion.2 = f32[28,96,128]{2,1,0:T(8,128)} fusion(f32[28,96,128]{2,1,0:T(8,128)} %multiply_dynamic-update-slice_fusion.3, f32[4,96,128]{2,1,0:T(8,128)S(1)} %copy-done.2, s32[4,96,128]{2,1,0:T(8,128)S(1)} %copy-done), kind=kLoop, calls=%fused_computation.5 | loop fusion | flops 98304 | bytes 589824
  22.0 0.7 %multiply_dynamic-update-slice_fusion.1 = f32[28,96,128]{2,1,0:T(8,128)} fusion(f32[28,96,128]{2,1,0:T(8,128)} %multiply_dynamic-update-slice_fusion.2, f32[4,96,128]{2,1,0:T(8,128)S(1)} %copy-done.3, s32[4,96,128]{2,1,0:T(8,128)S(1)} %copy-done), kind=kLoop, calls=%fused_computation.4 | loop fusion | flops 98304 | bytes 589824
  22.7 0.7 %multiply_dynamic-update-slice_fusion = f32[28,96,128]{2,1,0:T(8,128)} fusion(f32[28,96,128]{2,1,0:T(8,128)} %multiply_dynamic-update-slice_fusion.1, f32[4,96,128]{2,1,0:T(8,128)S(1)} %copy-done.4, s32[4,96,128]{2,1,0:T(8,128)S(1)} %copy-done), kind=kLoop, calls=%fused_computation.3 | loop fusion | flops 98304 | bytes 589824
  23.4 0.7 %convert_dynamic-update-slice_fusion = f32[28,96,128]{2,1,0:T(8,128)} fusion(f32[28,96,128]{2,1,0:T(8,128)} %multiply_dynamic-update-slice_fusion, s32[4,96,128]{2,1,0:T(8,128)S(1)} %copy-done), kind=kLoop, calls=%fused_computation.7 | loop fusion | flops 49152 | bytes 393216
  24.1 0.6 %constant_dynamic-update-slice_fusion.38 = f32[28,96,128]{2,1,0:T(8,128)} fusion(f32[28,96,128]{2,1,0:T(8,128)} %convert_dynamic-update-slice_fusion, s32[96,128]{1,0:T(8,128)S(1)} %copy-done.6), kind=kLoop, calls=%fused_computation.46 | loop fusion | flops 12288 | bytes 98304
  24.7 0.6 %constant_dynamic-update-slice_fusion.37 = f32[28,96,128]{2,1,0:T(8,128)} fusion(f32[28,96,128]{2,1,0:T(8,128)} %constant_dynamic-update-slice_fusion.38, f32[96,128]{1,0:T(8,128)S(1)} %copy-done.7), kind=kLoop, calls=%fused_computation.45 | loop fusion | bytes 98304
  25.3 0.6 %constant_dynamic-update-slice_fusion.36 = f32[28,96,128]{2,1,0:T(8,128)} fusion(f32[28,96,128]{2,1,0:T(8,128)} %constant_dynamic-update-slice_fusion.37, f32[96,128]{1,0:T(8,128)S(1)} %copy-done.8), kind=kLoop, calls=%fused_computation.44 | loop fusion | bytes 98304
  26.0 0.6 %constant_dynamic-update-slice_fusion.35 = f32[28,96,128]{2,1,0:T(8,128)} fusion(f32[28,96,128]{2,1,0:T(8,128)} %constant_dynamic-update-slice_fusion.36, f32[96,128]{1,0:T(8,128)S(1)} %copy-done.9), kind=kLoop, calls=%fused_computation.43 | loop fusion | bytes 98304
  26.6 0.6 %constant_dynamic-update-slice_fusion.34 = f32[28,96,128]{2,1,0:T(8,128)} fusion(f32[28,96,128]{2,1,0:T(8,128)} %constant_dynamic-update-slice_fusion.35, f32[96,128]{1,0:T(8,128)S(1)} %copy-done.10), kind=kLoop, calls=%fused_computation.42 | loop fusion | bytes 98304
  27.2 0.7 %constant_dynamic-update-slice_fusion.33 = f32[28,96,128]{2,1,0:T(8,128)} fusion(f32[28,96,128]{2,1,0:T(8,128)} %constant_dynamic-update-slice_fusion.34, f32[3,96,128]{2,1,0:T(8,128)S(1)} %copy-done.5), kind=kLoop, calls=%fused_computation.41 | loop fusion | bytes 294912 | tf_op jit(solution)/shard_map/concatenate | solution.py:186
  28.0 0.6 %add_convert_fusion.flag_ref = f32[2]{0:T(128)} fusion(pred[1]{0:T(512)(128)(4,1)} %constant.32.clone.1, pred[1]{0:T(512)(128)(4,1)} %bitcast), kind=kLoop, calls=%fused_computation.86 | loop fusion | flops 4 | bytes 10 | tf_op jit(solution)/shard_map/stack | solution.py:232
  28.9 0.5 copy.40
  29.4 0.5 copy.39
  30.4 9.3 %collective-permute-start.3 = (f32[28,2,132]{2,1,0:T(2,128)S(1)}, f32[28,2,132]{2,1,0:T(2,128)S(1)}, u32[]{:S(2)}, u32[]{:S(2)}) collective-permute-start(f32[28,2,132]{2,1,0:T(2,128)S(1)} %pad_maximum_fusion.1), channel_id=1, source_target_pairs={{7,511},{15,503},{23,495},{31,487},{39,479},{47,471},{55,463},{63,... | collective-permute-start | bytes 88712 | tf_op jit(solution)/shard_map/ppermute | solution.py:142
  39.6 1.3 %collective-permute-start.2 = (f32[28,2,132]{2,1,0:T(2,128)S(1)}, f32[28,2,132]{2,1,0:T(2,128)S(1)}, u32[]{:S(2)}, u32[]{:S(2)}) collective-permute-start(f32[28,2,132]{2,1,0:T(2,128)S(1)} %pad_maximum_fusion.1), channel_id=1, source_target_pairs={{0,1},{1,2},{2,3},{3,4},{4,5},{5,6},{6,7},{8,9},{9,10},{10,11},{11... | collective-permute-start | bytes 88712 | tf_op jit(solution)/shard_map/ppermute | solution.py:151
  41.1 4.5 %collective-permute-start.4 = (f32[28,2,132]{2,1,0:T(2,128)S(1)}, f32[28,2,132]{2,1,0:T(2,128)S(1)}, u32[]{:S(2)}, u32[]{:S(2)}) collective-permute-start(f32[28,2,132]{2,1,0:T(2,128)S(1)} %pad_maximum_fusion.3), channel_id=1, source_target_pairs={{1,0},{2,1},{3,2},{4,3},{5,4},{6,5},{7,6},{9,8},{10,9},{11,10},{12... | collective-permute-start | bytes 88712 | tf_op jit(solution)/shard_map/ppermute | solution.py:152
  45.7 3.4 %pad_maximum_fusion.middle_ref = f32[28,96,256]{2,1,0:T(8,128)} fusion(f32[28,96,2]{2,1,0:T(8,128)S(1)} %get-tuple-element.4, f32[28,96,2]{2,1,0:T(8,128)S(1)} %get-tuple-element.5, f32[28,96,128]{2,1,0:T(8,128)} %constant_dynamic-update-slice_fusion.33, f32[256]{0:T(256)S(1)} %pad.16.clone), kind=kLoop, calls=%fused_computation | loop fusion | flops 2064384 | bytes 4172800 | tf_op jit(solution)/shard_map/concatenate | solution.py:221
  50.6 0.7 %concatenate.49.low_ref = f32[28,8,256]{2,1,0:T(8,128)} pad(f32[28,2,256]{2,1,0:T(2,128)S(1)} %get-tuple-element.57, f32[]{:T(128)} %constant.38.clone.1), padding=0_0x6_0x0_0 | pad | bytes 286724 | tf_op jit(solution)/shard_map/concatenate | solution.py:226
  51.3 0.7 %concatenate.57.high_ref = f32[28,8,256]{2,1,0:T(8,128)} pad(f32[28,2,256]{2,1,0:T(2,128)S(1)} %get-tuple-element.56, f32[]{:T(128)} %constant.38.clone.1), padding=0_0x0_6x0_0 | pad | bytes 286724 | tf_op jit(solution)/shard_map/concatenate | solution.py:229
  52.0 7.3 %shard_map.156 = (f32[4,96,128]{2,1,0:T(8,128)}, f32[4,96,128]{2,1,0:T(8,128)}, f32[4,96,128]{2,1,0:T(8,128)}, f32[4,96,128]{2,1,0:T(8,128)}) custom-call(f32[4]{0:T(128)} %height_ref.1, f32[2]{0:T(128)} %add_convert_fusion.flag_ref, f32[28,8,256]{2,1,0:T(8,128)} %concatenate.49.low_ref, f32[28,96,256]{2,1,0:T(8,128)} %pad_maximum_fusion.middle_ref, ...), custom_call_target="tpu_custom_call" | custom-call | tf_op jit(solution)/shard_map/pallas_call | solution.py:236
  (111 shorter events, 5.6 us)
Async XLA Ops:
  0.6 1.7 %copy-start = (s32[4,96,128]{2,1,0:T(8,128)S(1)}, s32[4,96,128]{2,1,0:T(8,128)}, u32[]{:S(2)}) copy-start(s32[4,96,128]{2,1,0:T(8,128)} %param.17) | copy-start | bytes 589828
  0.7 2.1 %copy-start.3 = (f32[4,96,128]{2,1,0:T(8,128)S(1)}, f32[4,96,128]{2,1,0:T(8,128)}, u32[]{:S(2)}) copy-start(f32[4,96,128]{2,1,0:T(8,128)} %param.15) | copy-start | bytes 589828
  0.7 2.1 %copy-start.4 = (f32[4,96,128]{2,1,0:T(8,128)S(1)}, f32[4,96,128]{2,1,0:T(8,128)}, u32[]{:S(2)}) copy-start(f32[4,96,128]{2,1,0:T(8,128)} %param.16) | copy-start | bytes 589828
  2.5 0.9 %copy-start.6 = (s32[96,128]{1,0:T(8,128)S(1)}, s32[96,128]{1,0:T(8,128)}, u32[]{:S(2)}) copy-start(s32[96,128]{1,0:T(8,128)} %param.18) | copy-start | bytes 147460
  2.5 1.0 %copy-start.7 = (f32[96,128]{1,0:T(8,128)S(1)}, f32[96,128]{1,0:T(8,128)}, u32[]{:S(2)}) copy-start(f32[96,128]{1,0:T(8,128)} %param.19) | copy-start | bytes 147460
  2.6 1.0 %copy-start.8 = (f32[96,128]{1,0:T(8,128)S(1)}, f32[96,128]{1,0:T(8,128)}, u32[]{:S(2)}) copy-start(f32[96,128]{1,0:T(8,128)} %param.20) | copy-start | bytes 147460
  2.8 1.1 %copy-start.9 = (f32[96,128]{1,0:T(8,128)S(1)}, f32[96,128]{1,0:T(8,128)}, u32[]{:S(2)}) copy-start(f32[96,128]{1,0:T(8,128)} %param.21) | copy-start | bytes 147460
  2.8 1.1 %copy-start.10 = (f32[96,128]{1,0:T(8,128)S(1)}, f32[96,128]{1,0:T(8,128)}, u32[]{:S(2)}) copy-start(f32[96,128]{1,0:T(8,128)} %param.22) | copy-start | bytes 147460
  2.8 1.3 %copy-start.5 = (f32[3,96,128]{2,1,0:T(8,128)S(1)}, f32[3,96,128]{2,1,0:T(8,128)}, u32[]{:S(2)}) copy-start(f32[3,96,128]{2,1,0:T(8,128)} %param.23) | copy-start | bytes 442372
  3.9 16.7 %copy-start.1 = (f32[4,96,128]{2,1,0:T(8,128)S(1)}, f32[4,96,128]{2,1,0:T(8,128)}, u32[]{:S(2)}) copy-start(f32[4,96,128]{2,1,0:T(8,128)} %param.13) | copy-start | bytes 589828
  4.2 17.1 %copy-start.2 = (f32[4,96,128]{2,1,0:T(8,128)S(1)}, f32[4,96,128]{2,1,0:T(8,128)}, u32[]{:S(2)}) copy-start(f32[4,96,128]{2,1,0:T(8,128)} %param.14) | copy-start | bytes 589828
  4.5 24.4 %collective-permute-start.1 = (f32[28,96,2]{1,2,0:T(2,128)S(1)}, f32[28,96,2]{1,2,0:T(2,128)S(1)}, u32[]{:S(2)}, u32[]{:S(2)}) collective-permute-start(f32[28,96,2]{1,2,0:T(2,128)S(1)} %constant_dynamic-update-slice_fusion.11), channel_id=1, source_target_pairs={{0,8},{8,0},{16,24},{24,16},{32,40},{40,32},{48,56},{56,48},{64,72... | collective-permute-start | bytes 64520 | tf_op jit(solution)/shard_map/ppermute | solution.py:132
  7.6 21.8 %collective-permute-start = (f32[28,96,2]{1,2,0:T(2,128)S(1)}, f32[28,96,2]{1,2,0:T(2,128)S(1)}, u32[]{:S(2)}, u32[]{:S(2)}) collective-permute-start(f32[28,96,2]{1,2,0:T(2,128)S(1)} %constant_dynamic-update-slice_fusion), channel_id=1, source_target_pairs={{8,16},{16,8},{24,32},{32,24},{40,48},{48,40},{56,64},{64,56},{72,... | collective-permute-start | bytes 64520 | tf_op jit(solution)/shard_map/ppermute | solution.py:133
  22.0 6.7 %copy-start.11 = (f32[5]{0:T(128)S(1)}, f32[5]{0:T(128)}, u32[]{:S(2)}) copy-start(f32[5]{0:T(128)} %constant.41.clone) | copy-start | bytes 64
  30.4 18.7 %collective-permute-start.3 = (f32[28,2,132]{2,1,0:T(2,128)S(1)}, f32[28,2,132]{2,1,0:T(2,128)S(1)}, u32[]{:S(2)}, u32[]{:S(2)}) collective-permute-start(f32[28,2,132]{2,1,0:T(2,128)S(1)} %pad_maximum_fusion.1), channel_id=1, source_target_pairs={{7,511},{15,503},{23,495},{31,487},{39,479},{47,471},{55,463},{63,... | collective-permute-start | bytes 88712 | tf_op jit(solution)/shard_map/ppermute | solution.py:142
  39.6 10.6 %collective-permute-start.2 = (f32[28,2,132]{2,1,0:T(2,128)S(1)}, f32[28,2,132]{2,1,0:T(2,128)S(1)}, u32[]{:S(2)}, u32[]{:S(2)}) collective-permute-start(f32[28,2,132]{2,1,0:T(2,128)S(1)} %pad_maximum_fusion.1), channel_id=1, source_target_pairs={{0,1},{1,2},{2,3},{3,4},{4,5},{5,6},{6,7},{8,9},{9,10},{10,11},{11... | collective-permute-start | bytes 88712 | tf_op jit(solution)/shard_map/ppermute | solution.py:151
  41.1 8.9 %collective-permute-start.4 = (f32[28,2,132]{2,1,0:T(2,128)S(1)}, f32[28,2,132]{2,1,0:T(2,128)S(1)}, u32[]{:S(2)}, u32[]{:S(2)}) collective-permute-start(f32[28,2,132]{2,1,0:T(2,128)S(1)} %pad_maximum_fusion.3), channel_id=1, source_target_pairs={{1,0},{2,1},{3,2},{4,3},{5,4},{6,5},{7,6},{9,8},{10,9},{11,10},{12... | collective-permute-start | bytes 88712 | tf_op jit(solution)/shard_map/ppermute | solution.py:152

commit v16 on v15

--- a/solution.py
+++ b/solution.py
@@ -122,7 +122,7 @@
         east = lax.ppermute(take(every, slice(0, h)), "lon", west_pairs)
     else:
         even = lax.axis_index("lon") % 2 == 0
-        high = take_edge_size() - h
+        high = take_edge_size(2) - h
         inner = []
         for i in range(0, lon_count, 2):
             inner += [(i, i + 1), (i + 1, i)]
@@ -146,10 +146,31 @@
     folded = jnp.concatenate([mirrored[:, 1:2, :], mirrored[:, 0:1, :]], axis=1)
     folded = folded * sign[:, None, None]
 
-    north_pairs = [(j, j + 1) for j in range(lat_count - 1)]
-    south_pairs = [(j, i) for i, j in north_pairs]
-    south = lax.ppermute(top_band, "lat", north_pairs)
-    north = lax.ppermute(bottom_band, "lat", south_pairs)
+    if lat_count % 2:
+        north_pairs = [(j, j + 1) for j in range(lat_count - 1)]
+        south_pairs = [(j, i) for i, j in north_pairs]
+        south = lax.ppermute(top_band, "lat", north_pairs)
+        north = lax.ppermute(bottom_band, "lat", south_pairs)
+    else:
+        even = lax.axis_index("lat") % 2 == 0
+        high_row = take_edge_size(1) - h
+
+        def band(start):
+            def cut(a):
+                return lax.dynamic_slice_in_dim(a, start, h, axis=1)
+
+            return jnp.concatenate([cut(west), take_edge(start, 1), cut(east)], axis=2)
+
+        inner = []
+        for j in range(0, lat_count, 2):
+            inner += [(j, j + 1), (j + 1, j)]
+        outer = []
+        for j in range(1, lat_count - 1, 2):
+            outer += [(j, j + 1), (j + 1, j)]
+        from_inner = lax.ppermute(band(jnp.where(even, high_row, 0)), "lat", inner)
+        from_outer = lax.ppermute(band(jnp.where(even, 0, high_row)), "lat", outer)
+        south = jnp.where(even, from_outer, from_inner)
+        north = jnp.where(even, from_inner, from_outer)
     is_top = lax.axis_index("lat") == lat_count - 1
     north = jnp.where(is_top, folded, north)
     return west, east, south, north
@@ -185,9 +206,9 @@
         parts.append(diapycnal_diffusivity[:, rs, cs])
         return jnp.concatenate(parts, axis=0)
 
-    def take_edge(start):
+    def take_edge(start, axis=2):
         def cut(a):
-            return lax.dynamic_slice_in_dim(a, start, HALO, axis=a.ndim - 1)
+            return lax.dynamic_slice_in_dim(a, start, HALO, axis=a.ndim + axis - 3)
 
         wet = cut(water_indicator).astype(jnp.float32)
         parts = [cut(f) * wet for f in fields] + [wet]
@@ -201,7 +222,7 @@
     sign = jnp.concatenate(
         [jnp.repeat(channel_sign, levels), jnp.ones((len(surfaces) + levels - 1,), jnp.float32)]
     )
-    west, east, south, north = exchange(take, take_edge, lambda: cols, sign)
+    west, east, south, north = exchange(take, take_edge, lambda axis: (rows, cols)[axis - 1], sign)
     block = take(slice(None), slice(None))
     lanes = 2 * cols
     gap = lanes - cols - 2 * HALO

time: 59.6 us -> 61.9 us (1.039)
  the two profiles are of different devices: /device:TPU:224 before, /device:TPU:511 now
where the time goes in v16:
time: 61.9 us; the launch traced here: 61.7 us
  waiting for transfers between devices  21.7 us (35%)
  starting transfers between devices  18.5 us (30%)
  local copies, waits for them, and re-layouts  8.6 us (14%)
  Pallas kernels  7.29 us (12%)
  other arithmetic  4.26 us (7%)
  between operations  1.26 us (2%)
    ppermute x1, waiting for transfers between devices, exchange(): lax.ppermute(top_band, ('lon', 'lat'), fold_pairs(lon_count, lat_count, l...  11.2 us
    ppermute x1, waiting for transfers between devices, exchange(): from_outer = lax.ppermute(take_edge(jnp.where(even, 0, high)), 'lon', outer)  10.5 us
    pallas_call x1, Pallas kernels, shards(): pl.pallas_call(two_steps_kernel, out_shape=[field_shape] * (channels - 1)...  7.29 us
    ppermute x1, starting transfers between devices, exchange(): from_outer = lax.ppermute(take_edge(jnp.where(even, 0, high)), 'lon', outer)  5.53 us
    ppermute x1, starting transfers between devices, exchange(): lax.ppermute(top_band, ('lon', 'lat'), fold_pairs(lon_count, lat_count, l...  5.13 us
    ppermute x1, starting transfers between devices, exchange(): from_inner = lax.ppermute(band(jnp.where(even, high_row, 0)), 'lat', inner)  4.61 us
    dynamic_slice x14, local copies, waits for them, and re-layouts, cut(): return lax.dynamic_slice_in_dim(a, start, HALO, axis=a.ndim + axis - 3)  3.02 us
    ppermute x1, starting transfers between devices, exchange(): from_inner = lax.ppermute(take_edge(jnp.where(even, high, 0)), 'lon', inner)  2.58 us
  transfers between devices with their start and end apart: 5, of which 2 were waited for; matrix products, arithmetic and copies ran while one was open for 10% of the time, Pallas kernels for 0%

profile of v16, /device:TPU:511, one launch (start us, length us, event | category | flops | bytes accessed | tf_op | source)
XLA Modules:
  0.0 61.7 jit_solution(16962442675975435999)
XLA Ops:
  0.7 1.6 %constant_dynamic-slice_fusion.43 = (f32[4,96,2]{2,1,0:T(8,128)S(1)}, f32[4,96,2]{2,1,0:T(8,128)S(1)}, f32[4,96,2]{2,1,0:T(8,128)S(1)}, f32[4,96,2]{2,1,0:T(8,128)S(1)}) fusion(f32[4,96,128]{2,1,0:T(8,128)} %param.14, s32[]{:T(128)S(6)} %select_n.56, s32[]{:T(128)S(6)} %select_n.57, f32[4,96,128]{2,1,0:T(8,128)} %param.13), kind=kLoop, calls=%fused_computation.122 | loop fusion | bytes 24584 | tf_op jit(solution)/shard_map/dynamic_slice | solution.py:211
  2.4 0.2 constant_dynamic-slice_fusion.44
  2.8 0.3 constant_dynamic-slice_fusion.41
  4.2 0.2 constant_dynamic-slice_fusion.36
  4.5 2.6 %collective-permute-start.1 = (f32[28,96,2]{1,2,0:T(2,128)S(1)}, f32[28,96,2]{1,2,0:T(2,128)S(1)}, u32[]{:S(2)}, u32[]{:S(2)}) collective-permute-start(f32[28,96,2]{1,2,0:T(2,128)S(1)} %constant_dynamic-update-slice_fusion.11), channel_id=1, source_target_pairs={{0,8},{8,0},{16,24},{24,16},{32,40},{40,32},{48,56},{56,48},{64,72... | collective-permute-start | bytes 64520 | tf_op jit(solution)/shard_map/ppermute | solution.py:132
  8.3 5.5 %collective-permute-start = (f32[28,96,2]{1,2,0:T(2,128)S(1)}, f32[28,96,2]{1,2,0:T(2,128)S(1)}, u32[]{:S(2)}, u32[]{:S(2)}) collective-permute-start(f32[28,96,2]{1,2,0:T(2,128)S(1)} %constant_dynamic-update-slice_fusion), channel_id=1, source_target_pairs={{8,16},{16,8},{24,32},{32,24},{40,48},{48,40},{56,64},{64,56},{72,... | collective-permute-start | bytes 64520 | tf_op jit(solution)/shard_map/ppermute | solution.py:133
  14.4 0.7 %add_convert_fusion.flag_ref = f32[2]{0:T(128)} fusion(pred[1]{0:T(512)(128)(4,1)} %constant.40.clone.1, pred[1]{0:T(512)(128)(4,1)} %bitcast), kind=kLoop, calls=%fused_computation.135 | loop fusion | flops 4 | bytes 10 | tf_op jit(solution)/shard_map/stack | solution.py:253
  15.4 0.5 copy.40
  15.9 10.5 %collective-permute-done = f32[28,96,2]{1,2,0:T(2,128)S(1)} collective-permute-done((f32[28,96,2]{1,2,0:T(2,128)S(1)}, f32[28,96,2]{1,2,0:T(2,128)S(1)}, u32[]{:S(2)}, u32[]{:S(2)}) %collective-permute-start) | collective-permute-done | bytes 21536 | tf_op jit(solution)/shard_map/ppermute | solution.py:133
  26.4 0.5 copy.39
  26.9 0.2 broadcast_select_fusion.1
  27.2 0.2 pad_maximum_fusion.1
  27.4 0.7 %collective-permute-start.2 = (f32[28,2,132]{2,1,0:T(2,128)S(1)}, f32[28,2,132]{2,1,0:T(2,128)S(1)}, u32[]{:S(2)}, u32[]{:S(2)}) collective-permute-start(f32[28,2,132]{2,1,0:T(2,128)S(1)} %pad_maximum_fusion.1), channel_id=1, source_target_pairs={{1,2},{2,1},{3,4},{4,3},{5,6},{6,5},{9,10},{10,9},{11,12},{12,11},... | collective-permute-start | bytes 88712 | tf_op jit(solution)/shard_map/ppermute | solution.py:171
  28.1 0.2 pad_maximum_fusion.2
  28.2 4.6 %collective-permute-start.3 = (f32[28,2,132]{2,1,0:T(2,128)S(1)}, f32[28,2,132]{2,1,0:T(2,128)S(1)}, u32[]{:S(2)}, u32[]{:S(2)}) collective-permute-start(f32[28,2,132]{2,1,0:T(2,128)S(1)} %pad_maximum_fusion.2), channel_id=1, source_target_pairs={{0,1},{1,0},{2,3},{3,2},{4,5},{5,4},{6,7},{7,6},{8,9},{9,8},{10,11... | collective-permute-start | bytes 88712 | tf_op jit(solution)/shard_map/ppermute | solution.py:170
  32.8 0.2 pad_maximum_fusion.4
  33.0 5.1 %collective-permute-start.4 = (f32[28,2,132]{2,1,0:T(2,128)S(1)}, f32[28,2,132]{2,1,0:T(2,128)S(1)}, u32[]{:S(2)}, u32[]{:S(2)}) collective-permute-start(f32[28,2,132]{2,1,0:T(2,128)S(1)} %pad_maximum_fusion.4), channel_id=1, source_target_pairs={{7,511},{15,503},{23,495},{31,487},{39,479},{47,471},{55,463},{63,... | collective-permute-start | bytes 88712 | tf_op jit(solution)/shard_map/ppermute | solution.py:142
  38.1 2.1 %pad_maximum_fusion.middle_ref = f32[28,96,256]{2,1,0:T(8,128)} fusion(f32[28,96,2]{2,1,0:T(8,128)S(1)} %get-tuple-element.4, f32[28,96,2]{2,1,0:T(8,128)S(1)} %get-tuple-element.5, f32[28,96,128]{2,1,0:T(8,128)S(1)} %copy-done.6, f32[256]{0:T(256)S(1)} %pad.16.clone), kind=kLoop, calls=%fused_computation | loop fusion | flops 2064384 | bytes 4172800 | tf_op jit(solution)/shard_map/concatenate | solution.py:242
  40.2 11.2 %collective-permute-done.4 = f32[28,2,132]{2,1,0:T(2,128)S(1)} collective-permute-done((f32[28,2,132]{2,1,0:T(2,128)S(1)}, f32[28,2,132]{2,1,0:T(2,128)S(1)}, u32[]{:S(2)}, u32[]{:S(2)}) %collective-permute-start.4) | collective-permute-done | bytes 29600 | tf_op jit(solution)/shard_map/ppermute | solution.py:142
  51.5 0.3 reverse.2
  51.9 0.3 reverse.3
  52.9 0.7 %concatenate.57.low_ref = f32[28,8,256]{2,1,0:T(8,128)} pad(f32[28,2,256]{2,1,0:T(2,128)S(1)} %get-tuple-element.72, f32[]{:T(128)} %constant.47.clone.1), padding=0_0x6_0x0_0 | pad | bytes 286724 | tf_op jit(solution)/shard_map/concatenate | solution.py:247
  53.7 0.7 %concatenate.65.high_ref = f32[28,8,256]{2,1,0:T(8,128)} pad(f32[28,2,256]{2,1,0:T(2,128)S(1)} %get-tuple-element.71, f32[]{:T(128)} %constant.47.clone.1), padding=0_0x0_6x0_0 | pad | bytes 286724 | tf_op jit(solution)/shard_map/concatenate | solution.py:250
  54.4 7.3 %shard_map.156 = (f32[4,96,128]{2,1,0:T(8,128)}, f32[4,96,128]{2,1,0:T(8,128)}, f32[4,96,128]{2,1,0:T(8,128)}, f32[4,96,128]{2,1,0:T(8,128)}) custom-call(f32[4]{0:T(128)} %height_ref.1, f32[2]{0:T(128)} %add_convert_fusion.flag_ref, f32[28,8,256]{2,1,0:T(8,128)} %concatenate.57.low_ref, f32[28,96,256]{2,1,0:T(8,128)} %pad_maximum_fusion.middle_ref, ...), custom_call_target="tpu_custom_call" | custom-call | tf_op jit(solution)/shard_map/pallas_call | solution.py:257
  (116 shorter events, 4.2 us)
Async XLA Ops:
  0.6 1.7 %copy-start = (s32[4,96,128]{2,1,0:T(8,128)S(1)}, s32[4,96,128]{2,1,0:T(8,128)}, u32[]{:S(2)}) copy-start(s32[4,96,128]{2,1,0:T(8,128)} %param.17) | copy-start | bytes 589828
  0.7 2.1 %copy-start.3 = (f32[4,96,128]{2,1,0:T(8,128)S(1)}, f32[4,96,128]{2,1,0:T(8,128)}, u32[]{:S(2)}) copy-start(f32[4,96,128]{2,1,0:T(8,128)} %param.15) | copy-start | bytes 589828
  0.7 2.1 %copy-start.4 = (f32[4,96,128]{2,1,0:T(8,128)S(1)}, f32[4,96,128]{2,1,0:T(8,128)}, u32[]{:S(2)}) copy-start(f32[4,96,128]{2,1,0:T(8,128)} %param.16) | copy-start | bytes 589828
  2.5 0.9 %copy-start.8 = (s32[96,128]{1,0:T(8,128)S(1)}, s32[96,128]{1,0:T(8,128)}, u32[]{:S(2)}) copy-start(s32[96,128]{1,0:T(8,128)} %param.18) | copy-start | bytes 147460
  2.5 1.0 %copy-start.9 = (f32[96,128]{1,0:T(8,128)S(1)}, f32[96,128]{1,0:T(8,128)}, u32[]{:S(2)}) copy-start(f32[96,128]{1,0:T(8,128)} %param.19) | copy-start | bytes 147460
  2.6 1.0 %copy-start.10 = (f32[96,128]{1,0:T(8,128)S(1)}, f32[96,128]{1,0:T(8,128)}, u32[]{:S(2)}) copy-start(f32[96,128]{1,0:T(8,128)} %param.20) | copy-start | bytes 147460
  2.8 1.1 %copy-start.11 = (f32[96,128]{1,0:T(8,128)S(1)}, f32[96,128]{1,0:T(8,128)}, u32[]{:S(2)}) copy-start(f32[96,128]{1,0:T(8,128)} %param.21) | copy-start | bytes 147460
  2.8 1.1 %copy-start.12 = (f32[96,128]{1,0:T(8,128)S(1)}, f32[96,128]{1,0:T(8,128)}, u32[]{:S(2)}) copy-start(f32[96,128]{1,0:T(8,128)} %param.22) | copy-start | bytes 147460
  2.8 1.3 %copy-start.7 = (f32[3,96,128]{2,1,0:T(8,128)S(1)}, f32[3,96,128]{2,1,0:T(8,128)}, u32[]{:S(2)}) copy-start(f32[3,96,128]{2,1,0:T(8,128)} %param.23) | copy-start | bytes 442372
  3.9 9.9 %copy-start.1 = (f32[4,96,128]{2,1,0:T(8,128)S(1)}, f32[4,96,128]{2,1,0:T(8,128)}, u32[]{:S(2)}) copy-start(f32[4,96,128]{2,1,0:T(8,128)} %param.13) | copy-start | bytes 589828
  4.2 9.7 %copy-start.2 = (f32[4,96,128]{2,1,0:T(8,128)S(1)}, f32[4,96,128]{2,1,0:T(8,128)}, u32[]{:S(2)}) copy-start(f32[4,96,128]{2,1,0:T(8,128)} %param.14) | copy-start | bytes 589828
  4.5 10.9 %collective-permute-start.1 = (f32[28,96,2]{1,2,0:T(2,128)S(1)}, f32[28,96,2]{1,2,0:T(2,128)S(1)}, u32[]{:S(2)}, u32[]{:S(2)}) collective-permute-start(f32[28,96,2]{1,2,0:T(2,128)S(1)} %constant_dynamic-update-slice_fusion.11), channel_id=1, source_target_pairs={{0,8},{8,0},{16,24},{24,16},{32,40},{40,32},{48,56},{56,48},{64,72... | collective-permute-start | bytes 64520 | tf_op jit(solution)/shard_map/ppermute | solution.py:132
  8.3 18.1 %collective-permute-start = (f32[28,96,2]{1,2,0:T(2,128)S(1)}, f32[28,96,2]{1,2,0:T(2,128)S(1)}, u32[]{:S(2)}, u32[]{:S(2)}) collective-permute-start(f32[28,96,2]{1,2,0:T(2,128)S(1)} %constant_dynamic-update-slice_fusion), channel_id=1, source_target_pairs={{8,16},{16,8},{24,32},{32,24},{40,48},{48,40},{56,64},{64,56},{72,... | collective-permute-start | bytes 64520 | tf_op jit(solution)/shard_map/ppermute | solution.py:133
  13.9 1.3 %copy-start.13 = (f32[5]{0:T(128)S(1)}, f32[5]{0:T(128)}, u32[]{:S(2)}) copy-start(f32[5]{0:T(128)} %constant.50.clone) | copy-start | bytes 64
  14.1 1.3 %copy-start.5 = (f32[28,96,128]{2,1,0:T(8,128)}, f32[28,96,128]{2,1,0:T(8,128)S(1)}, u32[]{:S(2)}) copy-start(f32[28,96,128]{2,1,0:T(8,128)S(1)} %constant_dynamic-update-slice_fusion.44) | copy-start | bytes 4128772
  26.8 11.3 %copy-start.6 = (f32[28,96,128]{2,1,0:T(8,128)S(1)}, f32[28,96,128]{2,1,0:T(8,128)}, u32[]{:S(2)}) copy-start(f32[28,96,128]{2,1,0:T(8,128)} %copy-done.5) | copy-start | bytes 4128772
  27.4 25.0 %collective-permute-start.2 = (f32[28,2,132]{2,1,0:T(2,128)S(1)}, f32[28,2,132]{2,1,0:T(2,128)S(1)}, u32[]{:S(2)}, u32[]{:S(2)}) collective-permute-start(f32[28,2,132]{2,1,0:T(2,128)S(1)} %pad_maximum_fusion.1), channel_id=1, source_target_pairs={{1,2},{2,1},{3,4},{4,3},{5,6},{6,5},{9,10},{10,9},{11,12},{12,11},... | collective-permute-start | bytes 88712 | tf_op jit(solution)/shard_map/ppermute | solution.py:171
  28.2 24.2 %collective-permute-start.3 = (f32[28,2,132]{2,1,0:T(2,128)S(1)}, f32[28,2,132]{2,1,0:T(2,128)S(1)}, u32[]{:S(2)}, u32[]{:S(2)}) collective-permute-start(f32[28,2,132]{2,1,0:T(2,128)S(1)} %pad_maximum_fusion.2), channel_id=1, source_target_pairs={{0,1},{1,0},{2,3},{3,2},{4,5},{5,4},{6,7},{7,6},{8,9},{9,8},{10,11... | collective-permute-start | bytes 88712 | tf_op jit(solution)/shard_map/ppermute | solution.py:170
  33.0 18.4 %collective-permute-start.4 = (f32[28,2,132]{2,1,0:T(2,128)S(1)}, f32[28,2,132]{2,1,0:T(2,128)S(1)}, u32[]{:S(2)}, u32[]{:S(2)}) collective-permute-start(f32[28,2,132]{2,1,0:T(2,128)S(1)} %pad_maximum_fusion.4), channel_id=1, source_target_pairs={{7,511},{15,503},{23,495},{31,487},{39,479},{47,471},{55,463},{63,... | collective-permute-start | bytes 88712 | tf_op jit(solution)/shard_map/ppermute | solution.py:142

commit v17 on v15

--- a/solution.py
+++ b/solution.py
@@ -218,8 +218,8 @@
             axis=2,
         )
 
-    middle = jnp.concatenate(
-        [block, east, jnp.zeros((block.shape[0], rows, gap), jnp.float32), west], axis=2
+    edge = jnp.concatenate(
+        [east, jnp.zeros((east.shape[0], rows, gap), jnp.float32), west], axis=2
     )
     lead = ROW_OFFSET - HALO
     tail = ROW_PAD - ROW_OFFSET - rows - HALO
@@ -239,12 +239,20 @@
         in_specs=[
             pl.BlockSpec(memory_space=pltpu.SMEM),
             pl.BlockSpec(memory_space=pltpu.SMEM),
-            pl.BlockSpec(memory_space=pltpu.VMEM),
-            pl.BlockSpec(memory_space=pltpu.VMEM),
-            pl.BlockSpec(memory_space=pltpu.VMEM),
-        ],
+        ]
+        + [pl.BlockSpec(memory_space=pltpu.VMEM)] * (3 + len(fields) + 1 + len(surfaces) + 1),
         out_specs=[pl.BlockSpec(memory_space=pltpu.VMEM)] * (channels - 1),
-    )(layer_height, flags, rim_low, middle, rim_high)
+    )(
+        layer_height,
+        flags,
+        rim_low,
+        edge,
+        rim_high,
+        *fields,
+        water_indicator,
+        *surfaces,
+        diapycnal_diffusivity,
+    )
     return tuple(out)
 
 
@@ -252,14 +260,29 @@
 ROW_PAD = 112
 
 
-def two_steps_kernel(height_ref, flag_ref, low_ref, middle_ref, high_ref, *out_refs):
+def two_steps_kernel(height_ref, flag_ref, low_ref, edge_ref, high_ref, *refs):
+    field_refs, wet_ref = refs[:4], refs[4]
+    surface_refs, diapycnal_ref = refs[5:10], refs[10]
+    out_refs = refs[11:]
     levels = out_refs[0].shape[0]
     rows, cols = out_refs[0].shape[1], out_refs[0].shape[2]
-    count = low_ref.shape[1] + middle_ref.shape[1] + high_ref.shape[1]
-    width = middle_ref.shape[2]
+    count = low_ref.shape[1] + edge_ref.shape[1] + high_ref.shape[1]
+    width = 2 * edge_ref.shape[2]
+    wet_levels = [wet_ref[k].astype(jnp.float32) for k in range(levels)]
+
+    def centre(p):
+        if p < 4 * levels:
+            return field_refs[p // levels][p % levels] * wet_levels[p % levels]
+        if p < 5 * levels:
+            return wet_levels[p - 4 * levels]
+        q = p - 5 * levels
+        if q < len(surface_refs):
+            return surface_refs[q][...].astype(jnp.float32)
+        return diapycnal_ref[q - len(surface_refs)]
 
     def plane(p):
-        return jnp.concatenate([low_ref[p], middle_ref[p], high_ref[p]], axis=0)
+        middle = jnp.concatenate([centre(p), edge_ref[p]], axis=1)
+        return jnp.concatenate([low_ref[p], middle, high_ref[p]], axis=0)
 
     sub = lax.broadcasted_iota(jnp.int32, (count, width), 0)
 

time: 59.6 us -> 62.5 us (1.049)
  the two profiles are of different devices: /device:TPU:224 before, /device:TPU:192 now
where the time goes in v17:
time: 62.5 us; the launch traced here: 61.9 us
  starting transfers between devices  33.6 us (54%)
  local copies, waits for them, and re-layouts  9.78 us (16%)
  Pallas kernels  7.38 us (12%)
  waiting for transfers between devices  5.37 us (9%)
  other arithmetic  4.69 us (8%)
  between operations  1.15 us (2%)
    ppermute x1, starting transfers between devices, exchange(): south = lax.ppermute(top_band, 'lat', north_pairs)  15.2 us
    ppermute x1, starting transfers between devices, exchange(): from_outer = lax.ppermute(take_edge(jnp.where(even, 0, high)), 'lon', outer)  13.9 us
    pallas_call x1, Pallas kernels, shards(): pl.pallas_call(two_steps_kernel, out_shape=[field_shape] * (channels - 1)...  7.38 us
    ppermute x1, waiting for transfers between devices, exchange(): north = lax.ppermute(bottom_band, 'lat', south_pairs)  3.18 us
    dynamic_slice x14, local copies, waits for them, and re-layouts, cut(): return lax.dynamic_slice_in_dim(a, start, HALO, axis=a.ndim - 1)  3.05 us
    unnamed x60, local copies, waits for them, and re-layouts  2.94 us
    ppermute x1, waiting for transfers between devices, exchange(): from_outer = lax.ppermute(take_edge(jnp.where(even, 0, high)), 'lon', outer)  2.18 us
    ppermute x1, starting transfers between devices, exchange(): from_inner = lax.ppermute(take_edge(jnp.where(even, high, 0)), 'lon', inner)  1.92 us
  transfers between devices with their start and end apart: 5, of which 2 were waited for; matrix products, arithmetic and copies ran while one was open for 11% of the time, Pallas kernels for 0%

profile of v17, /device:TPU:192, one launch (start us, length us, event | category | flops | bytes accessed | tf_op | source)
XLA Modules:
  0.0 61.9 jit_solution(8139335366113768183)
XLA Ops:
  0.7 1.6 %constant_dynamic-slice_fusion.17 = (f32[4,96,2]{2,1,0:T(8,128)S(1)}, f32[4,96,2]{2,1,0:T(8,128)S(1)}, f32[4,96,2]{2,1,0:T(8,128)S(1)}, f32[4,96,2]{2,1,0:T(8,128)S(1)}) fusion(f32[4,96,128]{2,1,0:T(8,128)} %refs_1_.1, s32[]{:T(128)S(6)} %select_n.58, s32[]{:T(128)S(6)} %select_n.59, f32[4,96,128]{2,1,0:T(8,128)} %refs_0_.1), kind=kLoop, calls=%fused_computation.72 | loop fusion | bytes 24584 | tf_op jit(solution)/shard_map/dynamic_slice | solution.py:190
  2.4 0.2 constant_dynamic-slice_fusion.18
  2.8 0.3 constant_dynamic-slice_fusion.15
  4.2 0.2 constant_dynamic-slice_fusion.10
  4.5 1.9 %collective-permute-start.1 = (f32[28,96,2]{1,2,0:T(2,128)S(1)}, f32[28,96,2]{1,2,0:T(2,128)S(1)}, u32[]{:S(2)}, u32[]{:S(2)}) collective-permute-start(f32[28,96,2]{1,2,0:T(2,128)S(1)} %constant_dynamic-update-slice_fusion.11), channel_id=1, source_target_pairs={{0,8},{8,0},{16,24},{24,16},{32,40},{40,32},{48,56},{56,48},{64,72... | collective-permute-start | bytes 64520 | tf_op jit(solution)/shard_map/ppermute | solution.py:132
  7.6 13.9 %collective-permute-start = (f32[28,96,2]{1,2,0:T(2,128)S(1)}, f32[28,96,2]{1,2,0:T(2,128)}, u32[]{:S(2)}, u32[]{:S(2)}) collective-permute-start(f32[28,96,2]{1,2,0:T(2,128)S(1)} %constant_dynamic-update-slice_fusion), channel_id=1, source_target_pairs={{8,16},{16,8},{24,32},{32,24},{40,48},{48,40},{56,64},{64,56},{72,... | collective-permute-start | bytes 64520 | tf_op jit(solution)/shard_map/ppermute | solution.py:133
  21.5 0.7 %constant_dynamic-update-slice_fusion.43 = (f32[28,2,128]{2,1,0:T(2,128)S(1)}, f32[28,2,128]{2,1,0:T(2,128)S(1)}) fusion(f32[4,96,128]{2,1,0:T(8,128)} %refs_0_.1, s32[4,96,128]{2,1,0:T(8,128)S(1)} %copy-done), kind=kLoop, calls=%fused_computation.46 | loop fusion | flops 4094 | bytes 24576
  22.2 0.8 %constant_dynamic-update-slice_fusion.42 = (f32[28,2,128]{2,1,0:T(2,128)S(1)}, f32[28,2,128]{2,1,0:T(2,128)S(1)}) fusion(f32[28,2,128]{2,1,0:T(2,128)S(1)} %get-tuple-element.16, f32[4,96,128]{2,1,0:T(8,128)} %refs_1_.1, s32[4,96,128]{2,1,0:T(8,128)S(1)} %copy-done, f32[28,2,128]{2,1,0:T(2,128)S(1)} %get-tuple-element.17), kind=kLoop, calls=%fused_computation.45 | loop fusion | flops 4096 | bytes 24576
  23.2 0.6 add_convert_fusion.flag_ref
  24.1 0.5 copy.40
  24.6 2.2 %collective-permute-done = f32[28,96,2]{1,2,0:T(2,128)} collective-permute-done((f32[28,96,2]{1,2,0:T(2,128)S(1)}, f32[28,96,2]{1,2,0:T(2,128)}, u32[]{:S(2)}, u32[]{:S(2)}) %collective-permute-start) | collective-permute-done | bytes 21536 | tf_op jit(solution)/shard_map/ppermute | solution.py:133
  26.8 1.2 %copy.39 = f32[28,96,2]{2,1,0:T(8,128)S(1)} copy(f32[28,96,2]{1,2,0:T(2,128)} %collective-permute-done) | data formatting | bytes 43008 | tf_op jit(solution)/shard_map/ppermute | solution.py:133
  28.0 0.2 broadcast_select_fusion.1
  28.3 0.5 copy-done.12
  28.9 0.7 %collective-permute-start.3 = (f32[28,2,132]{2,1,0:T(2,128)S(1)}, f32[28,2,132]{2,1,0:T(2,128)S(1)}, u32[]{:S(2)}, u32[]{:S(2)}) collective-permute-start(f32[28,2,132]{2,1,0:T(2,128)S(1)} %pad_maximum_fusion.1), channel_id=1, source_target_pairs={{7,511},{15,503},{23,495},{31,487},{39,479},{47,471},{55,463},{63,... | collective-permute-start | bytes 88712 | tf_op jit(solution)/shard_map/ppermute | solution.py:142
  29.6 15.2 %collective-permute-start.2 = (f32[28,2,132]{2,1,0:T(2,128)S(1)}, f32[28,2,132]{2,1,0:T(2,128)S(1)}, u32[]{:S(2)}, u32[]{:S(2)}) collective-permute-start(f32[28,2,132]{2,1,0:T(2,128)S(1)} %pad_maximum_fusion.1), channel_id=1, source_target_pairs={{0,1},{1,2},{2,3},{3,4},{4,5},{5,6},{6,7},{8,9},{9,10},{10,11},{11... | collective-permute-start | bytes 88712 | tf_op jit(solution)/shard_map/ppermute | solution.py:151
  44.8 1.6 %pad_maximum_fusion.edge_ref = f32[28,96,128]{2,1,0:T(8,128)} fusion(f32[28,96,2]{2,1,0:T(8,128)S(1)} %get-tuple-element.4, f32[28,96,2]{2,1,0:T(8,128)S(1)} %get-tuple-element.5, f32[128]{0:T(128)S(1)} %pad.12.clone), kind=kLoop, calls=%fused_computation | loop fusion | flops 688128 | bytes 1419776 | tf_op jit(solution)/shard_map/concatenate | solution.py:221
  46.5 1.9 %collective-permute-start.4 = (f32[28,2,132]{2,1,0:T(2,128)S(1)}, f32[28,2,132]{2,1,0:T(2,128)S(1)}, u32[]{:S(2)}, u32[]{:S(2)}) collective-permute-start(f32[28,2,132]{2,1,0:T(2,128)S(1)} %pad_maximum_fusion.3), channel_id=1, source_target_pairs={{1,0},{2,1},{3,2},{4,3},{5,4},{6,5},{7,6},{9,8},{10,9},{11,10},{12... | collective-permute-start | bytes 88712 | tf_op jit(solution)/shard_map/ppermute | solution.py:152
  48.5 0.3 reverse.2
  48.9 0.3 reverse.3
  49.4 3.2 %collective-permute-done.4 = f32[28,2,132]{2,1,0:T(2,128)S(1)} collective-permute-done((f32[28,2,132]{2,1,0:T(2,128)S(1)}, f32[28,2,132]{2,1,0:T(2,128)S(1)}, u32[]{:S(2)}, u32[]{:S(2)}) %collective-permute-start.4) | collective-permute-done | bytes 29600 | tf_op jit(solution)/shard_map/ppermute | solution.py:152
  53.1 0.7 %concatenate.46.low_ref = f32[28,8,256]{2,1,0:T(8,128)} pad(f32[28,2,256]{2,1,0:T(2,128)S(1)} %get-tuple-element.57, f32[]{:T(128)} %constant.38.clone.1), padding=0_0x6_0x0_0 | pad | bytes 286724 | tf_op jit(solution)/shard_map/concatenate | solution.py:226
  53.8 0.7 %concatenate.53.high_ref = f32[28,8,256]{2,1,0:T(8,128)} pad(f32[28,2,256]{2,1,0:T(2,128)S(1)} %get-tuple-element.56, f32[]{:T(128)} %constant.38.clone.1), padding=0_0x0_6x0_0 | pad | bytes 286724 | tf_op jit(solution)/shard_map/concatenate | solution.py:229
  54.6 7.4 %shard_map.156 = (f32[4,96,128]{2,1,0:T(8,128)}, f32[4,96,128]{2,1,0:T(8,128)}, f32[4,96,128]{2,1,0:T(8,128)}, f32[4,96,128]{2,1,0:T(8,128)}) custom-call(f32[4]{0:T(128)} %height_ref.1, f32[2]{0:T(128)} %add_convert_fusion.flag_ref, f32[28,8,256]{2,1,0:T(8,128)} %concatenate.46.low_ref, f32[28,96,128]{2,1,0:T(8,128)} %pad_maximum_fusion.edge_ref, ...), custom_call_target="tpu_custom_call" | custom-call | tf_op jit(solution)/shard_map/pallas_call | solution.py:236
  (105 shorter events, 4.2 us)
Async XLA Ops:
  0.6 1.7 %copy-start = (s32[4,96,128]{2,1,0:T(8,128)S(1)}, s32[4,96,128]{2,1,0:T(8,128)}, u32[]{:S(2)}) copy-start(s32[4,96,128]{2,1,0:T(8,128)} %refs_4_.1) | copy-start | bytes 589828
  0.7 2.1 %copy-start.1 = (f32[4,96,128]{2,1,0:T(8,128)S(1)}, f32[4,96,128]{2,1,0:T(8,128)}, u32[]{:S(2)}) copy-start(f32[4,96,128]{2,1,0:T(8,128)} %refs_3_.1) | copy-start | bytes 589828
  0.7 2.1 %copy-start.2 = (f32[4,96,128]{2,1,0:T(8,128)S(1)}, f32[4,96,128]{2,1,0:T(8,128)}, u32[]{:S(2)}) copy-start(f32[4,96,128]{2,1,0:T(8,128)} %refs_2_.1) | copy-start | bytes 589828
  2.5 0.9 %copy-start.4 = (s32[96,128]{1,0:T(8,128)S(1)}, s32[96,128]{1,0:T(8,128)}, u32[]{:S(2)}) copy-start(s32[96,128]{1,0:T(8,128)} %refs_5_.1) | copy-start | bytes 147460
  2.6 1.0 %copy-start.5 = (f32[96,128]{1,0:T(8,128)S(1)}, f32[96,128]{1,0:T(8,128)}, u32[]{:S(2)}) copy-start(f32[96,128]{1,0:T(8,128)} %refs_7_.1) | copy-start | bytes 147460
  2.6 1.0 %copy-start.6 = (f32[96,128]{1,0:T(8,128)S(1)}, f32[96,128]{1,0:T(8,128)}, u32[]{:S(2)}) copy-start(f32[96,128]{1,0:T(8,128)} %refs_6_.1) | copy-start | bytes 147460
  2.8 1.1 %copy-start.7 = (f32[96,128]{1,0:T(8,128)S(1)}, f32[96,128]{1,0:T(8,128)}, u32[]{:S(2)}) copy-start(f32[96,128]{1,0:T(8,128)} %refs_9_.1) | copy-start | bytes 147460
  2.8 1.1 %copy-start.8 = (f32[96,128]{1,0:T(8,128)S(1)}, f32[96,128]{1,0:T(8,128)}, u32[]{:S(2)}) copy-start(f32[96,128]{1,0:T(8,128)} %refs_8_.1) | copy-start | bytes 147460
  2.8 1.3 %copy-start.3 = (f32[3,96,128]{2,1,0:T(8,128)S(1)}, f32[3,96,128]{2,1,0:T(8,128)}, u32[]{:S(2)}) copy-start(f32[3,96,128]{2,1,0:T(8,128)} %refs_10_.1) | copy-start | bytes 442372
  4.0 19.9 %copy-start.13 = (f32[5]{0:T(128)S(1)}, f32[5]{0:T(128)}, u32[]{:S(2)}) copy-start(f32[5]{0:T(128)} %constant.41.clone) | copy-start | bytes 64
  4.5 19.6 %collective-permute-start.1 = (f32[28,96,2]{1,2,0:T(2,128)S(1)}, f32[28,96,2]{1,2,0:T(2,128)S(1)}, u32[]{:S(2)}, u32[]{:S(2)}) collective-permute-start(f32[28,96,2]{1,2,0:T(2,128)S(1)} %constant_dynamic-update-slice_fusion.11), channel_id=1, source_target_pairs={{0,8},{8,0},{16,24},{24,16},{32,40},{40,32},{48,56},{56,48},{64,72... | collective-permute-start | bytes 64520 | tf_op jit(solution)/shard_map/ppermute | solution.py:132
  7.6 19.2 %collective-permute-start = (f32[28,96,2]{1,2,0:T(2,128)S(1)}, f32[28,96,2]{1,2,0:T(2,128)}, u32[]{:S(2)}, u32[]{:S(2)}) collective-permute-start(f32[28,96,2]{1,2,0:T(2,128)S(1)} %constant_dynamic-update-slice_fusion), channel_id=1, source_target_pairs={{8,16},{16,8},{24,32},{32,24},{40,48},{48,40},{56,64},{64,56},{72,... | collective-permute-start | bytes 64520 | tf_op jit(solution)/shard_map/ppermute | solution.py:133
  23.1 1.4 %copy-start.9 = (f32[28,2,128]{2,1,0:T(2,128)}, f32[28,2,128]{2,1,0:T(2,128)S(1)}, u32[]{:S(2)}) copy-start(f32[28,2,128]{2,1,0:T(2,128)S(1)} %get-tuple-element.30) | copy-start | bytes 86020
  23.1 1.4 %copy-start.11 = (f32[28,2,128]{2,1,0:T(2,128)}, f32[28,2,128]{2,1,0:T(2,128)S(1)}, u32[]{:S(2)}) copy-start(f32[28,2,128]{2,1,0:T(2,128)S(1)} %get-tuple-element.31) | copy-start | bytes 86020
  28.0 0.8 %copy-start.12 = (f32[28,2,128]{2,1,0:T(2,128)S(1)}, f32[28,2,128]{2,1,0:T(2,128)}, u32[]{:S(2)}) copy-start(f32[28,2,128]{2,1,0:T(2,128)} %copy-done.11) | copy-start | bytes 86020
  28.9 17.4 %copy-start.10 = (f32[28,2,128]{2,1,0:T(2,128)S(1)}, f32[28,2,128]{2,1,0:T(2,128)}, u32[]{:S(2)}) copy-start(f32[28,2,128]{2,1,0:T(2,128)} %copy-done.9) | copy-start | bytes 86020
  28.9 19.5 %collective-permute-start.3 = (f32[28,2,132]{2,1,0:T(2,128)S(1)}, f32[28,2,132]{2,1,0:T(2,128)S(1)}, u32[]{:S(2)}, u32[]{:S(2)}) collective-permute-start(f32[28,2,132]{2,1,0:T(2,128)S(1)} %pad_maximum_fusion.1), channel_id=1, source_target_pairs={{7,511},{15,503},{23,495},{31,487},{39,479},{47,471},{55,463},{63,... | collective-permute-start | bytes 88712 | tf_op jit(solution)/shard_map/ppermute | solution.py:142
  29.6 23.2 %collective-permute-start.2 = (f32[28,2,132]{2,1,0:T(2,128)S(1)}, f32[28,2,132]{2,1,0:T(2,128)S(1)}, u32[]{:S(2)}, u32[]{:S(2)}) collective-permute-start(f32[28,2,132]{2,1,0:T(2,128)S(1)} %pad_maximum_fusion.1), channel_id=1, source_target_pairs={{0,1},{1,2},{2,3},{3,4},{4,5},{5,6},{6,7},{8,9},{9,10},{10,11},{11... | collective-permute-start | bytes 88712 | tf_op jit(solution)/shard_map/ppermute | solution.py:151
  46.5 6.1 %collective-permute-start.4 = (f32[28,2,132]{2,1,0:T(2,128)S(1)}, f32[28,2,132]{2,1,0:T(2,128)S(1)}, u32[]{:S(2)}, u32[]{:S(2)}) collective-permute-start(f32[28,2,132]{2,1,0:T(2,128)S(1)} %pad_maximum_fusion.3), channel_id=1, source_target_pairs={{1,0},{2,1},{3,2},{4,3},{5,4},{6,5},{7,6},{9,8},{10,9},{11,10},{12... | collective-permute-start | bytes 88712 | tf_op jit(solution)/shard_map/ppermute | solution.py:152
